TPU v7x, 256 devices: a whole 4x4x8 slice. The times are simulated.
256 devices in a mesh: dp: 32 (over z, x), seq: 8 (over y, core).
Axes of the slice: x: 4, y: 4, z: 8, core: 2. Of those that a mesh axis runs over, the one named last changes fastest.
Arguments:
- hidden: bfloat16 [32, 6144, 2560], P('dp', 'seq'), may hold values from -6 to 6
- log_decay: float32 [32, 40, 6144], P('dp', None, 'seq'), may hold values from -2 to 0, as said below
- input_weight: bfloat16 [2816, 2560], P(('dp', 'seq')), may hold values from -0.125 to 0.125
- conv_weight: bfloat16 [4, 2816], replicated, may hold values from -3 to 3
- conv_bias: float32 [2816], replicated, may hold values from -0.5 to 0.5
- skip_gain: float32 [40], replicated, may hold values from 0.5 to 1.5
Outputs:
- mixer_out: bfloat16 [32, 6144, 2560], P('dp', 'seq')
Inputs may be any that keep to these rules, and one draw needn't show every extreme that they name: `log_decay`: every value is negative.
All inputs are finite; a program needn't handle non-finite values.
Results may differ from a plain program's by a relative error of at most 0.0064.
Values may be sent and summed in bfloat16 or wider, within the bound.
No kernel may reach another device: no remote copies, remote signals or barrier semaphores. Data moves between devices by JAX's collectives and lax.ppermute only.
A program may use at most 128 MiB of HBM per device.

v0:
```python
import jax
import jax.numpy as jnp
from jax import lax
from jax.sharding import PartitionSpec as P

HALF_HEADS = 40
HEAD_DIM = 64
STATE = 128
SPAN = 256
CONV = 4
INNER = 2560
COLS = 2816


def entering_2(part, axis, combine, identity):
    place = lax.axis_index(axis)
    gathered = jax.tree.map(lambda a: lax.all_gather(a, axis), part)
    state = jax.tree.map(lambda a, e: jnp.zeros_like(a) + jnp.asarray(e, a.dtype), part, identity)

    def one(lap, state):
        return combine(
            state, jax.tree.map(lambda a: lax.dynamic_index_in_dim(a, lap, 0, False), gathered)
        )

    return lax.fori_loop(0, place, one, state)


def passed_along(array, axis, by):
    peers = lax.axis_size(axis)
    pairs = [(i, i + by) for i in range(peers) if 0 <= i + by < peers]
    return lax.ppermute(array, axis, pairs)


def mixing_output(x_heads, b_span, c_span, cumulative, step_size):
    scores = jnp.dot(c_span, b_span.T, preferred_element_type=jnp.float32)
    span_len = cumulative.shape[1]
    causal = jnp.arange(span_len)[:, None] >= jnp.arange(span_len)[None, :]
    spread = jnp.where(causal[None], cumulative[:, :, None] - cumulative[:, None, :], -jnp.inf)
    mixing = (scores[None] * jnp.exp(spread) * step_size[:, None, :]).astype(jnp.bfloat16)
    return jnp.einsum("hqk,khp->qhp", mixing, x_heads, preferred_element_type=jnp.float32)


def span_state(x_heads, b_span, cumulative, step_size):
    weight = jnp.exp(cumulative[:, -1:] - cumulative) * step_size
    decayed = (x_heads * weight.T[:, :, None]).astype(jnp.bfloat16)
    return jnp.einsum("khp,kn->hpn", decayed, b_span, preferred_element_type=jnp.float32)


def state_output(c_span, entering, cumulative):
    readout = jnp.einsum(
        "qn,hpn->qhp", c_span.astype(jnp.float32), entering, precision=lax.Precision.HIGHEST
    )
    return jnp.exp(cumulative).T[:, :, None] * readout


def incoming(local_end, device_total):

    def combine(earlier, later_part):
        return (
            earlier[0] + later_part[0],
            jnp.exp(later_part[0])[:, None, None] * earlier[1] + later_part[1],
        )

    identity = (jnp.zeros_like(device_total), jnp.zeros_like(local_end))
    _, entering_dev = entering_2((device_total, local_end), "seq", combine, identity)
    return entering_dev


def body(hidden, log_decay, input_weight, conv_weight, conv_bias, skip_gain):
    token_rows = hidden[0]
    length = token_rows.shape[0]
    projected = lax.dot_general(
        token_rows,
        lax.all_gather(input_weight, ("dp", "seq"), axis=0, tiled=True),
        (((1,), (1,)), ((), ())),
        preferred_element_type=jnp.float32,
    ).astype(jnp.bfloat16)
    last_rows = projected[length - (CONV - 1) :]
    before_rows = passed_along(last_rows, "seq", 1)
    extended = jnp.concatenate([before_rows, projected], axis=0)
    filtered = jnp.broadcast_to(conv_bias[None, :], (length, COLS))
    for kernel_tap in range(CONV):
        filtered = (
            filtered
            + extended[kernel_tap : kernel_tap + length].astype(jnp.float32)
            * conv_weight[kernel_tap].astype(jnp.float32)[None, :]
        )
    active = jax.nn.silu(filtered).astype(jnp.bfloat16)
    span_count = length // SPAN
    x_all = active[:, :INNER].reshape(span_count, SPAN, HALF_HEADS, HEAD_DIM)
    b_all = active[:, INNER : INNER + STATE].reshape(span_count, SPAN, STATE)
    c_all = active[:, INNER + STATE :].reshape(span_count, SPAN, STATE)
    decay_spans = log_decay[0].reshape(HALF_HEADS, span_count, SPAN).transpose(1, 0, 2)
    cumulative = jnp.cumsum(decay_spans, axis=2)
    steps_all = -decay_spans
    totals = cumulative[:, :, -1]
    device_total = jnp.sum(totals, axis=0)
    zero_state = jnp.zeros((HALF_HEADS, HEAD_DIM, STATE), jnp.float32)

    def state_of(inputs):
        x_heads, b_span, cum_span, step_span = inputs
        return span_state(x_heads, b_span, cum_span, step_span)

    states = lax.map(state_of, (x_all, b_all, cumulative, steps_all))

    def gather_local(held_state, inputs):
        span_total, state_piece = inputs
        return (jnp.exp(span_total)[:, None, None] * held_state + state_piece, None)

    local_end, _ = lax.scan(gather_local, zero_state, (totals, states))
    entering_dev = incoming(local_end, device_total)

    def emit(held_state, inputs):
        x_heads, b_span, c_span, cum_span, step_span, span_total, state_piece = inputs
        outputs = mixing_output(x_heads, b_span, c_span, cum_span, step_span) + state_output(
            c_span, held_state, cum_span
        )
        return (jnp.exp(span_total)[:, None, None] * held_state + state_piece, outputs)

    _, outputs = lax.scan(
        emit, entering_dev, (x_all, b_all, c_all, cumulative, steps_all, totals, states)
    )
    outputs = outputs.reshape(length, HALF_HEADS, HEAD_DIM)
    final = outputs + skip_gain[None, :, None] * x_all.reshape(length, HALF_HEADS, HEAD_DIM).astype(
        jnp.float32
    )
    return final.reshape(1, length, INNER).astype(jnp.bfloat16)


def solution(mesh):
    placed = (P("dp", "seq", None), P("dp", None, "seq"), P(("dp", "seq"), None), P(), P(), P())
    return jax.shard_map(
        body, mesh=mesh, in_specs=placed, out_specs=P("dp", "seq", None), check_vma=False
    )
```

profile of v0, /device:TPU:16, one launch (start us, length us, event | category | flops | bytes accessed | tf_op | source)
XLA Modules:
  0.0 378.5 jit_solution(17181810627922723173)
XLA Ops:
  6.5 0.7 all-gather.8.cloned.1.call-update
  7.3 1.0 reshape_squeeze.3
  8.4 1.8 reduce-window.6
  10.4 1.0 convert_reduce_fusion.3
  11.6 133.1 %all-gather.8.cloned.1.call-done = bf16[256,11,2560]{2,1,0:T(8,128)(2,1)} async-done(((bf16[1,11,2560]{2,1,0:T(8,128)(2,1)}), bf16[256,11,2560]{2,1,0:T(8,128)(2,1)}) %all-gather.8.cloned.1.call-update) | async-done | bytes 14417936 | tf_op jit(solution)/shard_map/all_gather | solution.py:74
  144.7 25.0 %reshape.85 = bf16[2816,2560]{1,0:T(8,128)(2,1)} reshape(bf16[256,11,2560]{2,1,0:T(8,128)(2,1)} %all-gather.8.cloned.1.call-done) | data formatting | bytes 28835840
  169.8 16.5 %convolution_convert_fusion = bf16[768,2816]{1,0:T(8,128)(2,1)S(1)} fusion(bf16[2816,2560]{1,0:T(8,128)(2,1)} %reshape.85, bf16[1,768,2560]{2,1,0:T(8,128)(2,1)} %param.14), kind=kOutput, calls=%fused_computation.56 | convolution fusion | flops 11075125248 | bytes 22675456 | tf_op jit(solution)/shard_map/dot_general | solution.py:72
  186.3 2.0 copy-done.2
  188.3 2.2 collective-permute-start
  190.4 0.2 slice_reduce_fusion.1
  190.6 2.7 collective-permute-done
  193.4 10.6 %multiply_convert_fusion.5 = bf16[768,2816]{1,0:T(8,128)(2,1)S(1)} fusion(bf16[768,2816]{1,0:T(8,128)(2,1)} %copy-done.2, bf16[3,2816]{1,0:T(4,128)(2,1)S(1)} %collective-permute-done, f32[2816]{0:T(1024)S(1)} %get-tuple-element.242, f32[2816]{0:T(1024)S(1)} %get-tuple-element.243, f32[2816]{0:T(1024)S(1)} %get-tuple-element.241, ...), kind=kLoop, calls=%fused_computation.52 | loop fusion | flops 56229888 | bytes 8723968 | tf_op jit(solution)/shard_map/convert_element_type | solution.py:88
  204.0 2.1 copy-done.1
  206.1 2.3 slice.68
  208.4 10.7 %reshape.92 = bf16[3,256,40,64]{3,2,1,0:T(8,128)(2,1)} reshape(bf16[768,2560]{1,0:T(8,128)(2,1)} %slice.68) | data formatting | bytes 7864320 | tf_op jit(solution)/shard_map/reshape | solution.py:90
  219.1 11.3 %copy.42 = bf16[3,256,40,64]{1,3,2,0:T(8,128)(2,1)} copy(bf16[3,256,40,64]{3,2,1,0:T(8,128)(2,1)} %reshape.92) | data formatting | bytes 7864320 | tf_op jit(solution)/shard_map/while | solution.py:104
  230.4 9.8 %while.45 = (s32[]{:T(128)}, f32[3,40,64,128]{3,2,1,0:T(8,128)}, bf16[3,256,40,64]{1,3,2,0:T(8,128)(2,1)}, f32[3,40,256]{2,1,0:T(8,128)S(1)}, f32[3,40,256]{2,0,...) while((s32[]{:T(128)}, f32[3,40,64,128]{3,2,1,0:T(8,128)}, bf16[3,256,40,64]{1,3,2,0:T(8,128)(2,1)}, ...), condition=%wide.region_4.5_spmd, body=%wide.region_3.4_spmd.sunk | while | flops 169758720 | bytes 3262525 | solution.py:104
  230.8 2.9 fusion.54
  234.0 2.9 fusion.54
  237.3 2.9 fusion.54
  240.2 4.7 %while.48 = (s32[]{:T(128)}, f32[40,64,128]{2,1,0:T(8,128)S(1)}, f32[3,40]{1,0:T(4,128)S(1)}, f32[3,40,64,128]{3,2,1,0:T(8,128)}, s32[]{:T(128)}, /*index=5*/s32[]{:T(128)}) while((s32[]{:T(128)}, f32[40,64,128]{2,1,0:T(8,128)S(1)}, f32[3,40]{1,0:T(4,128)S(1)}, f32[3,40,64,128]{3,2,1,0:T(8,128)}, s32[]{:T(128)}, ...), condition=%wide.region_6.7_spmd.clone, body=%wide.region_5.6_spmd.clone.sunk | while | flops 983043 | bytes 3932735 | solution.py:110
  240.2 1.5 bitcast_add_fusion.9
  241.8 1.5 bitcast_add_fusion.9
  243.4 1.5 bitcast_add_fusion.9
  244.9 1.0 copy-done
  246.2 0.6 dynamic-slice
  247.4 0.2 dynamic-update-slice
  247.6 10.5 %all-reduce = f32[320]{0:T(512)S(1)} all-reduce(f32[320]{0:T(512)S(1)} %dynamic-update-slice), channel_id=2, replica_groups=mesh['dp'=32,'seq'=8] {'seq'}, use_global_device_ids=true, to_apply=%add | all-reduce | flops 320 | bytes 2560
  258.2 45.4 %all-gather.6.cloned.1.call-done = f32[320,64,128]{2,1,0:T(8,128)} async-done(((f32[40,64,128]{2,1,0:T(8,128)}), f32[320,64,128]{2,1,0:T(8,128)}) %all-gather.6.cloned.1.call-update) | async-done | bytes 10485776 | tf_op jit(solution)/shard_map/all_gather | solution.py:17
  303.8 6.7 %while.46 = (s32[]{:T(128)}, f32[40,64,128]{2,1,0:T(8,128)S(1)}, s32[]{:T(128)}, f32[8,40]{1,0:T(8,128)S(1)}, f32[8,40,64,128]{3,2,1,0:T(8,128)}, /*index=5*/s32[]{:T(128)}, s32[]{:T(128)}, s32[]{:T(128)}) while((s32[]{:T(128)}, f32[40,64,128]{2,1,0:T(8,128)S(1)}, s32[]{:T(128)}, f32[8,40]{1,0:T(8,128)S(1)}, f32[8,40,64,128]{3,2,1,0:T(8,128)}, ...), condition=%wide.region_8.9_spmd, body=%wide.region_7.8_spmd.sunk | while | flops 655365 | bytes 3932775 | solution.py:25
  303.8 1.6 bitcast_add_fusion.7
  305.4 1.6 bitcast_add_fusion.7
  307.0 1.6 bitcast_add_fusion.7
  308.7 1.6 bitcast_add_fusion.7
  310.4 25.4 %while.47 = (s32[]{:T(128)}, f32[40,64,128]{2,1,0:T(8,128)S(1)}, f32[3,256,40,64]{1,3,2,0:T(8,128)}, f32[3,40]{1,0:T(4,128)S(1)}, f32[3,40,64,128]{3,2,1,0:T(8,1...) while((s32[]{:T(128)}, f32[40,64,128]{2,1,0:T(8,128)S(1)}, ...), condition=%wide.region_10.11_spmd, body=%wide.region_9.10_spmd.sunk | while | flops 1374093312 | bytes 15723113 | solution.py:120
  310.8 1.2 fusion.61
  312.0 1.6 bitcast_add_fusion.8
  313.6 5.3 %bitcast_dynamic-update-slice_fusion.2 = f32[3,256,40,64]{1,3,2,0:T(8,128)} fusion(f32[3,256,40,64]{1,3,2,0:T(8,128)} %get-tuple-element.533, s32[]{:T(128)S(6)} %copy.94, f32[256,40,64]{0,2,1:T(8,128)S(1)} %fusion.61, f32[40,256]{1,0:T(8,128)S(1)} %bitcast.133, f32[40,256]{1,0:T(8,128)S(1)} %get-tuple-element.451, f32[256,256]{1,0:T(8,128)S(1)} %fusion.62, ...), kind=kOutput, calls=%fused_computation.24.clone.1 | convolution fusion | flops 349962240 | bytes 7046144 | tf_op jit(solution)/shard_map/while/body/eval_jaxpr/hqk,khp->qhp/dot_general | solution.py:40
  319.0 0.2 fusion.62
  319.2 1.2 fusion.61
  320.4 1.6 bitcast_add_fusion.8
  322.0 5.3 %bitcast_dynamic-update-slice_fusion.2 = f32[3,256,40,64]{1,3,2,0:T(8,128)} fusion(f32[3,256,40,64]{1,3,2,0:T(8,128)} %get-tuple-element.533, s32[]{:T(128)S(6)} %copy.94, f32[256,40,64]{0,2,1:T(8,128)S(1)} %fusion.61, f32[40,256]{1,0:T(8,128)S(1)} %bitcast.133, f32[40,256]{1,0:T(8,128)S(1)} %get-tuple-element.451, f32[256,256]{1,0:T(8,128)S(1)} %fusion.62, ...), kind=kOutput, calls=%fused_computation.24.clone.1 | convolution fusion | flops 349962240 | bytes 7046144 | tf_op jit(solution)/shard_map/while/body/eval_jaxpr/hqk,khp->qhp/dot_general | solution.py:40
  327.7 1.2 fusion.61
  328.9 1.6 bitcast_add_fusion.8
  330.5 5.4 %bitcast_dynamic-update-slice_fusion.2 = f32[3,256,40,64]{1,3,2,0:T(8,128)} fusion(f32[3,256,40,64]{1,3,2,0:T(8,128)} %get-tuple-element.533, s32[]{:T(128)S(6)} %copy.94, f32[256,40,64]{0,2,1:T(8,128)S(1)} %fusion.61, f32[40,256]{1,0:T(8,128)S(1)} %bitcast.133, f32[40,256]{1,0:T(8,128)S(1)} %get-tuple-element.451, f32[256,256]{1,0:T(8,128)S(1)} %fusion.62, ...), kind=kOutput, calls=%fused_computation.24.clone.1 | convolution fusion | flops 349962240 | bytes 7046144 | tf_op jit(solution)/shard_map/while/body/eval_jaxpr/hqk,khp->qhp/dot_general | solution.py:40
  335.8 14.6 %copy.51 = f32[3,256,40,64]{3,2,1,0:T(8,128)} copy(f32[3,256,40,64]{1,3,2,0:T(8,128)} %get-tuple-element.158) | data formatting | bytes 15728640 | tf_op jit(solution)/shard_map/reshape | solution.py:123
  350.4 13.7 %reshape.91 = f32[768,2560]{1,0:T(8,128)} reshape(f32[3,256,40,64]{3,2,1,0:T(8,128)} %copy.51) | data formatting | bytes 15728640 | tf_op jit(solution)/shard_map/reshape | solution.py:123
  364.1 7.5 %fusion.34 = bf16[1,768,2560]{2,1,0:T(8,128)(2,1)} fusion(f32[768,2560]{1,0:T(8,128)} %reshape.91, f32[2560]{0:T(1024)S(1)} %mul.153, bf16[768,2816]{1,0:T(8,128)(2,1)} %copy-done.1), kind=kLoop, calls=%fused_computation.60 | loop fusion | flops 7864320 | bytes 15738880 | tf_op jit(solution)/shard_map/convert_element_type | solution.py:127
  (74 shorter events, 2.8 us)
Async XLA Ops:
  6.5 138.2 %all-gather.8.cloned.1.call-start = ((), (), s32[]{:S(2)}) async-start(), calls=%async_computation.1 | async-start | bytes 21053440 | tf_op jit(solution)/shard_map/all_gather | solution.py:74
  7.3 296.3 %all-gather.6.cloned.1.call-start = ((), (), s32[]{:S(2)}) async-start(), calls=%async_computation | async-start | bytes 11796480 | tf_op jit(solution)/shard_map/all_gather | solution.py:17
  169.8 23.6 %copy-start.3 = (f32[2816]{0:T(1024)S(1)}, f32[2816]{0:T(1024)}, u32[]{:S(2)}) copy-start(f32[2816]{0:T(1024)} %param.18) | copy-start | bytes 33796
  186.3 2.0 copy-start.2
  188.3 5.1 %collective-permute-start = (bf16[3,2816]{1,0:T(4,128)(2,1)S(1)}, bf16[3,2816]{1,0:T(4,128)(2,1)S(1)}, u32[]{:S(2)}, u32[]{:S(2)}) collective-permute-start(bf16[3,2816]{1,0:T(4,128)(2,1)S(1)} %slice.63), channel_id=1, source_target_pairs={{0,1},{1,2},{2,3},{3,4},{4,5},{5,6},{6,7},{8,9},{9,10},{10,11},{11... | collective-permute-start | bytes 50696 | tf_op jit(solution)/shard_map/ppermute | solution.py:31
  204.0 2.1 copy-start.1
  240.2 5.8 %copy-start.4 = (f32[40]{0:T(128)S(1)}, f32[40]{0:T(128)}, u32[]{:S(2)}) copy-start(f32[40]{0:T(128)} %param.19) | copy-start | bytes 484
  240.2 6.0 %copy-start.5 = (u32[256]{0:T(256)S(1)}, u32[256]{0:T(256)}, u32[]{:S(2)}) copy-start(u32[256]{0:T(256)} %constant.77) | copy-start | bytes 3076
  244.9 1.1 copy-start
Sparse Core Ops, SparseCore 0:
  10.9 133.7 all-gather.7
  246.1 57.4 all-gather.5
where the time goes:
time: 385 us; the launch traced here: 379 us
  waiting for transfers between devices  182 us (47%)
  local copies, waits for them, and re-layouts  86.5 us (22%)
  matrix products  45.3 us (12%)
  other arithmetic  37.1 us (10%)
  between operations  14.2 us (4%)
  blocking collectives  10.5 us (3%)
    all_gather x1, waiting for transfers between devices, body(): lax.all_gather(input_weight, ('dp', 'seq'), axis=0, tiled=True)  133 us
    all_gather x1, waiting for transfers between devices, entering_2(): gathered = jax.tree.map(lambda a: lax.all_gather(a, axis), part)  45.4 us
    unnamed x16, local copies, waits for them, and re-layouts  31 us
    reshape x2, local copies, waits for them, and re-layouts, body(): outputs = outputs.reshape(length, HALF_HEADS, HEAD_DIM)  28.3 us
    dot_general x1, matrix products, body(): lax.dot_general(token_rows, lax.all_gather(input_weight, ('dp', 'seq'), a...  16.5 us
    dot_general x3, matrix products, mixing_output(): jnp.einsum('hqk,khp->qhp', mixing, x_heads, preferred_element_type=jnp.fl...  16 us
    while x1, local copies, waits for them, and re-layouts, body(): states = lax.map(state_of, (x_all, b_all, cumulative, steps_all))  11.3 us
    reshape x1, local copies, waits for them, and re-layouts, body(): x_all = active[:, :INNER].reshape(span_count, SPAN, HALF_HEADS, HEAD_DIM)  10.7 us
  transfers between devices with their start and end apart: 3, of which 3 were waited for; matrix products, arithmetic and copies ran while one was open for 1% of the time, Pallas kernels for 0%

commit v1 on v0

--- a/solution.py
+++ b/solution.py
@@ -1,7 +1,7 @@
 import jax
 import jax.numpy as jnp
 from jax import lax
-from jax.sharding import PartitionSpec as P
+from jax.sharding import Mesh, PartitionSpec as P
 
 HALF_HEADS = 40
 HEAD_DIM = 64
@@ -10,25 +10,6 @@
 CONV = 4
 INNER = 2560
 COLS = 2816
-
-
-def entering_2(part, axis, combine, identity):
-    place = lax.axis_index(axis)
-    gathered = jax.tree.map(lambda a: lax.all_gather(a, axis), part)
-    state = jax.tree.map(lambda a, e: jnp.zeros_like(a) + jnp.asarray(e, a.dtype), part, identity)
-
-    def one(lap, state):
-        return combine(
-            state, jax.tree.map(lambda a: lax.dynamic_index_in_dim(a, lap, 0, False), gathered)
-        )
-
-    return lax.fori_loop(0, place, one, state)
-
-
-def passed_along(array, axis, by):
-    peers = lax.axis_size(axis)
-    pairs = [(i, i + by) for i in range(peers) if 0 <= i + by < peers]
-    return lax.ppermute(array, axis, pairs)
 
 
 def mixing_output(x_heads, b_span, c_span, cumulative, step_size):
@@ -53,30 +34,49 @@
     return jnp.exp(cumulative).T[:, :, None] * readout
 
 
-def incoming(local_end, device_total):
+SEQ = ("y", "core")
 
-    def combine(earlier, later_part):
-        return (
-            earlier[0] + later_part[0],
-            jnp.exp(later_part[0])[:, None, None] * earlier[1] + later_part[1],
-        )
 
-    identity = (jnp.zeros_like(device_total), jnp.zeros_like(local_end))
-    _, entering_dev = entering_2((device_total, local_end), "seq", combine, identity)
-    return entering_dev
+def shifted(array, by):
+    peers = lax.axis_size(SEQ)
+    pairs = [(i, i + by) for i in range(peers) if i + by < peers]
+    return lax.ppermute(array, SEQ, pairs)
+
+
+def scan_entering(total, state):
+    acc_total, acc_state = shifted(total, 1), shifted(state, 1)
+    by = 1
+    while by < lax.axis_size(SEQ):
+        got_total, got_state = shifted(acc_total, by), shifted(acc_state, by)
+        acc_state = jnp.exp(acc_total)[:, None, None] * got_state + acc_state
+        acc_total = acc_total + got_total
+        by *= 2
+    return acc_state
+
+
+def project(token_rows, input_weight):
+    rows = input_weight.shape[0]
+    mine = lax.all_gather(input_weight, ("dp", "y"), axis=0, tiled=True)
+    other = lax.ppermute(mine, "core", [(0, 1), (1, 0)])
+    dims = (((1,), (1,)), ((), ()))
+    p_mine = lax.dot_general(token_rows, mine, dims, preferred_element_type=jnp.float32).astype(jnp.bfloat16)
+    p_other = lax.dot_general(token_rows, other, dims, preferred_element_type=jnp.float32).astype(jnp.bfloat16)
+    first = lax.axis_index("core") == 0
+    p0 = jnp.where(first, p_mine, p_other)
+    p1 = jnp.where(first, p_other, p_mine)
+    length = token_rows.shape[0]
+    groups = mine.shape[0] // rows
+    return jnp.stack(
+        [p0.reshape(length, groups, rows), p1.reshape(length, groups, rows)], axis=2
+    ).reshape(length, COLS)
 
 
 def body(hidden, log_decay, input_weight, conv_weight, conv_bias, skip_gain):
     token_rows = hidden[0]
     length = token_rows.shape[0]
-    projected = lax.dot_general(
-        token_rows,
-        lax.all_gather(input_weight, ("dp", "seq"), axis=0, tiled=True),
-        (((1,), (1,)), ((), ())),
-        preferred_element_type=jnp.float32,
-    ).astype(jnp.bfloat16)
+    projected = project(token_rows, input_weight)
     last_rows = projected[length - (CONV - 1) :]
-    before_rows = passed_along(last_rows, "seq", 1)
+    before_rows = shifted(last_rows, 1)
     extended = jnp.concatenate([before_rows, projected], axis=0)
     filtered = jnp.broadcast_to(conv_bias[None, :], (length, COLS))
     for kernel_tap in range(CONV):
@@ -108,7 +108,7 @@
         return (jnp.exp(span_total)[:, None, None] * held_state + state_piece, None)
 
     local_end, _ = lax.scan(gather_local, zero_state, (totals, states))
-    entering_dev = incoming(local_end, device_total)
+    entering_dev = scan_entering(device_total, local_end)
 
     def emit(held_state, inputs):
         x_heads, b_span, c_span, cum_span, step_span, span_total, state_piece = inputs
@@ -128,7 +128,8 @@
 
 
 def solution(mesh):
-    placed = (P("dp", "seq", None), P("dp", None, "seq"), P(("dp", "seq"), None), P(), P(), P())
+    split = Mesh(mesh.devices.reshape(mesh.shape["dp"], mesh.shape["seq"] // 2, 2), ("dp", "y", "core"))
+    placed = (P("dp", SEQ, None), P("dp", None, SEQ), P(("dp",) + SEQ, None), P(), P(), P())
     return jax.shard_map(
-        body, mesh=mesh, in_specs=placed, out_specs=P("dp", "seq", None), check_vma=False
+        body, mesh=split, in_specs=placed, out_specs=P("dp", SEQ, None), check_vma=False
     )

time: 385 us -> 615 us (1.60)
  local copies, waits for them, and re-layouts: 86.5 us -> 262 us
  waiting for transfers between devices: 182 us -> 225 us
  starting transfers between devices: 2.21 us -> 19.1 us
  blocking collectives: 10.5 us -> 0 us
    dynamic_update_slice x0 -> x6, local copies, waits for them, and re-layouts: none -> 179 us  [body(): lax.scan(emit, entering_dev, (x_all, b_all, c_all, cumulative, steps_all,...]
    ppermute x1 -> x9, waiting for transfers between devices: 2.73 us -> 88.8 us  [the longest x8 88.8 us: shifted(): return lax.ppermute(array, SEQ, pairs)]
    all_gather x2 -> x1, waiting for transfers between devices: 179 us -> 136 us  [project(): mine = lax.all_gather(input_weight, ('dp', 'y'), axis=0, tiled=True)]
    reshape x4 -> x3, local copies, waits for them, and re-layouts: 28.5 us -> 7.83 us  [the longest x1 7.71 us: project(): return jnp.stack([p0.reshape(length, groups, rows), p1.reshape(length, gr...]
    ppermute x1 -> x9, starting transfers between devices: 2.17 us -> 19.1 us  [the longest x8 19.1 us: shifted(): return lax.ppermute(array, SEQ, pairs)]
    another operation x2 -> x5, local copies, waits for them, and re-layouts: 0.15 us -> 13.8 us  [the longest x4 13.8 us: project(): jnp.stack([p0.reshape(length, groups, rows), p1.reshape(length, groups, r...]
    unnamed x1 -> x0, blocking collectives: 10.5 us -> none
    unnamed x16 -> x15, local copies, waits for them, and re-layouts: 31 us -> 21 us
  transfers between devices with their start and end apart: 3 -> 10, of which waited for: 3 -> 7; matrix products, arithmetic and copies ran while one was open for 1% -> 5% of each run, Pallas kernels for 0% -> 0%
where the time goes in v1:
time: 615 us; the launch traced here: 608 us
  local copies, waits for them, and re-layouts  262 us (43%)
  waiting for transfers between devices  225 us (37%)
  matrix products  50.5 us (8%)
  other arithmetic  37.3 us (6%)
  starting transfers between devices  19.1 us (3%)
  between operations  13.7 us (2%)
    dynamic_update_slice x6, local copies, waits for them, and re-layouts, body(): lax.scan(emit, entering_dev, (x_all, b_all, c_all, cumulative, steps_all,...  179 us
    all_gather x1, waiting for transfers between devices, project(): mine = lax.all_gather(input_weight, ('dp', 'y'), axis=0, tiled=True)  136 us
    ppermute x8, waiting for transfers between devices, shifted(): return lax.ppermute(array, SEQ, pairs)  88.8 us
    unnamed x15, local copies, waits for them, and re-layouts  21 us
    ppermute x8, starting transfers between devices, shifted(): return lax.ppermute(array, SEQ, pairs)  19.1 us
    convert_element_type x1, other arithmetic, body(): active = jax.nn.silu(filtered).astype(jnp.bfloat16)  15.4 us
    another operation x4, local copies, waits for them, and re-layouts, project(): jnp.stack([p0.reshape(length, groups, rows), p1.reshape(length, groups, r...  13.8 us
    dot_general x3, matrix products, mixing_output(): jnp.einsum('hqk,khp->qhp', mixing, x_heads, preferred_element_type=jnp.fl...  12.8 us
  transfers between devices with their start and end apart: 10, of which 7 were waited for; matrix products, arithmetic and copies ran while one was open for 5% of the time, Pallas kernels for 0%

profile of v1, /device:TPU:16, one launch (start us, length us, event | category | flops | bytes accessed | tf_op | source)
XLA Modules:
  0.0 607.9 jit_solution(4100899505798613028)
XLA Ops:
  7.3 135.9 %all-gather.3.cloned.1.call-done = bf16[128,11,2560]{2,1,0:T(8,128)(2,1)} async-done(((bf16[1,11,2560]{2,1,0:T(8,128)(2,1)}), bf16[128,11,2560]{2,1,0:T(8,128)(2,1)}) %all-gather.3.cloned.1.call-update) | async-done | bytes 7208976 | tf_op jit(solution)/shard_map/all_gather | solution.py:59
  143.2 13.2 %reshape.82 = bf16[1408,2560]{1,0:T(8,128)(2,1)} reshape(bf16[128,11,2560]{2,1,0:T(8,128)(2,1)} %all-gather.3.cloned.1.call-done) | data formatting | bytes 14417920
  158.8 10.3 %fusion.40 = bf16[768,1408]{1,0:T(8,128)(2,1)S(1)} fusion(bf16[1408,2560]{1,0:T(8,128)(2,1)} %reshape.82, bf16[1,768,2560]{2,1,0:T(8,128)(2,1)} %param.12), kind=kOutput, calls=%fused_computation.64 | convolution fusion | flops 5537562624 | bytes 13303808 | tf_op jit(solution)/shard_map/dot_general | solution.py:62
  169.2 10.6 %broadcast_select_fusion = (bf16[768,1408]{1,0:T(8,128)(2,1)}, bf16[768,1408]{1,0:T(8,128)(2,1)S(1)}) fusion(bf16[768,1408]{1,0:T(8,128)(2,1)S(1)} %fusion.40, pred[]{:T(512)S(6)} %eq.3, bf16[1408,2560]{1,0:T(8,128)(2,1)} %collective-permute-done.3, bf16[1,768,2560]{2,1,0:T(8,128)(2,1)S(1)} %copy-done.5), kind=kOutput, calls=%fused_computation.66 | convolution fusion | flops 5539725312 | bytes 17629184 | tf_op jit(solution)/shard_map/dot_general | solution.py:63
  179.7 2.5 copy.56
  182.2 2.8 stack_reshape.6
  186.8 4.2 copy.57
  191.1 2.8 stack_reshape.7
  199.6 2.6 collective-permute-start.4
  202.4 6.4 %copy.59 = bf16[768,128,2,11]{0,3,2,1:T(8,128)(2,1)} copy(bf16[768,128,2,11]{0,3,1,2:T(8,128)(2,1)} %constant_dynamic-update-slice_fusion) | data formatting | bytes 8650752 | tf_op jit(solution)/shard_map/stack | solution.py:69
  208.8 7.7 %reshape.72 = bf16[768,2816]{0,1:T(8,128)(2,1)} reshape(bf16[768,128,2,11]{0,3,2,1:T(8,128)(2,1)} %copy.59) | data formatting | bytes 8650752 | tf_op jit(solution)/shard_map/reshape | solution.py:71
  217.0 15.4 %multiply_convert_fusion.5 = bf16[768,2816]{0,1:T(8,128)(2,1)S(1)} fusion(bf16[768,2816]{0,1:T(8,128)(2,1)} %reshape.72, bf16[3,2816]{0,1:T(8,128)(2,1)S(1)} %copy.60, f32[2816]{0:T(1024)S(1)} %get-tuple-element.197, f32[2816]{0:T(1024)S(1)} %get-tuple-element.198, f32[2816]{0:T(1024)S(1)} %get-tuple-element.196, f32[2816]{0:T(1024)S(1)} %get-tuple-element.195, ...), kind=kLoop, calls=%fused_computation.50 | loop fusion | flops 56229888 | bytes 8723968 | tf_op jit(solution)/shard_map/convert_element_type | solution.py:88
  233.2 2.5 slice.72
  235.8 11.3 %reshape.73 = bf16[3,256,40,64]{1,0,3,2:T(4,128)(2,1)} reshape(bf16[768,2560]{0,1:T(8,128)(2,1)} %slice.72) | data formatting | bytes 7864320 | tf_op jit(solution)/shard_map/reshape | solution.py:90
  247.1 5.2 copy.62
  252.3 9.8 %while.33 = (s32[]{:T(128)}, f32[3,40,64,128]{3,2,1,0:T(8,128)}, bf16[3,256,40,64]{1,3,2,0:T(8,128)(2,1)}, f32[3,40,256]{2,1,0:T(8,128)S(1)}, f32[3,40,256]{2,0,...) while((s32[]{:T(128)}, f32[3,40,64,128]{3,2,1,0:T(8,128)}, bf16[3,256,40,64]{1,3,2,0:T(8,128)(2,1)}, ...), condition=%wide.region_4.5_spmd, body=%wide.region_3.4_spmd.sunk | while | flops 169758720 | bytes 3262517 | solution.py:104
  252.6 2.9 fusion.67
  255.9 2.9 fusion.67
  259.2 2.9 fusion.67
  262.1 4.7 while.35
  266.8 2.7 collective-permute-start.5
  269.5 16.2 %collective-permute-done.5 = f32[40,64,128]{2,1,0:T(8,128)S(1)} collective-permute-done((f32[40,64,128]{2,1,0:T(8,128)S(1)}, f32[40,64,128]{2,1,0:T(8,128)S(1)}, u32[]{:S(2)}, u32[]{:S(2)}) %collective-permute-start.5) | collective-permute-done | bytes 1310752 | tf_op jit(solution)/shard_map/ppermute | solution.py:43
  287.6 3.2 collective-permute-start
  290.8 13.8 %collective-permute-done = f32[40]{0:T(128)S(1)} collective-permute-done((f32[40]{0:T(128)S(1)}, f32[40]{0:T(128)S(1)}, u32[]{:S(2)}, u32[]{:S(2)}) %collective-permute-start) | collective-permute-done | bytes 192 | tf_op jit(solution)/shard_map/ppermute | solution.py:43
  306.6 2.9 collective-permute-done.1
  309.8 3.1 collective-permute-start.7
  312.9 28.5 %collective-permute-done.7 = f32[40,64,128]{2,1,0:T(8,128)S(1)} collective-permute-done((f32[40,64,128]{2,1,0:T(8,128)S(1)}, f32[40,64,128]{2,1,0:T(8,128)S(1)}, u32[]{:S(2)}, u32[]{:S(2)}) %collective-permute-start.7) | collective-permute-done | bytes 1310752 | tf_op jit(solution)/shard_map/ppermute | solution.py:43
  345.5 3.3 collective-permute-done.2
  350.0 23.9 %collective-permute-done.8 = f32[40,64,128]{2,1,0:T(8,128)S(1)} collective-permute-done((f32[40,64,128]{2,1,0:T(8,128)S(1)}, f32[40,64,128]{2,1,0:T(8,128)S(1)}, u32[]{:S(2)}, u32[]{:S(2)}) %collective-permute-start.8) | collective-permute-done | bytes 1310752 | tf_op jit(solution)/shard_map/ppermute | solution.py:43
  375.1 209.5 %while.34 = (s32[]{:T(128)}, f32[40,64,128]{2,1,0:T(8,128)}, f32[3,256,40,64]{1,0,3,2:T(4,128)}, f32[3,40]{1,0:T(4,128)S(1)}, f32[3,40,64,128]{3,2,1,0:T(8,128)}...) while((s32[]{:T(128)}, f32[40,64,128]{2,1,0:T(8,128)}, ...), condition=%wide.region_8.9_spmd, body=%wide.region_7.8_spmd.sunk | while | flops 1374093312 | bytes 26208364 | solution.py:120
  375.1 2.5 fusion.74
  378.0 4.3 fusion.76
  382.3 2.9 copy.94
  385.2 56.8 %dynamic_update_slice.12 = f32[3,256,40,64]{1,0,3,2:T(4,128)} dynamic-update-slice(f32[3,256,40,64]{1,0,3,2:T(4,128)} %get-tuple-element.428, f32[1,256,40,64]{1,0,3,2:T(1,128)S(1)} %copy.94, s32[]{:T(128)} %get-tuple-element.426, s32[]{:T(128)} %constant.52.clone.1..sunk, s32[]{:T(128)} %constant.52.clone.1..sunk, s32[]{:T(128)} %constant.52.clone.1..sunk) | dynamic-update-slice | bytes 5242884 | tf_op jit(solution)/shard_map/while/body/jit(dynamic_update_index_in_dim)/dynamic_update_slice | solution.py:120
  442.0 3.0 bitcast_add_fusion.5
  445.0 2.5 fusion.74
  447.8 4.3 fusion.76
  452.1 2.9 copy.94
  455.0 56.8 %dynamic_update_slice.12 = f32[3,256,40,64]{1,0,3,2:T(4,128)} dynamic-update-slice(f32[3,256,40,64]{1,0,3,2:T(4,128)} %get-tuple-element.428, f32[1,256,40,64]{1,0,3,2:T(1,128)S(1)} %copy.94, s32[]{:T(128)} %get-tuple-element.426, s32[]{:T(128)} %constant.52.clone.1..sunk, s32[]{:T(128)} %constant.52.clone.1..sunk, s32[]{:T(128)} %constant.52.clone.1..sunk) | dynamic-update-slice | bytes 5242884 | tf_op jit(solution)/shard_map/while/body/jit(dynamic_update_index_in_dim)/dynamic_update_slice | solution.py:120
  511.8 3.0 bitcast_add_fusion.5
  514.8 2.5 fusion.74
  517.6 4.3 fusion.76
  521.9 2.9 copy.94
  524.9 56.8 %dynamic_update_slice.12 = f32[3,256,40,64]{1,0,3,2:T(4,128)} dynamic-update-slice(f32[3,256,40,64]{1,0,3,2:T(4,128)} %get-tuple-element.428, f32[1,256,40,64]{1,0,3,2:T(1,128)S(1)} %copy.94, s32[]{:T(128)} %get-tuple-element.426, s32[]{:T(128)} %constant.52.clone.1..sunk, s32[]{:T(128)} %constant.52.clone.1..sunk, s32[]{:T(128)} %constant.52.clone.1..sunk) | dynamic-update-slice | bytes 5242884 | tf_op jit(solution)/shard_map/while/body/jit(dynamic_update_index_in_dim)/dynamic_update_slice | solution.py:120
  581.6 3.0 bitcast_add_fusion.5
  584.6 5.9 copy.81
  590.6 4.3 fusion.35
  594.8 6.3 %copy.69 = bf16[1,768,2560]{2,1,0:T(8,128)(2,1)} copy(bf16[1,768,2560]{1,2,0:T(8,128)(2,1)} %fusion.35) | data formatting | bytes 7864320 | tf_op jit(solution)/shard_map/convert_element_type | solution.py:127
  (97 shorter events, 29.4 us)
Async XLA Ops:
  6.5 136.6 %all-gather.3.cloned.1.call-start = ((), (), s32[]{:S(2)}) async-start(), calls=%async_computation | async-start | bytes 10567680 | tf_op jit(solution)/shard_map/all_gather | solution.py:59
  7.3 149.1 %copy-start.1 = (f32[1,40,768]{2,1,0:T(8,128)S(1)}, f32[1,40,768]{2,1,0:T(8,128)}, u32[]{:S(2)}) copy-start(f32[1,40,768]{2,1,0:T(8,128)} %param.13) | copy-start | bytes 368644
  7.3 151.3 %copy-start.2 = (bf16[4,2816]{1,0:T(4,128)(2,1)S(1)}, bf16[4,2816]{1,0:T(4,128)(2,1)}, u32[]{:S(2)}) copy-start(bf16[4,2816]{1,0:T(4,128)(2,1)} %param.15) | copy-start | bytes 67588
  156.3 12.8 %collective-permute-start.3 = (bf16[1408,2560]{1,0:T(8,128)(2,1)}, bf16[1408,2560]{1,0:T(8,128)(2,1)}, u32[]{:S(2)}, u32[]{:S(2)}) collective-permute-start(bf16[1408,2560]{1,0:T(8,128)(2,1)} %reshape.82), channel_id=1, source_target_pairs={{0,1},{1,0},{2,3},{3,2},{4,5},{5,4},{6,7},{7,6},{8,9},{9,8},{10,11... | collective-permute-start | bytes 21626888 | tf_op jit(solution)/shard_map/ppermute | solution.py:60
  158.8 10.3 %copy-start.5 = (bf16[1,768,2560]{2,1,0:T(8,128)(2,1)S(1)}, bf16[1,768,2560]{2,1,0:T(8,128)(2,1)}, u32[]{:S(2)}) copy-start(bf16[1,768,2560]{2,1,0:T(8,128)(2,1)} %param.12) | copy-start | bytes 11796484
  199.6 17.0 %collective-permute-start.4 = (bf16[3,2816]{1,0:T(4,128)(2,1)S(1)}, bf16[3,2816]{1,0:T(4,128)(2,1)S(1)}, u32[]{:S(2)}, u32[]{:S(2)}) collective-permute-start(bf16[3,2816]{1,0:T(4,128)(2,1)S(1)} %slice.52), channel_id=1, source_target_pairs={{0,1},{1,2},{2,3},{3,4},{4,5},{5,6},{6,7},{8,9},{9,10},{10,11},{11... | collective-permute-start | bytes 50696 | tf_op jit(solution)/shard_map/ppermute | solution.py:43
  208.8 8.1 %copy-start.3 = (f32[2816]{0:T(1024)S(1)}, f32[2816]{0:T(1024)}, u32[]{:S(2)}) copy-start(f32[2816]{0:T(1024)} %param.16) | copy-start | bytes 33796
  232.4 3.3 copy-start
  266.8 18.9 %collective-permute-start.5 = (f32[40,64,128]{2,1,0:T(8,128)S(1)}, f32[40,64,128]{2,1,0:T(8,128)S(1)}, u32[]{:S(2)}, u32[]{:S(2)}) collective-permute-start(f32[40,64,128]{2,1,0:T(8,128)S(1)} %get-tuple-element.112), channel_id=1, source_target_pairs={{0,1},{1,2},{2,3},{3,4},{4,5},{5,6},{6,7},{8,9},{9,10},{10,11},{11... | collective-permute-start | bytes 3932168 | tf_op jit(solution)/shard_map/ppermute | solution.py:43
  285.7 23.8 %collective-permute-start.6 = (f32[40,64,128]{2,1,0:T(8,128)S(1)}, f32[40,64,128]{2,1,0:T(8,128)S(1)}, u32[]{:S(2)}, u32[]{:S(2)}) collective-permute-start(f32[40,64,128]{2,1,0:T(8,128)S(1)} %collective-permute-done.5), channel_id=1, source_target_pairs={{0,1},{1,2},{2,3},{3,4},{4,5},{5,6},{6,7},{8,9},{9,10},{10,11},{11... | collective-permute-start | bytes 3932168 | tf_op jit(solution)/shard_map/ppermute | solution.py:43
  287.6 17.1 %collective-permute-start = (f32[40]{0:T(128)S(1)}, f32[40]{0:T(128)S(1)}, u32[]{:S(2)}, u32[]{:S(2)}) collective-permute-start(f32[40]{0:T(128)S(1)} %get-tuple-element.193), channel_id=1, source_target_pairs={{0,1},{1,2},{2,3},{3,4},{4,5},{5,6},{6,7},{8,9},{9,10},{10,11},{11... | collective-permute-start | bytes 488 | tf_op jit(solution)/shard_map/ppermute | solution.py:43
  304.7 4.8 collective-permute-start.1
  309.5 35.8 %copy-start.4 = (f32[40]{0:T(128)S(1)}, f32[40]{0:T(128)}, u32[]{:S(2)}) copy-start(f32[40]{0:T(128)} %param.17) | copy-start | bytes 484
  309.8 31.6 %collective-permute-start.7 = (f32[40,64,128]{2,1,0:T(8,128)S(1)}, f32[40,64,128]{2,1,0:T(8,128)S(1)}, u32[]{:S(2)}, u32[]{:S(2)}) collective-permute-start(f32[40,64,128]{2,1,0:T(8,128)S(1)} %multiply_add_fusion.2), channel_id=1, source_target_pairs={{0,2},{1,3},{2,4},{3,5},{4,6},{5,7},{8,10},{9,11},{10,12},{11,13},... | collective-permute-start | bytes 3932168 | tf_op jit(solution)/shard_map/ppermute | solution.py:43
  341.6 32.2 %collective-permute-start.8 = (f32[40,64,128]{2,1,0:T(8,128)S(1)}, f32[40,64,128]{2,1,0:T(8,128)S(1)}, u32[]{:S(2)}, u32[]{:S(2)}) collective-permute-start(f32[40,64,128]{2,1,0:T(8,128)S(1)} %multiply_add_fusion.1), channel_id=1, source_target_pairs={{0,4},{1,5},{2,6},{3,7},{8,12},{9,13},{10,14},{11,15},{16,20},{17,... | collective-permute-start | bytes 3932168 | tf_op jit(solution)/shard_map/ppermute | solution.py:43
  343.0 5.9 collective-permute-start.2
Sparse Core Ops, SparseCore 0:
  10.8 132.2 all-gather.2

commit v2 on v1

v2 whole, which is shorter than its diff:
```python
import jax
import jax.numpy as jnp
from jax import lax
from jax.experimental import pallas as pl
from jax.sharding import Mesh, PartitionSpec as P

HALF_HEADS = 40
HEAD_DIM = 64
STATE = 128
SPAN = 256
CONV = 4
INNER = 2560
COLS = 2816
GROUP = 8
SEQ = ("y", "core")


def shifted(array, by):
    peers = lax.axis_size(SEQ)
    pairs = [(i, i + by) for i in range(peers) if i + by < peers]
    return lax.ppermute(array, SEQ, pairs)


def scan_entering(total, state):
    acc_total, acc_state = shifted(total, 1), shifted(state, 1)
    by = 1
    while by < lax.axis_size(SEQ):
        got_total, got_state = shifted(acc_total, by), shifted(acc_state, by)
        acc_state = jnp.exp(acc_total)[:, None, None] * got_state + acc_state
        acc_total = acc_total + got_total
        by *= 2
    return acc_state


def pair_lanes(columns, pair):
    lane = lax.broadcasted_iota(jnp.int32, (columns.shape[0], 2 * HEAD_DIM), 1)
    return jnp.where(lane < HEAD_DIM, columns[:, 2 * pair : 2 * pair + 1], columns[:, 2 * pair + 1 : 2 * pair + 2])


def states_kernel(x_ref, b_ref, cum_ref, step_ref, out_ref):
    cum = cum_ref[0]
    weight = jnp.exp(cum[SPAN - 1 : SPAN, :] - cum) * step_ref[0]
    b_span = b_ref[...]
    for pair in range(GROUP // 2):
        lanes = slice(2 * HEAD_DIM * pair, 2 * HEAD_DIM * (pair + 1))
        decayed = (x_ref[:, lanes].astype(jnp.float32) * pair_lanes(weight, pair)).astype(jnp.bfloat16)
        out_ref[0, lanes, :] = lax.dot_general(
            decayed, b_span, (((0,), (0,)), ((), ())), preferred_element_type=jnp.float32
        )


def output_kernel(x_ref, b_ref, c_ref, cum_ref, cum_row_ref, step_row_ref, enter_ref, gain_ref, out_ref):
    c_span = c_ref[...]
    scores = lax.dot_general(c_span, b_ref[...], (((1,), (1,)), ((), ())), preferred_element_type=jnp.float32)
    causal = lax.broadcasted_iota(jnp.int32, (SPAN, SPAN), 0) >= lax.broadcasted_iota(jnp.int32, (SPAN, SPAN), 1)
    cum = cum_ref[0]
    rise = jnp.exp(cum)
    c32 = c_span.astype(jnp.float32)
    lane = lax.broadcasted_iota(jnp.int32, (SPAN, 2 * HEAD_DIM), 1)
    for pair in range(GROUP // 2):
        lanes = slice(2 * HEAD_DIM * pair, 2 * HEAD_DIM * (pair + 1))
        x_pair = x_ref[:, lanes]
        parts = []
        for half in range(2):
            head = 2 * pair + half
            spread = cum[:, head : head + 1] - cum_row_ref[head : head + 1, :]
            decay = jnp.where(causal, jnp.exp(jnp.where(causal, spread, 0.0)), 0.0)
            mixing = (scores * decay * step_row_ref[head : head + 1, :]).astype(jnp.bfloat16)
            parts.append(jnp.dot(mixing, x_pair, preferred_element_type=jnp.float32))
        intra = jnp.where(lane < HEAD_DIM, parts[0], parts[1])
        readout = lax.dot_general(
            c32, enter_ref[0, lanes, :], (((1,), (1,)), ((), ())),
            precision=lax.Precision.HIGHEST, preferred_element_type=jnp.float32,
        )
        total = intra + pair_lanes(rise, pair) * readout + gain_ref[:, lanes] * x_pair.astype(jnp.float32)
        out_ref[:, lanes] = total.astype(jnp.bfloat16)


def project(token_rows, input_weight):
    rows = input_weight.shape[0]
    mine = lax.all_gather(input_weight, ("dp", "y"), axis=0, tiled=True)
    other = lax.ppermute(mine, "core", [(0, 1), (1, 0)])
    dims = (((1,), (1,)), ((), ()))
    p_mine = lax.dot_general(token_rows, mine, dims, preferred_element_type=jnp.float32).astype(jnp.bfloat16)
    p_other = lax.dot_general(token_rows, other, dims, preferred_element_type=jnp.float32).astype(jnp.bfloat16)
    first = lax.axis_index("core") == 0
    p0 = jnp.where(first, p_mine, p_other)
    p1 = jnp.where(first, p_other, p_mine)
    length = token_rows.shape[0]
    groups = mine.shape[0] // rows
    return jnp.stack(
        [p0.reshape(length, groups, rows), p1.reshape(length, groups, rows)], axis=2
    ).reshape(length, COLS)


def body(hidden, log_decay, input_weight, conv_weight, conv_bias, skip_gain):
    token_rows = hidden[0]
    length = token_rows.shape[0]
    span_count = length // SPAN
    groups = HALF_HEADS // GROUP
    projected = project(token_rows, input_weight)
    before_rows = shifted(projected[length - (CONV - 1) :], 1)
    extended = jnp.concatenate([before_rows, projected], axis=0)
    filtered = jnp.broadcast_to(conv_bias[None, :], (length, COLS))
    for kernel_tap in range(CONV):
        filtered = (
            filtered
            + extended[kernel_tap : kernel_tap + length].astype(jnp.float32)
            * conv_weight[kernel_tap].astype(jnp.float32)[None, :]
        )
    active = jax.nn.silu(filtered).astype(jnp.bfloat16)

    decay = log_decay[0]
    cum_row = jnp.cumsum(decay.reshape(HALF_HEADS, span_count, SPAN), axis=2).reshape(HALF_HEADS, length)
    step_row = -decay
    cum_grouped = cum_row.reshape(groups, GROUP, length).transpose(0, 2, 1)
    step_grouped = step_row.reshape(groups, GROUP, length).transpose(0, 2, 1)
    totals = cum_row.reshape(HALF_HEADS, span_count, SPAN)[:, :, -1].T

    x_spec = pl.BlockSpec((SPAN, GROUP * HEAD_DIM), lambda c, g: (c, g))
    b_spec = pl.BlockSpec((SPAN, STATE), lambda c, g: (c, INNER // STATE))
    c_spec = pl.BlockSpec((SPAN, STATE), lambda c, g: (c, INNER // STATE + 1))
    col_spec = pl.BlockSpec((1, SPAN, GROUP), lambda c, g: (g, c, 0))
    row_spec = pl.BlockSpec((GROUP, SPAN), lambda c, g: (g, c))
    state_spec = pl.BlockSpec((1, GROUP * HEAD_DIM, STATE), lambda c, g: (c, g, 0))
    states = pl.pallas_call(
        states_kernel,
        grid=(span_count, groups),
        in_specs=[x_spec, b_spec, col_spec, col_spec],
        out_specs=state_spec,
        out_shape=jax.ShapeDtypeStruct((span_count, INNER, STATE), jnp.float32),
    )(active, active, cum_grouped, step_grouped)
    states = states.reshape(span_count, HALF_HEADS, HEAD_DIM, STATE)

    local = jnp.zeros((HALF_HEADS, HEAD_DIM, STATE), jnp.float32)
    for span in range(span_count):
        local = jnp.exp(totals[span])[:, None, None] * local + states[span]
    held = scan_entering(jnp.sum(totals, axis=0), local)
    entering = []
    for span in range(span_count):
        entering.append(held)
        held = jnp.exp(totals[span])[:, None, None] * held + states[span]
    entering = jnp.stack(entering).reshape(span_count, INNER, STATE)

    gain = jnp.repeat(skip_gain, HEAD_DIM)[None, :]
    out = pl.pallas_call(
        output_kernel,
        grid=(span_count, groups),
        in_specs=[
            x_spec, b_spec, c_spec, col_spec, row_spec, row_spec, state_spec,
            pl.BlockSpec((1, GROUP * HEAD_DIM), lambda c, g: (0, g)),
        ],
        out_specs=x_spec,
        out_shape=jax.ShapeDtypeStruct((length, INNER), jnp.bfloat16),
    )(active, active, active, cum_grouped, cum_row, step_row, entering, gain)
    return out[None]


def solution(mesh):
    split = Mesh(mesh.devices.reshape(mesh.shape["dp"], mesh.shape["seq"] // 2, 2), ("dp", "y", "core"))
    placed = (P("dp", SEQ, None), P("dp", None, SEQ), P(("dp",) + SEQ, None), P(), P(), P())
    return jax.shard_map(
        body, mesh=split, in_specs=placed, out_specs=P("dp", SEQ, None), check_vma=False
    )
```

time: 615 us -> 402 us (0.65)
  local copies, waits for them, and re-layouts: 262 us -> 61.6 us
  Pallas kernels: 0 us -> 37 us
  matrix products: 50.5 us -> 20.9 us
  other arithmetic: 37.3 us -> 23 us
    dynamic_update_slice x6 -> x0, local copies, waits for them, and re-layouts: 179 us -> none  [body(): lax.scan(emit, entering_dev, (x_all, b_all, c_all, cumulative, steps_all,...]
    pallas_call x0 -> x2, Pallas kernels: none -> 37 us  [the longest x1 21.1 us: body(): pl.pallas_call(output_kernel, grid=(span_count, groups), in_specs=[x_spec...]
    dot_general x12 -> x0, matrix products: 29.6 us -> none  [the longest x3 12.8 us: mixing_output(): jnp.einsum('hqk,khp->qhp', mixing, x_heads, preferred_element_type=jnp.fl...]
    reshape x3 -> x2, local copies, waits for them, and re-layouts: 11.4 us -> 0.07 us  [the longest x1 11.3 us: body(): x_all = active[:, :INNER].reshape(span_count, SPAN, HALF_HEADS, HEAD_DIM)]
    add x6 -> x2, other arithmetic: 13.5 us -> 2.45 us  [the longest x1 2.12 us: body(): held = jnp.exp(totals[span])[:, None, None] * held + states[span]]
    reshape x1 -> x2, local copies, waits for them, and re-layouts: 7.71 us -> 14.2 us  [project(): return jnp.stack([p0.reshape(length, groups, rows), p1.reshape(length, gr...]
    convert_element_type x1 -> x0, local copies, waits for them, and re-layouts: 6.28 us -> none  [body(): return final.reshape(1, length, INNER).astype(jnp.bfloat16)]
    unnamed x15 -> x12, local copies, waits for them, and re-layouts: 21 us -> 15 us
  transfers between devices with their start and end apart: 10 -> 10, of which waited for: 7 -> 7; matrix products, arithmetic and copies ran while one was open for 5% -> 10% of each run, Pallas kernels for 0% -> 0%
where the time goes in v2:
time: 402 us; the launch traced here: 401 us
  waiting for transfers between devices  226 us (56%)
  local copies, waits for them, and re-layouts  61.6 us (15%)
  Pallas kernels  37 us (9%)
  other arithmetic  23 us (6%)
  matrix products  20.9 us (5%)
  starting transfers between devices  18.9 us (5%)
  between operations  13.7 us (3%)
    all_gather x1, waiting for transfers between devices, project(): mine = lax.all_gather(input_weight, ('dp', 'y'), axis=0, tiled=True)  136 us
    ppermute x8, waiting for transfers between devices, shifted(): return lax.ppermute(array, SEQ, pairs)  89.1 us
    pallas_call x1, Pallas kernels, body(): pl.pallas_call(output_kernel, grid=(span_count, groups), in_specs=[x_spec...  21.1 us
    ppermute x8, starting transfers between devices, shifted(): return lax.ppermute(array, SEQ, pairs)  18.9 us
    pallas_call x1, Pallas kernels, body(): pl.pallas_call(states_kernel, grid=(span_count, groups), in_specs=[x_spec...  15.9 us
    unnamed x12, local copies, waits for them, and re-layouts  15 us
    reshape x2, local copies, waits for them, and re-layouts, project(): return jnp.stack([p0.reshape(length, groups, rows), p1.reshape(length, gr...  14.2 us
    convert_element_type x1, other arithmetic, body(): active = jax.nn.silu(filtered).astype(jnp.bfloat16)  14 us
  transfers between devices with their start and end apart: 10, of which 7 were waited for; matrix products, arithmetic and copies ran while one was open for 10% of the time, Pallas kernels for 0%

profile of v2, /device:TPU:16, one launch (start us, length us, event | category | flops | bytes accessed | tf_op | source)
XLA Modules:
  0.0 400.8 jit_solution(16497899232845801511)
XLA Ops:
  6.5 0.7 all-gather.3.cloned.1.call-update
  7.3 135.9 %all-gather.3.cloned.1.call-done = bf16[128,11,2560]{2,1,0:T(8,128)(2,1)} async-done(((bf16[1,11,2560]{2,1,0:T(8,128)(2,1)}), bf16[128,11,2560]{2,1,0:T(8,128)(2,1)}) %all-gather.3.cloned.1.call-update) | async-done | bytes 7208976 | tf_op jit(solution)/shard_map/all_gather | solution.py:81
  143.2 13.1 %reshape.72 = bf16[1408,2560]{1,0:T(8,128)(2,1)} reshape(bf16[128,11,2560]{2,1,0:T(8,128)(2,1)} %all-gather.3.cloned.1.call-done) | data formatting | bytes 14417920
  156.4 1.8 reduce-window.6
  158.5 0.2 slice_reduce_fusion.1
  158.8 0.7 negate_bitcast_fusion
  159.6 10.3 %fusion.6 = bf16[768,1408]{1,0:T(8,128)(2,1)S(1)} fusion(bf16[1408,2560]{1,0:T(8,128)(2,1)} %reshape.72, bf16[1,768,2560]{2,1,0:T(8,128)(2,1)} %param.6), kind=kOutput, calls=%fused_computation.11 | convolution fusion | flops 5537562624 | bytes 13303808 | tf_op jit(solution)/shard_map/dot_general | solution.py:84
  169.9 10.6 %broadcast_select_fusion = (bf16[768,1408]{1,0:T(8,128)(2,1)}, bf16[768,1408]{1,0:T(8,128)(2,1)S(1)}) fusion(bf16[768,1408]{1,0:T(8,128)(2,1)S(1)} %fusion.6, pred[]{:T(512)S(6)} %eq.3, bf16[1408,2560]{1,0:T(8,128)(2,1)} %collective-permute-done, bf16[1,768,2560]{2,1,0:T(8,128)(2,1)S(1)} %copy-done.4), kind=kOutput, calls=%fused_computation.13 | convolution fusion | flops 5539725312 | bytes 17629184 | tf_op jit(solution)/shard_map/dot_general | solution.py:85
  180.5 2.5 copy.40
  182.9 2.8 stack_reshape.6
  185.7 1.9 constant_dynamic-update-slice_fusion.1
  187.6 4.2 %copy.41 = bf16[768,1408]{0,1:T(8,128)(2,1)} copy(bf16[768,1408]{1,0:T(8,128)(2,1)} %get-tuple-element.16) | data formatting | bytes 4325376 | tf_op jit(solution)/shard_map/jit(_where)/select_n | solution.py:88
  191.7 2.8 stack_reshape.7
  194.5 1.9 constant_dynamic-update-slice_fusion
  196.4 1.6 slice.79
  198.0 2.0 copy.42
  200.0 0.3 slice.62
  200.2 2.6 collective-permute-start.1
  202.9 0.1 convert_reduce_fusion.3
  203.2 1.9 copy.50
  205.0 1.9 copy.53
  206.9 6.4 %copy.43 = bf16[768,128,2,11]{0,3,2,1:T(8,128)(2,1)} copy(bf16[768,128,2,11]{0,3,1,2:T(8,128)(2,1)} %constant_dynamic-update-slice_fusion) | data formatting | bytes 8650752 | tf_op jit(solution)/shard_map/stack | solution.py:91
  213.3 7.7 %reshape.64 = bf16[768,2816]{0,1:T(8,128)(2,1)} reshape(bf16[768,128,2,11]{0,3,2,1:T(8,128)(2,1)} %copy.43) | data formatting | bytes 8650752 | tf_op jit(solution)/shard_map/reshape | solution.py:93
  221.0 6.5 %copy.44 = bf16[768,2816]{1,0:T(8,128)(2,1)} copy(bf16[768,2816]{0,1:T(8,128)(2,1)} %reshape.64) | data formatting | bytes 8650752 | tf_op jit(solution)/shard_map/reshape | solution.py:93
  227.6 14.0 %multiply_convert_fusion.x_ref.b_ref.c_ref = bf16[768,2816]{1,0:T(8,128)(2,1)} fusion(bf16[768,2816]{1,0:T(8,128)(2,1)} %copy.44, bf16[3,2816]{1,0:T(4,128)(2,1)S(1)} %collective-permute-done.1, f32[2816]{0:T(1024)S(1)} %get-tuple-element.9, f32[2816]{0:T(1024)S(1)} %get-tuple-element.10, f32[2816]{0:T(1024)S(1)} %get-tuple-element.8, ...), kind=kLoop, calls=%fused_computation | loop fusion | flops 56229888 | bytes 8723968 | tf_op jit(solution)/shard_map/convert_element_type | solution.py:111
  241.5 15.9 %shard_map.64 = f32[3,2560,128]{2,1,0:T(8,128)} custom-call(bf16[768,2816]{1,0:T(8,128)(2,1)} %multiply_convert_fusion.x_ref.b_ref.c_ref, bf16[768,2816]{1,0:T(8,128)(2,1)} %multiply_convert_fusion.x_ref.b_ref.c_ref, f32[5,768,8]{2,1,0:T(8,128)} %bitcast.48, f32[5,768,8]{2,1,0:T(8,128)} %bitcast.54), custom_call_target="tpu_custom_call" | custom-call | tf_op jit(solution)/shard_map/pallas_call | solution.py:126
  257.4 2.4 fusion.13
  259.8 0.3 multiply_add_fusion.5
  260.1 2.7 collective-permute-start.5
  262.9 16.2 %collective-permute-done.5 = f32[40,64,128]{2,1,0:T(8,128)S(1)} collective-permute-done((f32[40,64,128]{2,1,0:T(8,128)S(1)}, f32[40,64,128]{2,1,0:T(8,128)S(1)}, u32[]{:S(2)}, u32[]{:S(2)}) %collective-permute-start.5) | collective-permute-done | bytes 1310752 | tf_op jit(solution)/shard_map/ppermute | solution.py:21
  279.1 1.9 collective-permute-start.6
  281.0 3.2 collective-permute-start.2
  284.2 13.8 %collective-permute-done.2 = f32[40]{0:T(128)S(1)} collective-permute-done((f32[40]{0:T(128)S(1)}, f32[40]{0:T(128)S(1)}, u32[]{:S(2)}, u32[]{:S(2)}) %collective-permute-start.2) | collective-permute-done | bytes 192 | tf_op jit(solution)/shard_map/ppermute | solution.py:21
  298.0 1.9 collective-permute-start.3
  300.0 2.9 collective-permute-done.3
  302.9 0.2 multiply_add_fusion.4
  303.1 3.1 collective-permute-start.7
  306.2 28.5 %collective-permute-done.7 = f32[40,64,128]{2,1,0:T(8,128)S(1)} collective-permute-done((f32[40,64,128]{2,1,0:T(8,128)S(1)}, f32[40,64,128]{2,1,0:T(8,128)S(1)}, u32[]{:S(2)}, u32[]{:S(2)}) %collective-permute-start.7) | collective-permute-done | bytes 1310752 | tf_op jit(solution)/shard_map/ppermute | solution.py:21
  334.8 1.2 multiply_add_fusion.3
  336.0 1.3 collective-permute-start.8
  337.3 0.7 reduce_window_sum.25.cum_row_ref
  338.0 2.2 collective-permute-start.4
  340.3 0.7 broadcast_in_dim_reshape.3.gain_ref
  341.0 3.9 collective-permute-done.4
  344.9 23.6 %collective-permute-done.8 = f32[40,64,128]{2,1,0:T(8,128)} collective-permute-done((f32[40,64,128]{2,1,0:T(8,128)}, f32[40,64,128]{2,1,0:T(8,128)}, u32[]{:S(2)}, u32[]{:S(2)}) %collective-permute-start.8) | collective-permute-done | bytes 1310752 | tf_op jit(solution)/shard_map/ppermute | solution.py:21
  368.5 2.1 multiply_add_fusion
  370.7 2.1 pad_maximum_fusion.1.enter_ref
  372.8 21.1 %shard_map.65 = bf16[768,2560]{1,0:T(8,128)(2,1)} custom-call(bf16[768,2816]{1,0:T(8,128)(2,1)} %multiply_convert_fusion.x_ref.b_ref.c_ref, bf16[768,2816]{1,0:T(8,128)(2,1)} %multiply_convert_fusion.x_ref.b_ref.c_ref, bf16[768,2816]{1,0:T(8,128)(2,1)} %multiply_convert_fusion.x_ref.b_ref.c_ref, f32[5,768,8]{2,1,0:T(8,128)} %bitcast.49, ...), custom_call_target="tpu_custom_call" | custom-call | tf_op jit(solution)/shard_map/pallas_call | solution.py:146
  (31 shorter events, 0.8 us)
Async XLA Ops:
  6.5 136.6 %all-gather.3.cloned.1.call-start = ((), (), s32[]{:S(2)}) async-start(), calls=%async_computation | async-start | bytes 10567680 | tf_op jit(solution)/shard_map/all_gather | solution.py:81
  7.3 149.1 %copy-start = (f32[1,40,768]{2,1,0:T(8,128)S(1)}, f32[1,40,768]{2,1,0:T(8,128)}, u32[]{:S(2)}) copy-start(f32[1,40,768]{2,1,0:T(8,128)} %param.7) | copy-start | bytes 368644
  156.3 13.5 %collective-permute-start = (bf16[1408,2560]{1,0:T(8,128)(2,1)}, bf16[1408,2560]{1,0:T(8,128)(2,1)}, u32[]{:S(2)}, u32[]{:S(2)}) collective-permute-start(bf16[1408,2560]{1,0:T(8,128)(2,1)} %reshape.72), channel_id=1, source_target_pairs={{0,1},{1,0},{2,3},{3,2},{4,5},{5,4},{6,7},{7,6},{8,9},{9,8},{10,11... | collective-permute-start | bytes 21626888 | tf_op jit(solution)/shard_map/ppermute | solution.py:82
  159.5 10.3 %copy-start.4 = (bf16[1,768,2560]{2,1,0:T(8,128)(2,1)S(1)}, bf16[1,768,2560]{2,1,0:T(8,128)(2,1)}, u32[]{:S(2)}) copy-start(bf16[1,768,2560]{2,1,0:T(8,128)(2,1)} %param.6) | copy-start | bytes 11796484
  194.5 8.4 %copy-start.1 = (bf16[4,2816]{1,0:T(4,128)(2,1)S(1)}, bf16[4,2816]{1,0:T(4,128)(2,1)}, u32[]{:S(2)}) copy-start(bf16[4,2816]{1,0:T(4,128)(2,1)} %param.9) | copy-start | bytes 67588
  200.2 27.3 %collective-permute-start.1 = (bf16[3,2816]{1,0:T(4,128)(2,1)S(1)}, bf16[3,2816]{1,0:T(4,128)(2,1)S(1)}, u32[]{:S(2)}, u32[]{:S(2)}) collective-permute-start(bf16[3,2816]{1,0:T(4,128)(2,1)S(1)} %slice.62), channel_id=1, source_target_pairs={{0,1},{1,2},{2,3},{3,4},{4,5},{5,6},{6,7},{8,9},{9,10},{10,11},{11... | collective-permute-start | bytes 50696 | tf_op jit(solution)/shard_map/ppermute | solution.py:21
  221.0 6.5 %copy-start.2 = (f32[2816]{0:T(1024)S(1)}, f32[2816]{0:T(1024)}, u32[]{:S(2)}) copy-start(f32[2816]{0:T(1024)} %param.10) | copy-start | bytes 33796
  260.1 18.9 %collective-permute-start.5 = (f32[40,64,128]{2,1,0:T(8,128)S(1)}, f32[40,64,128]{2,1,0:T(8,128)S(1)}, u32[]{:S(2)}, u32[]{:S(2)}) collective-permute-start(f32[40,64,128]{2,1,0:T(8,128)S(1)} %multiply_add_fusion.5), channel_id=1, source_target_pairs={{0,1},{1,2},{2,3},{3,4},{4,5},{5,6},{6,7},{8,9},{9,10},{10,11},{11... | collective-permute-start | bytes 3932168 | tf_op jit(solution)/shard_map/ppermute | solution.py:21
  279.1 23.8 %collective-permute-start.6 = (f32[40,64,128]{2,1,0:T(8,128)S(1)}, f32[40,64,128]{2,1,0:T(8,128)S(1)}, u32[]{:S(2)}, u32[]{:S(2)}) collective-permute-start(f32[40,64,128]{2,1,0:T(8,128)S(1)} %collective-permute-done.5), channel_id=1, source_target_pairs={{0,1},{1,2},{2,3},{3,4},{4,5},{5,6},{6,7},{8,9},{9,10},{10,11},{11... | collective-permute-start | bytes 3932168 | tf_op jit(solution)/shard_map/ppermute | solution.py:21
  281.0 17.1 %collective-permute-start.2 = (f32[40]{0:T(128)S(1)}, f32[40]{0:T(128)S(1)}, u32[]{:S(2)}, u32[]{:S(2)}) collective-permute-start(f32[40]{0:T(128)S(1)} %get-tuple-element.5), channel_id=1, source_target_pairs={{0,1},{1,2},{2,3},{3,4},{4,5},{5,6},{6,7},{8,9},{9,10},{10,11},{11... | collective-permute-start | bytes 488 | tf_op jit(solution)/shard_map/ppermute | solution.py:21
  298.0 4.8 %collective-permute-start.3 = (f32[40]{0:T(128)S(1)}, f32[40]{0:T(128)S(1)}, u32[]{:S(2)}, u32[]{:S(2)}) collective-permute-start(f32[40]{0:T(128)S(1)} %collective-permute-done.2), channel_id=1, source_target_pairs={{0,1},{1,2},{2,3},{3,4},{4,5},{5,6},{6,7},{8,9},{9,10},{10,11},{11... | collective-permute-start | bytes 488 | tf_op jit(solution)/shard_map/ppermute | solution.py:21
  302.9 37.3 %copy-start.3 = (f32[40]{0:T(128)S(1)}, f32[40]{0:T(128)}, u32[]{:S(2)}) copy-start(f32[40]{0:T(128)} %param.11) | copy-start | bytes 484
  303.1 31.6 %collective-permute-start.7 = (f32[40,64,128]{2,1,0:T(8,128)S(1)}, f32[40,64,128]{2,1,0:T(8,128)S(1)}, u32[]{:S(2)}, u32[]{:S(2)}) collective-permute-start(f32[40,64,128]{2,1,0:T(8,128)S(1)} %multiply_add_fusion.4), channel_id=1, source_target_pairs={{0,2},{1,3},{2,4},{3,5},{4,6},{5,7},{8,10},{9,11},{10,12},{11,13},... | collective-permute-start | bytes 3932168 | tf_op jit(solution)/shard_map/ppermute | solution.py:21
  336.0 32.5 %collective-permute-start.8 = (f32[40,64,128]{2,1,0:T(8,128)}, f32[40,64,128]{2,1,0:T(8,128)}, u32[]{:S(2)}, u32[]{:S(2)}) collective-permute-start(f32[40,64,128]{2,1,0:T(8,128)} %multiply_add_fusion.3), channel_id=1, source_target_pairs={{0,4},{1,5},{2,6},{3,7},{8,12},{9,13},{10,14},{11,15},{16,20},{17,... | collective-permute-start | bytes 3932168 | tf_op jit(solution)/shard_map/ppermute | solution.py:21
  338.0 6.9 %collective-permute-start.4 = (f32[40]{0:T(128)S(1)}, f32[40]{0:T(128)S(1)}, u32[]{:S(2)}, u32[]{:S(2)}) collective-permute-start(f32[40]{0:T(128)S(1)} %get-tuple-element.15), channel_id=1, source_target_pairs={{0,2},{1,3},{2,4},{3,5},{4,6},{5,7},{8,10},{9,11},{10,12},{11,13},... | collective-permute-start | bytes 488 | tf_op jit(solution)/shard_map/ppermute | solution.py:21
Sparse Core Ops, SparseCore 0:
  10.8 132.2 all-gather.2

commit v3 on v2

--- a/solution.py
+++ b/solution.py
@@ -21,15 +21,39 @@
     return lax.ppermute(array, SEQ, pairs)
 
 
+def swapped(array):
+    return lax.ppermute(array, "core", [(0, 1), (1, 0)])
+
+
 def scan_entering(total, state):
-    acc_total, acc_state = shifted(total, 1), shifted(state, 1)
-    by = 1
-    while by < lax.axis_size(SEQ):
-        got_total, got_state = shifted(acc_total, by), shifted(acc_state, by)
-        acc_state = jnp.exp(acc_total)[:, None, None] * got_state + acc_state
-        acc_total = acc_total + got_total
-        by *= 2
-    return acc_state
+    core = lax.axis_index("core")
+    half = HALF_HEADS // 2
+    halves = state.reshape(2, half, HEAD_DIM, STATE)
+    mine = lax.dynamic_index_in_dim(halves, core, 0, False)
+    sent = swapped(lax.dynamic_index_in_dim(halves, 1 - core, 0, False))
+    totals = total.reshape(2, half)
+    my_total = lax.dynamic_index_in_dim(totals, core, 0, False)
+    peer_total = swapped(lax.dynamic_index_in_dim(totals, 1 - core, 0, False))
+    first = core == 0
+    early_state = jnp.where(first, mine, sent)
+    late_state = jnp.where(first, sent, mine)
+    early_total = jnp.where(first, my_total, peer_total)
+    late_total = jnp.where(first, peer_total, my_total)
+    chip_state = jnp.exp(late_total)[:, None, None] * early_state + late_state
+    chip_total = early_total + late_total
+    chips = lax.axis_size("y")
+    held = jnp.zeros_like(chip_state)
+    gap = jnp.zeros_like(chip_total)
+    for by in range(1, chips):
+        pairs = [(i, i + by) for i in range(chips) if i + by < chips]
+        got_state = lax.ppermute(chip_state, "y", pairs)
+        got_total = lax.ppermute(chip_total, "y", pairs)
+        held = held + jnp.exp(gap)[:, None, None] * got_state
+        gap = gap + got_total
+    later = jnp.exp(early_total)[:, None, None] * held + early_state
+    mine_in = jnp.where(first, held, later)
+    other_in = swapped(jnp.where(first, later, held))
+    return jnp.where(first, jnp.concatenate([mine_in, other_in]), jnp.concatenate([other_in, mine_in]))
 
 
 def pair_lanes(columns, pair):
@@ -77,20 +101,12 @@
 
 
 def project(token_rows, input_weight):
-    rows = input_weight.shape[0]
-    mine = lax.all_gather(input_weight, ("dp", "y"), axis=0, tiled=True)
-    other = lax.ppermute(mine, "core", [(0, 1), (1, 0)])
-    dims = (((1,), (1,)), ((), ()))
-    p_mine = lax.dot_general(token_rows, mine, dims, preferred_element_type=jnp.float32).astype(jnp.bfloat16)
-    p_other = lax.dot_general(token_rows, other, dims, preferred_element_type=jnp.float32).astype(jnp.bfloat16)
-    first = lax.axis_index("core") == 0
-    p0 = jnp.where(first, p_mine, p_other)
-    p1 = jnp.where(first, p_other, p_mine)
-    length = token_rows.shape[0]
-    groups = mine.shape[0] // rows
-    return jnp.stack(
-        [p0.reshape(length, groups, rows), p1.reshape(length, groups, rows)], axis=2
-    ).reshape(length, COLS)
+    return lax.dot_general(
+        token_rows,
+        lax.all_gather(input_weight, ("dp",) + SEQ, axis=0, tiled=True),
+        (((1,), (1,)), ((), ())),
+        preferred_element_type=jnp.float32,
+    ).astype(jnp.bfloat16)
 
 
 def body(hidden, log_decay, input_weight, conv_weight, conv_bias, skip_gain):

time: 402 us -> 303 us (0.75)
  waiting for transfers between devices: 226 us -> 161 us
  local copies, waits for them, and re-layouts: 61.6 us -> 36.7 us
  starting transfers between devices: 18.9 us -> 11.9 us
  matrix products: 20.9 us -> 16.5 us
    ppermute x8 -> x1, waiting for transfers between devices: 89.1 us -> 0.01 us  [shifted(): return lax.ppermute(array, SEQ, pairs)]
    ppermute x1 -> x8, waiting for transfers between devices: 0.01 us -> 28.3 us  [the longest x2 26.4 us: scan_entering(): got_total = lax.ppermute(chip_total, 'y', pairs)]
    ppermute x8 -> x1, starting transfers between devices: 18.9 us -> 2.17 us  [shifted(): return lax.ppermute(array, SEQ, pairs)]
    another operation x10 -> x6, local copies, waits for them, and re-layouts: 16.6 us -> 2.83 us  [the longest x4 13.8 us: project(): jnp.stack([p0.reshape(length, groups, rows), p1.reshape(length, groups, r...]
    reshape x4 -> x3, local copies, waits for them, and re-layouts: 14.3 us -> 1.06 us  [the longest x2 14.2 us: project(): return jnp.stack([p0.reshape(length, groups, rows), p1.reshape(length, gr...]
    unnamed x12 -> x9, local copies, waits for them, and re-layouts: 15 us -> 27.1 us
    ppermute x1 -> x8, starting transfers between devices: 0.01 us -> 9.68 us  [the longest x3 5.02 us: scan_entering(): got_state = lax.ppermute(chip_state, 'y', pairs)]
    select_n x2 -> x0, local copies, waits for them, and re-layouts: 6.66 us -> none  [the longest x1 4.17 us: project(): p1 = jnp.where(first, p_other, p_mine)]
  transfers between devices with their start and end apart: 10 -> 10, of which waited for: 7 -> 5; matrix products, arithmetic and copies ran while one was open for 10% -> 4% of each run, Pallas kernels for 0% -> 0%
where the time goes in v3:
time: 303 us; the launch traced here: 301 us
  waiting for transfers between devices  161 us (53%)
  Pallas kernels  37 us (12%)
  local copies, waits for them, and re-layouts  36.7 us (12%)
  other arithmetic  24.1 us (8%)
  matrix products  16.5 us (5%)
  between operations  13.7 us (5%)
  starting transfers between devices  11.9 us (4%)
    all_gather x1, waiting for transfers between devices, project(): lax.all_gather(input_weight, ('dp',) + SEQ, axis=0, tiled=True)  132 us
    unnamed x9, local copies, waits for them, and re-layouts  27.1 us
    ppermute x2, waiting for transfers between devices, scan_entering(): got_total = lax.ppermute(chip_total, 'y', pairs)  26.4 us
    pallas_call x1, Pallas kernels, body(): pl.pallas_call(output_kernel, grid=(span_count, groups), in_specs=[x_spec...  21.1 us
    dot_general x1, matrix products, project(): lax.dot_general(token_rows, lax.all_gather(input_weight, ('dp',) + SEQ, a...  16.5 us
    pallas_call x1, Pallas kernels, body(): pl.pallas_call(states_kernel, grid=(span_count, groups), in_specs=[x_spec...  15.9 us
    convert_element_type x1, other arithmetic, body(): active = jax.nn.silu(filtered).astype(jnp.bfloat16)  14 us
  transfers between devices with their start and end apart: 10, of which 5 were waited for; matrix products, arithmetic and copies ran while one was open for 4% of the time, Pallas kernels for 0%

profile of v3, /device:TPU:16, one launch (start us, length us, event | category | flops | bytes accessed | tf_op | source)
XLA Modules:
  0.0 301.2 jit_solution(13840601561750747070)
XLA Ops:
  6.5 0.7 all-gather.3.cloned.1.call-update
  7.3 1.0 reshape.147
  8.2 1.8 reduce-window.6
  10.0 0.1 slice.80
  10.1 0.1 copy.27
  10.3 0.1 copy_bitcast_fusion
  10.4 0.2 slice_reduce_fusion.1
  10.6 1.6 negate_bitcast_fusion
  12.2 0.1 broadcast_add_fusion
  12.3 132.4 %all-gather.3.cloned.1.call-done = bf16[256,11,2560]{2,1,0:T(8,128)(2,1)} async-done(((bf16[1,11,2560]{2,1,0:T(8,128)(2,1)}), bf16[256,11,2560]{2,1,0:T(8,128)(2,1)}) %all-gather.3.cloned.1.call-update) | async-done | bytes 14417936 | tf_op jit(solution)/shard_map/all_gather | solution.py:106
  144.7 25.0 %reshape.155 = bf16[2816,2560]{1,0:T(8,128)(2,1)} reshape(bf16[256,11,2560]{2,1,0:T(8,128)(2,1)} %all-gather.3.cloned.1.call-done) | data formatting | bytes 28835840
  169.8 16.5 %convolution_convert_fusion = bf16[768,2816]{1,0:T(8,128)(2,1)S(1)} fusion(bf16[2816,2560]{1,0:T(8,128)(2,1)} %reshape.155, bf16[1,768,2560]{2,1,0:T(8,128)(2,1)} %param.6), kind=kOutput, calls=%fused_computation.3 | convolution fusion | flops 11075125248 | bytes 22675456 | tf_op jit(solution)/shard_map/dot_general | solution.py:104
  186.3 2.0 copy-done
  188.3 2.2 collective-permute-start
  190.5 0.1 convert_reduce_fusion.3
  190.7 0.1 reduce_window_sum.24
  190.8 1.9 copy.30
  192.7 1.8 copy.33
  194.5 0.1 mul.176
  194.6 0.1 exp.59
  194.7 0.1 exp.57
  194.8 14.0 %multiply_convert_fusion.x_ref.b_ref.c_ref = bf16[768,2816]{1,0:T(8,128)(2,1)} fusion(bf16[768,2816]{1,0:T(8,128)(2,1)} %copy-done, bf16[3,2816]{1,0:T(4,128)(2,1)S(1)} %collective-permute-done, f32[2816]{0:T(1024)S(1)} %get-tuple-element.9, f32[2816]{0:T(1024)S(1)} %get-tuple-element.10, f32[2816]{0:T(1024)S(1)} %get-tuple-element.8, ...), kind=kLoop, calls=%fused_computation | loop fusion | flops 56229888 | bytes 8723968 | tf_op jit(solution)/shard_map/convert_element_type | solution.py:127
  208.8 15.9 %shard_map.64 = f32[3,2560,128]{2,1,0:T(8,128)} custom-call(bf16[768,2816]{1,0:T(8,128)(2,1)} %multiply_convert_fusion.x_ref.b_ref.c_ref, bf16[768,2816]{1,0:T(8,128)(2,1)} %multiply_convert_fusion.x_ref.b_ref.c_ref, f32[5,768,8]{2,1,0:T(8,128)} %bitcast.55, f32[5,768,8]{2,1,0:T(8,128)} %bitcast.58), custom_call_target="tpu_custom_call" | custom-call | tf_op jit(solution)/shard_map/pallas_call | solution.py:142
  224.6 2.4 fusion.12
  227.0 0.3 multiply_add_fusion.2
  227.4 1.1 collective-permute-start.2
  228.5 0.1 reshape.149
  228.7 1.6 collective-permute-done.1
  230.3 0.1 fusion.3
  230.5 0.7 collective-permute-start.7
  231.2 3.0 %collective-permute-start.3 = (f32[20,64,128]{2,1,0:T(8,128)S(1)}, f32[20,64,128]{2,1,0:T(8,128)S(1)}, u32[]{:S(2)}, u32[]{:S(2)}) collective-permute-start(f32[20,64,128]{2,1,0:T(8,128)S(1)} %fusion.3), channel_id=1, source_target_pairs={{0,2},{2,4},{4,6},{1,3},{3,5},{5,7},{8,10},{10,12},{12,14},{9,11},... | collective-permute-start | bytes 1966088 | tf_op jit(solution)/shard_map/ppermute | solution.py:49
  234.2 1.3 collective-permute-start.5
  235.5 1.9 collective-permute-start.4
  237.4 1.3 collective-permute-start.6
  238.7 11.4 %collective-permute-done.4 = f32[20]{0:T(128)S(1)} collective-permute-done((f32[20]{0:T(128)S(1)}, f32[20]{0:T(128)S(1)}, u32[]{:S(2)}, u32[]{:S(2)}) %collective-permute-start.4) | collective-permute-done | bytes 112 | tf_op jit(solution)/shard_map/ppermute | solution.py:50
  250.2 15.0 %collective-permute-done.6 = f32[20]{0:T(128)S(1)} collective-permute-done((f32[20]{0:T(128)S(1)}, f32[20]{0:T(128)S(1)}, u32[]{:S(2)}, u32[]{:S(2)}) %collective-permute-start.6) | collective-permute-done | bytes 112 | tf_op jit(solution)/shard_map/ppermute | solution.py:50
  265.2 0.3 select_bitcast_fusion
  265.5 0.2 fusion.4
  265.6 0.3 collective-permute-start.8
  265.9 0.8 reduce_window_sum.25.cum_row_ref
  266.8 0.1 mul.192
  266.9 0.1 mul.188
  267.1 0.7 broadcast_in_dim_reshape.3.gain_ref
  267.7 0.3 collective-permute-done.8
  268.0 0.1 maximum_select_fusion
  268.1 2.8 multiply_add_fusion
  271.0 2.3 pad_maximum_fusion.1.enter_ref
  273.3 21.1 %shard_map.65 = bf16[768,2560]{1,0:T(8,128)(2,1)} custom-call(bf16[768,2816]{1,0:T(8,128)(2,1)} %multiply_convert_fusion.x_ref.b_ref.c_ref, bf16[768,2816]{1,0:T(8,128)(2,1)} %multiply_convert_fusion.x_ref.b_ref.c_ref, bf16[768,2816]{1,0:T(8,128)(2,1)} %multiply_convert_fusion.x_ref.b_ref.c_ref, f32[5,768,8]{2,1,0:T(8,128)} %bitcast.56, ...), custom_call_target="tpu_custom_call" | custom-call | tf_op jit(solution)/shard_map/pallas_call | solution.py:162
  (30 shorter events, 0.5 us)
Async XLA Ops:
  6.5 138.2 %all-gather.3.cloned.1.call-start = ((), (), s32[]{:S(2)}) async-start(), calls=%async_computation | async-start | bytes 21053440 | tf_op jit(solution)/shard_map/all_gather | solution.py:106
  169.8 20.7 %copy-start.1 = (bf16[4,2816]{1,0:T(4,128)(2,1)S(1)}, bf16[4,2816]{1,0:T(4,128)(2,1)}, u32[]{:S(2)}) copy-start(bf16[4,2816]{1,0:T(4,128)(2,1)} %param.9) | copy-start | bytes 67588
  186.3 2.0 copy-start
  188.3 6.5 %copy-start.2 = (f32[2816]{0:T(1024)S(1)}, f32[2816]{0:T(1024)}, u32[]{:S(2)}) copy-start(f32[2816]{0:T(1024)} %param.10) | copy-start | bytes 33796
  188.3 6.5 %collective-permute-start = (bf16[3,2816]{1,0:T(4,128)(2,1)S(1)}, bf16[3,2816]{1,0:T(4,128)(2,1)S(1)}, u32[]{:S(2)}, u32[]{:S(2)}) collective-permute-start(bf16[3,2816]{1,0:T(4,128)(2,1)S(1)} %slice.75), channel_id=1, source_target_pairs={{0,1},{1,2},{2,3},{3,4},{4,5},{5,6},{6,7},{8,9},{9,10},{10,11},{11... | collective-permute-start | bytes 50696 | tf_op jit(solution)/shard_map/ppermute | solution.py:21
  227.4 2.9 collective-permute-start.2
  228.6 1.6 collective-permute-start.1
  230.5 36.5 %copy-start.3 = (f32[40]{0:T(128)S(1)}, f32[40]{0:T(128)}, u32[]{:S(2)}) copy-start(f32[40]{0:T(128)} %param.11) | copy-start | bytes 484
  230.5 34.7 %collective-permute-start.7 = (f32[20,64,128]{2,1,0:T(8,128)S(1)}, f32[20,64,128]{2,1,0:T(8,128)S(1)}, u32[]{:S(2)}, u32[]{:S(2)}) collective-permute-start(f32[20,64,128]{2,1,0:T(8,128)S(1)} %fusion.3), channel_id=1, source_target_pairs={{0,6},{1,7},{8,14},{9,15},{16,22},{17,23},{24,30},{25,31},{32,38},... | collective-permute-start | bytes 1966088 | tf_op jit(solution)/shard_map/ppermute | solution.py:49
  231.2 34.0 %collective-permute-start.3 = (f32[20,64,128]{2,1,0:T(8,128)S(1)}, f32[20,64,128]{2,1,0:T(8,128)S(1)}, u32[]{:S(2)}, u32[]{:S(2)}) collective-permute-start(f32[20,64,128]{2,1,0:T(8,128)S(1)} %fusion.3), channel_id=1, source_target_pairs={{0,2},{2,4},{4,6},{1,3},{3,5},{5,7},{8,10},{10,12},{12,14},{9,11},... | collective-permute-start | bytes 1966088 | tf_op jit(solution)/shard_map/ppermute | solution.py:49
  234.2 31.0 %collective-permute-start.5 = (f32[20,64,128]{2,1,0:T(8,128)S(1)}, f32[20,64,128]{2,1,0:T(8,128)S(1)}, u32[]{:S(2)}, u32[]{:S(2)}) collective-permute-start(f32[20,64,128]{2,1,0:T(8,128)S(1)} %fusion.3), channel_id=1, source_target_pairs={{0,4},{2,6},{1,5},{3,7},{8,12},{10,14},{9,13},{11,15},{16,20},{18,... | collective-permute-start | bytes 1966088 | tf_op jit(solution)/shard_map/ppermute | solution.py:49
  235.5 14.7 %collective-permute-start.4 = (f32[20]{0:T(128)S(1)}, f32[20]{0:T(128)S(1)}, u32[]{:S(2)}, u32[]{:S(2)}) collective-permute-start(f32[20]{0:T(128)S(1)} %get-tuple-element.20), channel_id=1, source_target_pairs={{0,2},{2,4},{4,6},{1,3},{3,5},{5,7},{8,10},{10,12},{12,14},{9,11},... | collective-permute-start | bytes 248 | tf_op jit(solution)/shard_map/ppermute | solution.py:50
  237.4 27.7 %collective-permute-start.6 = (f32[20]{0:T(128)S(1)}, f32[20]{0:T(128)S(1)}, u32[]{:S(2)}, u32[]{:S(2)}) collective-permute-start(f32[20]{0:T(128)S(1)} %get-tuple-element.20), channel_id=1, source_target_pairs={{0,4},{2,6},{1,5},{3,7},{8,12},{10,14},{9,13},{11,15},{16,20},{18,... | collective-permute-start | bytes 248 | tf_op jit(solution)/shard_map/ppermute | solution.py:50
  265.6 2.4 collective-permute-start.8
Sparse Core Ops, SparseCore 0:
  10.9 133.7 all-gather.2

commit v4 on v3

--- a/solution.py
+++ b/solution.py
@@ -25,7 +25,7 @@
     return lax.ppermute(array, "core", [(0, 1), (1, 0)])
 
 
-def scan_entering(total, state):
+def scan_entering(total, state, side, side_inputs):
     core = lax.axis_index("core")
     half = HALF_HEADS // 2
     halves = state.reshape(2, half, HEAD_DIM, STATE)
@@ -42,18 +42,22 @@
     chip_state = jnp.exp(late_total)[:, None, None] * early_state + late_state
     chip_total = early_total + late_total
     chips = lax.axis_size("y")
+    chip_state, chip_total, side_inputs = lax.optimization_barrier((chip_state, chip_total, side_inputs))
+    got = []
+    for by in range(1, chips):
+        pairs = [(i, i + by) for i in range(chips) if i + by < chips]
+        got.append((lax.ppermute(chip_state, "y", pairs), lax.ppermute(chip_total, "y", pairs)))
+    side_out = side(*side_inputs)
+    got, side_out = lax.optimization_barrier((got, side_out))
     held = jnp.zeros_like(chip_state)
     gap = jnp.zeros_like(chip_total)
-    for by in range(1, chips):
-        pairs = [(i, i + by) for i in range(chips) if i + by < chips]
-        got_state = lax.ppermute(chip_state, "y", pairs)
-        got_total = lax.ppermute(chip_total, "y", pairs)
+    for got_state, got_total in got:
         held = held + jnp.exp(gap)[:, None, None] * got_state
         gap = gap + got_total
     later = jnp.exp(early_total)[:, None, None] * held + early_state
     mine_in = jnp.where(first, held, later)
     other_in = swapped(jnp.where(first, later, held))
-    return jnp.where(first, jnp.concatenate([mine_in, other_in]), jnp.concatenate([other_in, mine_in]))
+    return jnp.where(first, jnp.concatenate([mine_in, other_in]), jnp.concatenate([other_in, mine_in])), side_out
 
 
 def pair_lanes(columns, pair):
@@ -73,13 +77,10 @@
         )
 
 
-def output_kernel(x_ref, b_ref, c_ref, cum_ref, cum_row_ref, step_row_ref, enter_ref, gain_ref, out_ref):
-    c_span = c_ref[...]
-    scores = lax.dot_general(c_span, b_ref[...], (((1,), (1,)), ((), ())), preferred_element_type=jnp.float32)
+def intra_kernel(x_ref, b_ref, c_ref, cum_ref, cum_row_ref, step_row_ref, gain_ref, part_ref):
+    scores = lax.dot_general(c_ref[...], b_ref[...], (((1,), (1,)), ((), ())), preferred_element_type=jnp.float32)
     causal = lax.broadcasted_iota(jnp.int32, (SPAN, SPAN), 0) >= lax.broadcasted_iota(jnp.int32, (SPAN, SPAN), 1)
     cum = cum_ref[0]
-    rise = jnp.exp(cum)
-    c32 = c_span.astype(jnp.float32)
     lane = lax.broadcasted_iota(jnp.int32, (SPAN, 2 * HEAD_DIM), 1)
     for pair in range(GROUP // 2):
         lanes = slice(2 * HEAD_DIM * pair, 2 * HEAD_DIM * (pair + 1))
@@ -92,21 +93,32 @@
             mixing = (scores * decay * step_row_ref[head : head + 1, :]).astype(jnp.bfloat16)
             parts.append(jnp.dot(mixing, x_pair, preferred_element_type=jnp.float32))
         intra = jnp.where(lane < HEAD_DIM, parts[0], parts[1])
+        part_ref[:, lanes] = intra + gain_ref[:, lanes] * x_pair.astype(jnp.float32)
+
+
+def readout_kernel(part_ref, c_ref, cum_ref, enter_ref, out_ref):
+    rise = jnp.exp(cum_ref[0])
+    c32 = c_ref[...].astype(jnp.float32)
+    for pair in range(GROUP // 2):
+        lanes = slice(2 * HEAD_DIM * pair, 2 * HEAD_DIM * (pair + 1))
         readout = lax.dot_general(
             c32, enter_ref[0, lanes, :], (((1,), (1,)), ((), ())),
             precision=lax.Precision.HIGHEST, preferred_element_type=jnp.float32,
         )
-        total = intra + pair_lanes(rise, pair) * readout + gain_ref[:, lanes] * x_pair.astype(jnp.float32)
-        out_ref[:, lanes] = total.astype(jnp.bfloat16)
-
-
-def project(token_rows, input_weight):
-    return lax.dot_general(
-        token_rows,
-        lax.all_gather(input_weight, ("dp",) + SEQ, axis=0, tiled=True),
-        (((1,), (1,)), ((), ())),
-        preferred_element_type=jnp.float32,
-    ).astype(jnp.bfloat16)
+        out_ref[:, lanes] = (part_ref[:, lanes] + pair_lanes(rise, pair) * readout).astype(jnp.bfloat16)
+
+
+def project(token_rows, input_weight, chunks=4):
+    width = token_rows.shape[1] // chunks
+    total = None
+    for chunk in range(chunks):
+        cols = slice(chunk * width, (chunk + 1) * width)
+        weight = lax.all_gather(input_weight[:, cols], ("dp",) + SEQ, axis=0, tiled=True)
+        piece = lax.dot_general(
+            token_rows[:, cols], weight, (((1,), (1,)), ((), ())), preferred_element_type=jnp.float32
+        )
+        total = piece if total is None else total + piece
+    return total.astype(jnp.bfloat16)
 
 
 def body(hidden, log_decay, input_weight, conv_weight, conv_bias, skip_gain):
@@ -139,36 +151,57 @@
     col_spec = pl.BlockSpec((1, SPAN, GROUP), lambda c, g: (g, c, 0))
     row_spec = pl.BlockSpec((GROUP, SPAN), lambda c, g: (g, c))
     state_spec = pl.BlockSpec((1, GROUP * HEAD_DIM, STATE), lambda c, g: (c, g, 0))
+    gain = jnp.repeat(skip_gain, HEAD_DIM)[None, :]
+    gain_spec = pl.BlockSpec((1, GROUP * HEAD_DIM), lambda c, g: (0, g))
     states = pl.pallas_call(
         states_kernel,
         grid=(span_count, groups),
         in_specs=[x_spec, b_spec, col_spec, col_spec],
         out_specs=state_spec,
         out_shape=jax.ShapeDtypeStruct((span_count, INNER, STATE), jnp.float32),
+        cost_estimate=pl.CostEstimate(
+            flops=2 * length * INNER * STATE, transcendentals=length * HALF_HEADS,
+            bytes_accessed=2 * length * (INNER + STATE) + 4 * span_count * INNER * STATE,
+        ),
     )(active, active, cum_grouped, step_grouped)
     states = states.reshape(span_count, HALF_HEADS, HEAD_DIM, STATE)
 
     local = jnp.zeros((HALF_HEADS, HEAD_DIM, STATE), jnp.float32)
     for span in range(span_count):
         local = jnp.exp(totals[span])[:, None, None] * local + states[span]
-    held = scan_entering(jnp.sum(totals, axis=0), local)
+    def intra(active, cum_grouped, cum_row, step_row, gain):
+        return pl.pallas_call(
+            intra_kernel,
+            grid=(span_count, groups),
+            in_specs=[x_spec, b_spec, c_spec, col_spec, row_spec, row_spec, gain_spec],
+            out_specs=x_spec,
+            out_shape=jax.ShapeDtypeStruct((length, INNER), jnp.float32),
+            cost_estimate=pl.CostEstimate(
+                flops=2 * length * SPAN * (groups * STATE + 2 * INNER), transcendentals=length * SPAN * HALF_HEADS,
+                bytes_accessed=2 * length * (INNER + 2 * STATE) + 4 * length * INNER,
+            ),
+        )(active, active, active, cum_grouped, cum_row, step_row, gain)
+
+    held, part = scan_entering(
+        jnp.sum(totals, axis=0), local, intra, (active, cum_grouped, cum_row, step_row, gain)
+    )
     entering = []
     for span in range(span_count):
         entering.append(held)
         held = jnp.exp(totals[span])[:, None, None] * held + states[span]
     entering = jnp.stack(entering).reshape(span_count, INNER, STATE)
 
-    gain = jnp.repeat(skip_gain, HEAD_DIM)[None, :]
     out = pl.pallas_call(
-        output_kernel,
+        readout_kernel,
         grid=(span_count, groups),
-        in_specs=[
-            x_spec, b_spec, c_spec, col_spec, row_spec, row_spec, state_spec,
-            pl.BlockSpec((1, GROUP * HEAD_DIM), lambda c, g: (0, g)),
-        ],
+        in_specs=[x_spec, c_spec, col_spec, state_spec],
         out_specs=x_spec,
         out_shape=jax.ShapeDtypeStruct((length, INNER), jnp.bfloat16),
-    )(active, active, active, cum_grouped, cum_row, step_row, entering, gain)
+        cost_estimate=pl.CostEstimate(
+            flops=12 * length * STATE * INNER, transcendentals=length * HALF_HEADS,
+            bytes_accessed=6 * length * INNER + 4 * span_count * INNER * STATE,
+        ),
+    )(part, active, cum_grouped, entering)
     return out[None]
 
 

time: 303 us -> 614 us (2.03)
  waiting for transfers between devices: 161 us -> 433 us
  matrix products: 16.5 us -> 34.4 us
  Pallas kernels: 37 us -> 48.2 us
    all_gather x1 -> x4, waiting for transfers between devices: 132 us -> 421 us  [project(): lax.all_gather(input_weight[:, cols], ('dp',) + SEQ, axis=0, tiled=True)]
    ppermute x5, waiting for transfers between devices: 26.4 us -> 8.47 us  [the longest x2 8.46 us: scan_entering(): lax.ppermute(chip_total, 'y', pairs)]
    dot_general x1 -> x4, matrix products: 16.5 us -> 34.4 us  [project(): lax.dot_general(token_rows[:, cols], weight, (((1,), (1,)), ((), ())), pr...]
    pallas_call x1 -> x2, Pallas kernels: 21.1 us -> 32.3 us  [the longest x1 16.5 us: intra(): pl.pallas_call(intra_kernel, grid=(span_count, groups), in_specs=[x_spec,...]
    unnamed x9 -> x21, local copies, waits for them, and re-layouts: 27.1 us -> 33 us
  transfers between devices with their start and end apart: 10 -> 13, of which waited for: 5 -> 7; matrix products, arithmetic and copies ran while one was open for 4% -> 9% of each run, Pallas kernels for 0% -> 3%
where the time goes in v4:
time: 614 us; the launch traced here: 610 us
  waiting for transfers between devices  433 us (71%)
  Pallas kernels  48.2 us (8%)
  local copies, waits for them, and re-layouts  42.6 us (7%)
  matrix products  34.4 us (6%)
  other arithmetic  26 us (4%)
  between operations  13.4 us (2%)
  starting transfers between devices  12.3 us (2%)
    all_gather x4, waiting for transfers between devices, project(): lax.all_gather(input_weight[:, cols], ('dp',) + SEQ, axis=0, tiled=True)  421 us
    dot_general x4, matrix products, project(): lax.dot_general(token_rows[:, cols], weight, (((1,), (1,)), ((), ())), pr...  34.4 us
    unnamed x21, local copies, waits for them, and re-layouts  33 us
    pallas_call x1, Pallas kernels, intra(): pl.pallas_call(intra_kernel, grid=(span_count, groups), in_specs=[x_spec,...  16.5 us
    pallas_call x1, Pallas kernels, body(): pl.pallas_call(states_kernel, grid=(span_count, groups), in_specs=[x_spec...  15.9 us
    pallas_call x1, Pallas kernels, body(): pl.pallas_call(readout_kernel, grid=(span_count, groups), in_specs=[x_spe...  15.8 us
    convert_element_type x1, other arithmetic, body(): active = jax.nn.silu(filtered).astype(jnp.bfloat16)  14 us
  transfers between devices with their start and end apart: 13, of which 7 were waited for; matrix products, arithmetic and copies ran while one was open for 9% of the time, Pallas kernels for 3%

profile of v4, /device:TPU:16, one launch (start us, length us, event | category | flops | bytes accessed | tf_op | source)
XLA Modules:
  0.0 610.4 jit_solution(1404252388052086080)
XLA Ops:
  6.5 1.4 slice_bitcast_fusion
  8.0 0.7 all-gather.11.cloned.1.call-update
  8.8 0.7 all-gather.9.cloned.1.call-update
  9.5 0.5 all-gather.15.cloned.1.call-update
  10.0 1.0 reshape.147
  11.0 1.8 reduce-window.6
  13.2 0.2 slice_reduce_fusion.1
  13.4 1.6 negate_bitcast_fusion
  15.1 114.3 %all-gather.13.cloned.1.call-done = bf16[256,11,640]{2,1,0:T(8,128)(2,1)} async-done(((bf16[1,11,640]{2,1,0:T(8,128)(2,1)}), bf16[256,11,640]{2,1,0:T(8,128)(2,1)}) %all-gather.13.cloned.1.call-update) | async-done | bytes 3604496 | tf_op jit(solution)/shard_map/all_gather | solution.py:116
  129.4 7.2 %reshape.159 = bf16[2816,640]{1,0:T(8,128)(2,1)} reshape(bf16[256,11,640]{2,1,0:T(8,128)(2,1)} %all-gather.13.cloned.1.call-done) | data formatting | bytes 7208960
  136.6 109.3 %all-gather.11.cloned.1.call-done = bf16[256,11,640]{2,1,0:T(8,128)(2,1)} async-done(((bf16[1,11,640]{2,1,0:T(8,128)(2,1)}), bf16[256,11,640]{2,1,0:T(8,128)(2,1)}) %all-gather.11.cloned.1.call-update) | async-done | bytes 3604496 | tf_op jit(solution)/shard_map/all_gather | solution.py:116
  245.9 7.2 %reshape.157 = bf16[2816,640]{1,0:T(8,128)(2,1)} reshape(bf16[256,11,640]{2,1,0:T(8,128)(2,1)} %all-gather.11.cloned.1.call-done) | data formatting | bytes 7208960
  253.1 109.3 %all-gather.9.cloned.1.call-done = bf16[256,11,640]{2,1,0:T(8,128)(2,1)} async-done(((bf16[1,11,640]{2,1,0:T(8,128)(2,1)}), bf16[256,11,640]{2,1,0:T(8,128)(2,1)}) %all-gather.9.cloned.1.call-update) | async-done | bytes 3604496 | tf_op jit(solution)/shard_map/all_gather | solution.py:116
  362.5 7.2 %reshape.155 = bf16[2816,640]{1,0:T(8,128)(2,1)} reshape(bf16[256,11,640]{2,1,0:T(8,128)(2,1)} %all-gather.9.cloned.1.call-done) | data formatting | bytes 7208960
  369.7 9.3 %fusion.3 = f32[768,2816]{1,0:T(8,128)} fusion(bf16[2816,640]{1,0:T(8,128)(2,1)} %reshape.159, bf16[768,2560]{1,0:T(8,128)(2,1)} %bitcast.72), kind=kOutput, calls=%fused_computation.13 | convolution fusion | flops 2768240640 | bytes 13238272 | tf_op jit(solution)/shard_map/dot_general | solution.py:117
  379.0 5.8 fusion.5
  384.8 5.8 fusion.7
  390.6 88.2 %all-gather.15.cloned.1.call-done = bf16[256,11,640]{2,1,0:T(8,128)(2,1)} async-done(((bf16[1,11,640]{2,1,0:T(8,128)(2,1)}), bf16[256,11,640]{2,1,0:T(8,128)(2,1)}) %all-gather.15.cloned.1.call-update) | async-done | bytes 3604496 | tf_op jit(solution)/shard_map/all_gather | solution.py:116
  478.8 7.2 %reshape.161 = bf16[2816,640]{1,0:T(8,128)(2,1)} reshape(bf16[256,11,640]{2,1,0:T(8,128)(2,1)} %all-gather.15.cloned.1.call-done) | data formatting | bytes 7208960
  486.0 13.4 %add_convert_fusion = bf16[768,2816]{1,0:T(8,128)(2,1)S(1)} fusion(f32[768,2816]{1,0:T(8,128)} %fusion.3, f32[768,2816]{1,0:T(8,128)} %fusion.7, f32[768,2816]{1,0:T(8,128)} %fusion.5, bf16[2816,640]{1,0:T(8,128)(2,1)} %reshape.161, bf16[768,2560]{1,0:T(8,128)(2,1)} %bitcast.73), kind=kOutput, calls=%fused_computation.1 | convolution fusion | flops 2776891392 | bytes 34865152 | tf_op jit(solution)/shard_map/dot_general | solution.py:117
  499.5 2.0 copy-done
  501.5 2.4 collective-permute-start.1
  503.9 0.1 convert_reduce_fusion.3
  504.2 1.9 copy.31
  506.0 1.9 copy.32
  508.1 14.0 %multiply_convert_fusion.x_ref.b_ref.c_ref = bf16[768,2816]{1,0:T(8,128)(2,1)} fusion(bf16[768,2816]{1,0:T(8,128)(2,1)} %copy-done, bf16[3,2816]{1,0:T(4,128)(2,1)S(1)} %collective-permute-done.1, f32[2816]{0:T(1024)S(1)} %get-tuple-element.35, f32[2816]{0:T(1024)S(1)} %get-tuple-element.36, f32[2816]{0:T(1024)S(1)} %get-tuple-element.34, ...), kind=kLoop, calls=%fused_computation | loop fusion | flops 56229888 | bytes 8723968 | tf_op jit(solution)/shard_map/convert_element_type | solution.py:139
  522.1 15.9 %shard_map.64 = f32[3,2560,128]{2,1,0:T(8,128)} custom-call(bf16[768,2816]{1,0:T(8,128)(2,1)} %multiply_convert_fusion.x_ref.b_ref.c_ref, bf16[768,2816]{1,0:T(8,128)(2,1)} %multiply_convert_fusion.x_ref.b_ref.c_ref, f32[5,768,8]{2,1,0:T(8,128)} %bitcast.63, f32[5,768,8]{2,1,0:T(8,128)} %bitcast.67), custom_call_target="tpu_custom_call" | custom-call | flops 503316480 | bytes 8060928 | tf_op jit(solution)/shard_map/pallas_call | solution.py:156
  538.0 2.4 fusion.18
  540.3 0.3 multiply_add_fusion.2
  540.7 1.1 collective-permute-start.2
  542.0 0.7 reduce_window_sum.26.cum_row_ref
  542.8 0.7 broadcast_in_dim_reshape.3.gain_ref
  543.6 1.0 fusion.9
  544.6 2.5 collective-permute-start.3
  547.1 1.3 collective-permute-start.5
  548.4 1.6 collective-permute-start.7
  550.0 1.9 collective-permute-start.4
  551.9 1.3 collective-permute-start.6
  553.2 16.5 %shard_map.65.part_ref = f32[768,2560]{1,0:T(8,128)} custom-call(bf16[768,2816]{1,0:T(8,128)(2,1)} %multiply_convert_fusion.x_ref.b_ref.c_ref, bf16[768,2816]{1,0:T(8,128)(2,1)} %multiply_convert_fusion.x_ref.b_ref.c_ref, bf16[768,2816]{1,0:T(8,128)(2,1)} %multiply_convert_fusion.x_ref.b_ref.c_ref, f32[5,768,8]{2,1,0:T(8,128)} %bitcast.64, ...), custom_call_target="tpu_custom_call" | custom-call | flops 2264924160 | bytes 12189696 | tf_op jit(solution)/shard_map/pallas_call | solution.py:173
  569.7 8.5 %collective-permute-done.6 = f32[20]{0:T(128)S(1)} collective-permute-done((f32[20]{0:T(128)S(1)}, f32[20]{0:T(128)S(1)}, u32[]{:S(2)}, u32[]{:S(2)}) %collective-permute-start.6) | collective-permute-done | bytes 112 | tf_op jit(solution)/shard_map/ppermute | solution.py:49
  578.2 0.8 copy-done.3
  579.0 1.6 select_bitcast_fusion
  580.6 0.2 fusion.10
  581.2 1.8 collective-permute-done.8
  582.9 0.1 maximum_select_fusion
  583.1 2.8 multiply_add_fusion
  585.9 2.1 pad_maximum_fusion.1.enter_ref
  588.0 15.8 %shard_map.66 = bf16[768,2560]{1,0:T(8,128)(2,1)} custom-call(f32[768,2560]{1,0:T(8,128)} %shard_map.65.part_ref, bf16[768,2816]{1,0:T(8,128)(2,1)} %multiply_convert_fusion.x_ref.b_ref.c_ref, f32[5,768,8]{2,1,0:T(8,128)} %bitcast.65, f32[3,2560,128]{2,1,0:T(8,128)} %pad_maximum_fusion.1.enter_ref), custom_call_target="tpu_custom_call" | custom-call | flops 3019898880 | bytes 15728640 | tf_op jit(solution)/shard_map/pallas_call | solution.py:194
  (55 shorter events, 1.8 us)
Async XLA Ops:
  6.5 122.9 %all-gather.13.cloned.1.call-start = ((), (), s32[]{:S(2)}) async-start(), calls=%async_computation.2 | async-start | bytes 5263360 | tf_op jit(solution)/shard_map/all_gather | solution.py:116
  8.0 237.9 %all-gather.11.cloned.1.call-start = ((), (), s32[]{:S(2)}) async-start(), calls=%async_computation.1 | async-start | bytes 5263360 | tf_op jit(solution)/shard_map/all_gather | solution.py:116
  8.7 353.7 %all-gather.9.cloned.1.call-start = ((), (), s32[]{:S(2)}) async-start(), calls=%async_computation | async-start | bytes 5263360 | tf_op jit(solution)/shard_map/all_gather | solution.py:116
  9.5 469.4 %all-gather.15.cloned.1.call-start = ((), (), s32[]{:S(2)}) async-start(), calls=%async_computation.3 | async-start | bytes 5263360 | tf_op jit(solution)/shard_map/all_gather | solution.py:116
  369.7 9.4 %copy-start.1 = (bf16[2816,640]{1,0:T(8,128)(2,1)S(1)}, bf16[2816,640]{1,0:T(8,128)(2,1)}, u32[]{:S(2)}) copy-start(bf16[2816,640]{1,0:T(8,128)(2,1)} %reshape.157) | copy-start | bytes 10813444
  369.7 9.4 %copy-start.4 = (bf16[1,768,2560]{2,1,0:T(8,128)(2,1)S(1)}, bf16[1,768,2560]{2,1,0:T(8,128)(2,1)}, u32[]{:S(2)}) copy-start(bf16[1,768,2560]{2,1,0:T(8,128)(2,1)} %param.6) | copy-start | bytes 11796484
  379.0 5.8 copy-start.2
  486.0 17.8 %copy-start.5 = (bf16[4,2816]{1,0:T(4,128)(2,1)S(1)}, bf16[4,2816]{1,0:T(4,128)(2,1)}, u32[]{:S(2)}) copy-start(bf16[4,2816]{1,0:T(4,128)(2,1)} %param.9) | copy-start | bytes 67588
  499.4 2.0 copy-start
  501.4 6.7 %copy-start.6 = (f32[2816]{0:T(1024)S(1)}, f32[2816]{0:T(1024)}, u32[]{:S(2)}) copy-start(f32[2816]{0:T(1024)} %param.10) | copy-start | bytes 33796
  501.5 6.7 %collective-permute-start.1 = (bf16[3,2816]{1,0:T(4,128)(2,1)S(1)}, bf16[3,2816]{1,0:T(4,128)(2,1)S(1)}, u32[]{:S(2)}, u32[]{:S(2)}) collective-permute-start(bf16[3,2816]{1,0:T(4,128)(2,1)S(1)} %slice.114), channel_id=1, source_target_pairs={{0,1},{1,2},{2,3},{3,4},{4,5},{5,6},{6,7},{8,9},{9,10},{10,11},{11... | collective-permute-start | bytes 50696 | tf_op jit(solution)/shard_map/ppermute | solution.py:21
  540.3 2.4 copy-start.7
  540.7 2.9 collective-permute-start.2
  542.0 1.6 collective-permute-start
  544.6 33.6 %collective-permute-start.3 = (f32[20,64,128]{2,1,0:T(8,128)}, f32[20,64,128]{2,1,0:T(8,128)S(1)}, u32[]{:S(2)}, u32[]{:S(2)}) collective-permute-start(f32[20,64,128]{2,1,0:T(8,128)} %fusion.9), channel_id=1, source_target_pairs={{0,2},{2,4},{4,6},{1,3},{3,5},{5,7},{8,10},{10,12},{12,14},{9,11},... | collective-permute-start | bytes 1966088 | tf_op jit(solution)/shard_map/ppermute | solution.py:49
  547.1 31.1 %collective-permute-start.5 = (f32[20,64,128]{2,1,0:T(8,128)}, f32[20,64,128]{2,1,0:T(8,128)S(1)}, u32[]{:S(2)}, u32[]{:S(2)}) collective-permute-start(f32[20,64,128]{2,1,0:T(8,128)} %fusion.9), channel_id=1, source_target_pairs={{0,4},{2,6},{1,5},{3,7},{8,12},{10,14},{9,13},{11,15},{16,20},{18,... | collective-permute-start | bytes 1966088 | tf_op jit(solution)/shard_map/ppermute | solution.py:49
  548.4 29.8 %collective-permute-start.7 = (f32[20,64,128]{2,1,0:T(8,128)}, f32[20,64,128]{2,1,0:T(8,128)}, u32[]{:S(2)}, u32[]{:S(2)}) collective-permute-start(f32[20,64,128]{2,1,0:T(8,128)} %fusion.9), channel_id=1, source_target_pairs={{0,6},{1,7},{8,14},{9,15},{16,22},{17,23},{24,30},{25,31},{32,38},... | collective-permute-start | bytes 1966088 | tf_op jit(solution)/shard_map/ppermute | solution.py:49
  550.0 19.7 %collective-permute-start.4 = (f32[20]{0:T(128)S(1)}, f32[20]{0:T(128)S(1)}, u32[]{:S(2)}, u32[]{:S(2)}) collective-permute-start(f32[20]{0:T(128)S(1)} %get-tuple-element.19), channel_id=1, source_target_pairs={{0,2},{2,4},{4,6},{1,3},{3,5},{5,7},{8,10},{10,12},{12,14},{9,11},... | collective-permute-start | bytes 248 | tf_op jit(solution)/shard_map/ppermute | solution.py:49
  551.9 26.3 %collective-permute-start.6 = (f32[20]{0:T(128)S(1)}, f32[20]{0:T(128)S(1)}, u32[]{:S(2)}, u32[]{:S(2)}) collective-permute-start(f32[20]{0:T(128)S(1)} %get-tuple-element.19), channel_id=1, source_target_pairs={{0,4},{2,6},{1,5},{3,7},{8,12},{10,14},{9,13},{11,15},{16,20},{18,... | collective-permute-start | bytes 248 | tf_op jit(solution)/shard_map/ppermute | solution.py:49
  578.2 0.8 copy-start.3
  580.8 2.2 collective-permute-start.8
Sparse Core Ops, SparseCore 0:
  11.0 118.2 all-gather.12
  133.1 112.7 all-gather.10
  249.6 112.7 all-gather.8
  366.0 112.7 all-gather.14

commit v5 on v4

--- a/solution.py
+++ b/solution.py
@@ -13,6 +13,7 @@
 COLS = 2816
 GROUP = 8
 SEQ = ("y", "core")
+DP = ("z", "x")
 
 
 def shifted(array, by):
@@ -108,17 +109,31 @@
         out_ref[:, lanes] = (part_ref[:, lanes] + pair_lanes(rise, pair) * readout).astype(jnp.bfloat16)
 
 
-def project(token_rows, input_weight, chunks=4):
-    width = token_rows.shape[1] // chunks
-    total = None
-    for chunk in range(chunks):
-        cols = slice(chunk * width, (chunk + 1) * width)
-        weight = lax.all_gather(input_weight[:, cols], ("dp",) + SEQ, axis=0, tiled=True)
-        piece = lax.dot_general(
-            token_rows[:, cols], weight, (((1,), (1,)), ((), ())), preferred_element_type=jnp.float32
-        )
-        total = piece if total is None else total + piece
-    return total.astype(jnp.bfloat16)
+def gathered_along(piece, axis):
+    n = lax.axis_size(axis)
+    if n == 1:
+        return piece
+    place = lax.axis_index(axis)
+    got = [piece] + [lax.ppermute(piece, axis, [(i, (i + s) % n) for i in range(n)]) for s in range(1, n)]
+    ring = jnp.stack(got[::-1])
+    rows = lax.dynamic_slice_in_dim(jnp.concatenate([ring, ring]), n - 1 - place, n, axis=0)
+    return rows.reshape((n * piece.shape[0],) + piece.shape[1:])
+
+
+def full_weight(local):
+    mine = gathered_along(gathered_along(gathered_along(local, "y"), "x"), "z")
+    other = lax.ppermute(mine, "core", [(0, 1), (1, 0)])
+    first = lax.axis_index("core") == 0
+    pieces = mine.shape[0] // local.shape[0]
+    early = jnp.where(first, mine, other).reshape((pieces, 1) + local.shape)
+    late = jnp.where(first, other, mine).reshape((pieces, 1) + local.shape)
+    return jnp.concatenate([early, late], axis=1).reshape((-1,) + local.shape[1:])
+
+
+def project(token_rows, input_weight):
+    return lax.dot_general(
+        token_rows, full_weight(input_weight), (((1,), (1,)), ((), ())), preferred_element_type=jnp.float32
+    ).astype(jnp.bfloat16)
 
 
 def body(hidden, log_decay, input_weight, conv_weight, conv_bias, skip_gain):
@@ -206,8 +221,12 @@
 
 
 def solution(mesh):
-    split = Mesh(mesh.devices.reshape(mesh.shape["dp"], mesh.shape["seq"] // 2, 2), ("dp", "y", "core"))
-    placed = (P("dp", SEQ, None), P("dp", None, SEQ), P(("dp",) + SEQ, None), P(), P(), P())
+    contexts = mesh.shape["dp"]
+    across = 4 if contexts % 4 == 0 else 1
+    split = Mesh(
+        mesh.devices.reshape(contexts // across, across, mesh.shape["seq"] // 2, 2), ("z", "x", "y", "core")
+    )
+    placed = (P(DP, SEQ, None), P(DP, None, SEQ), P(DP + SEQ, None), P(), P(), P())
     return jax.shard_map(
-        body, mesh=split, in_specs=placed, out_specs=P("dp", SEQ, None), check_vma=False
+        body, mesh=split, in_specs=placed, out_specs=P(DP, SEQ, None), check_vma=False
     )

time: 614 us -> 433 us (0.71)
  waiting for transfers between devices: 433 us -> 179 us
  local copies, waits for them, and re-layouts: 42.6 us -> 105 us
  starting transfers between devices: 12.3 us -> 33.5 us
  other arithmetic: 26 us -> 45.7 us
  matrix products: 34.4 us -> 16.5 us
  between operations: 13.4 us -> 0.4 us
    all_gather x4 -> x0, waiting for transfers between devices: 421 us -> none  [project(): lax.all_gather(input_weight[:, cols], ('dp',) + SEQ, axis=0, tiled=True)]
    ppermute x0 -> x14, waiting for transfers between devices: none -> 168 us  [the longest x13 160 us: gathered_along(): lax.ppermute(piece, axis, [(i, (i + s) % n) for i in range(n)])]
    reshape x2 -> x7, local copies, waits for them, and re-layouts: 0.98 us -> 52.2 us  [the longest x1 25.1 us: full_weight(): jnp.concatenate([early, late], axis=1).reshape((-1,) + local.shape[1:])]
    ppermute x0 -> x14, starting transfers between devices: none -> 22 us  [the longest x13 22 us: gathered_along(): lax.ppermute(piece, axis, [(i, (i + s) % n) for i in range(n)])]
    dot_general x4 -> x1, matrix products: 34.4 us -> 16.5 us  [project(): lax.dot_general(token_rows, full_weight(input_weight), (((1,), (1,)), (()...]
    concatenate x0 -> x1, other arithmetic: none -> 10.3 us  [full_weight(): jnp.concatenate([early, late], axis=1).reshape((-1,) + local.shape[1:])]
    select_n x0 -> x1, other arithmetic: none -> 10.2 us  [full_weight(): early = jnp.where(first, mine, other).reshape((pieces, 1) + local.shape)]
    concatenate x0 -> x4, local copies, waits for them, and re-layouts: none -> 9.29 us  [the longest x1 7.38 us: full_weight(): jnp.concatenate([early, late], axis=1).reshape((-1,) + local.shape[1:])]
  transfers between devices with their start and end apart: 13 -> 23, of which waited for: 7 -> 14; matrix products, arithmetic and copies ran while one was open for 9% -> 5% of each run, Pallas kernels for 3% -> 4%
where the time goes in v5:
time: 433 us; the launch traced here: 429 us
  waiting for transfers between devices  179 us (41%)
  local copies, waits for them, and re-layouts  105 us (24%)
  Pallas kernels  48.2 us (11%)
  other arithmetic  45.7 us (11%)
  starting transfers between devices  33.5 us (8%)
  matrix products  16.5 us (4%)
    ppermute x13, waiting for transfers between devices, gathered_along(): lax.ppermute(piece, axis, [(i, (i + s) % n) for i in range(n)])  160 us
    unnamed x41, local copies, waits for them, and re-layouts  28.4 us
    reshape x1, local copies, waits for them, and re-layouts, full_weight(): jnp.concatenate([early, late], axis=1).reshape((-1,) + local.shape[1:])  25.1 us
    ppermute x13, starting transfers between devices, gathered_along(): lax.ppermute(piece, axis, [(i, (i + s) % n) for i in range(n)])  22 us
    pallas_call x1, Pallas kernels, intra(): pl.pallas_call(intra_kernel, grid=(span_count, groups), in_specs=[x_spec,...  16.5 us
    dot_general x1, matrix products, project(): lax.dot_general(token_rows, full_weight(input_weight), (((1,), (1,)), (()...  16.5 us
    pallas_call x1, Pallas kernels, body(): pl.pallas_call(states_kernel, grid=(span_count, groups), in_specs=[x_spec...  15.9 us
    pallas_call x1, Pallas kernels, body(): pl.pallas_call(readout_kernel, grid=(span_count, groups), in_specs=[x_spe...  15.8 us
  transfers between devices with their start and end apart: 23, of which 14 were waited for; matrix products, arithmetic and copies ran while one was open for 5% of the time, Pallas kernels for 4%

profile of v5, /device:TPU:16, one launch (start us, length us, event | category | flops | bytes accessed | tf_op | source)
XLA Modules:
  0.0 428.7 jit_solution(15850635420260644219)
XLA Ops:
  0.5 2.9 collective-permute-start.2
  3.4 1.4 collective-permute-start.3
  5.3 1.8 collective-permute-done.2
  10.0 2.8 collective-permute-start.4
  14.6 7.9 %collective-permute-done.4 = bf16[44,2560]{1,0:T(8,128)(2,1)S(1)} collective-permute-done((bf16[44,2560]{1,0:T(8,128)(2,1)S(1)}, bf16[44,2560]{1,0:T(8,128)(2,1)S(1)}, u32[]{:S(2)}, u32[]{:S(2)}) %collective-permute-start.4) | collective-permute-done | bytes 225312 | tf_op jit(solution)/shard_map/ppermute | solution.py:117
  23.3 2.9 collective-permute-done.6
  27.5 5.9 %collective-permute-start.7 = (bf16[176,2560]{1,0:T(8,128)(2,1)}, bf16[176,2560]{1,0:T(8,128)(2,1)S(1)}, u32[]{:S(2)}, u32[]{:S(2)}) collective-permute-start(bf16[176,2560]{1,0:T(8,128)(2,1)} %reshape.169), channel_id=1, source_target_pairs={{0,224},{32,0},{64,32},{96,64},{128,96},{160,128},{192,160},{224,1... | collective-permute-start | bytes 2703368 | tf_op jit(solution)/shard_map/ppermute | solution.py:117
  33.4 1.5 collective-permute-start.8
  35.3 5.0 %collective-permute-start.10 = (bf16[176,2560]{1,0:T(8,128)(2,1)}, bf16[176,2560]{1,0:T(8,128)(2,1)}, u32[]{:S(2)}, u32[]{:S(2)}) collective-permute-start(bf16[176,2560]{1,0:T(8,128)(2,1)} %reshape.169), channel_id=1, source_target_pairs={{0,128},{32,160},{64,192},{96,224},{128,0},{160,32},{192,64},{224,... | collective-permute-start | bytes 2703368 | tf_op jit(solution)/shard_map/ppermute | solution.py:117
  40.5 34.2 %collective-permute-done.7 = bf16[176,2560]{1,0:T(8,128)(2,1)S(1)} collective-permute-done((bf16[176,2560]{1,0:T(8,128)(2,1)}, bf16[176,2560]{1,0:T(8,128)(2,1)S(1)}, u32[]{:S(2)}, u32[]{:S(2)}) %collective-permute-start.7) | collective-permute-done | bytes 901152 | tf_op jit(solution)/shard_map/ppermute | solution.py:117
  75.7 25.5 %collective-permute-done.8 = bf16[176,2560]{1,0:T(8,128)(2,1)} collective-permute-done((bf16[176,2560]{1,0:T(8,128)(2,1)}, bf16[176,2560]{1,0:T(8,128)(2,1)}, u32[]{:S(2)}, u32[]{:S(2)}) %collective-permute-start.8) | collective-permute-done | bytes 901152 | tf_op jit(solution)/shard_map/ppermute | solution.py:117
  101.3 2.2 bitcast_dynamic-update-slice_fusion.10
  103.4 84.9 %collective-permute-done.9 = bf16[176,2560]{1,0:T(8,128)(2,1)} collective-permute-done((bf16[176,2560]{1,0:T(8,128)(2,1)}, bf16[176,2560]{1,0:T(8,128)(2,1)}, u32[]{:S(2)}, u32[]{:S(2)}) %collective-permute-start.9) | collective-permute-done | bytes 901152 | tf_op jit(solution)/shard_map/ppermute | solution.py:117
  188.3 2.2 bitcast_dynamic-update-slice_fusion.8
  190.5 2.2 bitcast_dynamic-update-slice_fusion.6
  192.7 2.1 bitcast_dynamic-update-slice_fusion.4
  198.9 2.2 bitcast_dynamic-update-slice_fusion.11
  201.1 2.2 bitcast_dynamic-update-slice_fusion.9
  203.2 2.2 bitcast_dynamic-update-slice_fusion.7
  205.4 2.2 bitcast_dynamic-update-slice_fusion.5
  210.6 6.4 %constant_dynamic-slice_fusion = bf16[8,176,2560]{2,1,0:T(8,128)(2,1)} fusion(bf16[16,176,2560]{2,1,0:T(8,128)(2,1)} %constant_dynamic-update-slice_fusion.2, s32[]{:T(128)S(6)} %select_n.97), kind=kLoop, calls=%fused_computation.67 | loop fusion | bytes 14417924 | tf_op jit(solution)/shard_map/dynamic_slice | solution.py:119
  217.1 1.8 reduce-window.6
  220.3 8.6 %collective-permute-done.14 = bf16[1408,2560]{1,0:T(8,128)(2,1)} collective-permute-done((bf16[1408,2560]{1,0:T(8,128)(2,1)}, bf16[1408,2560]{1,0:T(8,128)(2,1)}, u32[]{:S(2)}, u32[]{:S(2)}) %collective-permute-start.14) | collective-permute-done | bytes 7208992 | tf_op jit(solution)/shard_map/ppermute | solution.py:125
  228.8 10.2 %broadcast_select_fusion.1 = (bf16[1408,2560]{1,0:T(8,128)(2,1)}, bf16[1408,2560]{1,0:T(8,128)(2,1)}) fusion(bf16[1408,2560]{1,0:T(8,128)(2,1)} %collective-permute-done.14, pred[]{:T(512)S(6)} %eq.4, bf16[8,176,2560]{2,1,0:T(8,128)(2,1)} %constant_dynamic-slice_fusion), kind=kLoop, calls=%fused_computation.3 | loop fusion | flops 7208960 | bytes 28835840 | tf_op jit(solution)/shard_map/jit(_where)/select_n | solution.py:128
  239.0 12.9 %reshape.171 = bf16[128,1,11,2560]{3,2,0,1:T(8,128)(2,1)} reshape(bf16[1408,2560]{1,0:T(8,128)(2,1)} %get-tuple-element.48) | data formatting | bytes 14417920 | tf_op jit(solution)/shard_map/reshape | solution.py:128
  251.9 12.9 %reshape.172 = bf16[128,1,11,2560]{3,2,0,1:T(8,128)(2,1)} reshape(bf16[1408,2560]{1,0:T(8,128)(2,1)} %get-tuple-element.49) | data formatting | bytes 14417920 | tf_op jit(solution)/shard_map/reshape | solution.py:129
  264.9 10.3 %pad_maximum_fusion = bf16[128,2,11,2560]{3,2,0,1:T(8,128)(2,1)S(1)} fusion(bf16[128,1,11,2560]{3,2,0,1:T(8,128)(2,1)} %reshape.172, bf16[128,1,11,2560]{3,2,0,1:T(8,128)(2,1)} %reshape.171), kind=kLoop, calls=%fused_computation | loop fusion | flops 7208960 | bytes 28835840 | tf_op jit(solution)/shard_map/concatenate | solution.py:130
  275.2 7.4 %copy.23 = bf16[128,2,11,2560]{3,2,1,0:T(8,128)(2,1)} copy(bf16[128,2,11,2560]{3,2,0,1:T(8,128)(2,1)S(1)} %pad_maximum_fusion) | data formatting | bytes 28835840 | tf_op jit(solution)/shard_map/concatenate | solution.py:130
  282.6 25.1 %reshape.173 = bf16[2816,2560]{1,0:T(8,128)(2,1)} reshape(bf16[128,2,11,2560]{3,2,1,0:T(8,128)(2,1)} %copy.23) | data formatting | bytes 28835840 | tf_op jit(solution)/shard_map/reshape | solution.py:130
  307.7 16.5 %fusion = bf16[768,2816]{1,0:T(8,128)(2,1)S(1)} fusion(bf16[2816,2560]{1,0:T(8,128)(2,1)} %reshape.173, bf16[1,768,2560]{2,1,0:T(8,128)(2,1)} %param.6), kind=kOutput, calls=%fused_computation.7 | convolution fusion | flops 11075125248 | bytes 22675456 | tf_op jit(solution)/shard_map/dot_general | solution.py:134
  324.2 2.1 copy-done
  326.4 2.0 collective-permute-start.15
  328.7 1.9 copy.25
  330.6 1.9 copy.26
  332.7 14.1 %multiply_convert_fusion.x_ref.b_ref.c_ref = bf16[768,2816]{1,0:T(8,128)(2,1)} fusion(bf16[768,2816]{1,0:T(8,128)(2,1)} %copy-done, bf16[3,2816]{1,0:T(4,128)(2,1)S(1)} %collective-permute-done.15, f32[2816]{0:T(1024)S(1)} %get-tuple-element.35, f32[2816]{0:T(1024)S(1)} %get-tuple-element.36, f32[2816]{0:T(1024)S(1)} %get-tuple-element.34, ...), kind=kLoop, calls=%fused_computation.1 | loop fusion | flops 56229888 | bytes 8723968 | tf_op jit(solution)/shard_map/convert_element_type | solution.py:154
  346.8 15.9 %shard_map.64 = f32[3,2560,128]{2,1,0:T(8,128)} custom-call(bf16[768,2816]{1,0:T(8,128)(2,1)} %multiply_convert_fusion.x_ref.b_ref.c_ref, bf16[768,2816]{1,0:T(8,128)(2,1)} %multiply_convert_fusion.x_ref.b_ref.c_ref, f32[5,768,8]{2,1,0:T(8,128)} %bitcast.101, f32[5,768,8]{2,1,0:T(8,128)} %bitcast.105), custom_call_target="tpu_custom_call" | custom-call | flops 503316480 | bytes 8060928 | tf_op jit(solution)/shard_map/pallas_call | solution.py:171
  362.7 2.4 fusion.13
  369.0 2.3 collective-permute-start.17
  372.6 1.5 collective-permute-start.21
  374.1 1.9 collective-permute-start.18
  376.0 1.5 collective-permute-start.20
  377.5 16.5 %shard_map.65.part_ref = f32[768,2560]{1,0:T(8,128)} custom-call(bf16[768,2816]{1,0:T(8,128)(2,1)} %multiply_convert_fusion.x_ref.b_ref.c_ref, bf16[768,2816]{1,0:T(8,128)(2,1)} %multiply_convert_fusion.x_ref.b_ref.c_ref, bf16[768,2816]{1,0:T(8,128)(2,1)} %multiply_convert_fusion.x_ref.b_ref.c_ref, f32[5,768,8]{2,1,0:T(8,128)} %bitcast.102, ...), custom_call_target="tpu_custom_call" | custom-call | flops 2264924160 | bytes 12189696 | tf_op jit(solution)/shard_map/pallas_call | solution.py:188
  394.1 9.0 %collective-permute-done.20 = f32[20]{0:T(128)S(1)} collective-permute-done((f32[20]{0:T(128)S(1)}, f32[20]{0:T(128)S(1)}, u32[]{:S(2)}, u32[]{:S(2)}) %collective-permute-start.20) | collective-permute-done | bytes 112 | tf_op jit(solution)/shard_map/ppermute | solution.py:50
  403.9 1.6 select_bitcast_fusion
  406.0 1.8 collective-permute-done.22
  407.9 2.8 multiply_add_fusion
  410.7 2.1 pad_maximum_fusion.2.enter_ref
  412.9 15.8 %shard_map.66 = bf16[768,2560]{1,0:T(8,128)(2,1)} custom-call(f32[768,2560]{1,0:T(8,128)} %shard_map.65.part_ref, bf16[768,2816]{1,0:T(8,128)(2,1)} %multiply_convert_fusion.x_ref.b_ref.c_ref, f32[5,768,8]{2,1,0:T(8,128)} %bitcast.103, f32[3,2560,128]{2,1,0:T(8,128)} %pad_maximum_fusion.2.enter_ref), custom_call_target="tpu_custom_call" | custom-call | flops 3019898880 | bytes 15728640 | tf_op jit(solution)/shard_map/pallas_call | solution.py:209
  (104 shorter events, 25.1 us)
Async XLA Ops:
  0.0 5.3 %collective-permute-start.1 = (bf16[11,2560]{1,0:T(8,128)(2,1)}, bf16[11,2560]{1,0:T(8,128)(2,1)S(1)}, u32[]{:S(2)}, u32[]{:S(2)}) collective-permute-start(bf16[11,2560]{1,0:T(8,128)(2,1)} %param.8), channel_id=1, source_target_pairs={{0,6},{2,0},{4,2},{6,4},{1,7},{3,1},{5,3},{7,5},{8,14},{10,8},{12,... | collective-permute-start | bytes 168968 | tf_op jit(solution)/shard_map/ppermute | solution.py:117
  0.5 6.6 %collective-permute-start.2 = (bf16[11,2560]{1,0:T(8,128)(2,1)}, bf16[11,2560]{1,0:T(8,128)(2,1)S(1)}, u32[]{:S(2)}, u32[]{:S(2)}) collective-permute-start(bf16[11,2560]{1,0:T(8,128)(2,1)} %param.8), channel_id=1, source_target_pairs={{0,4},{2,6},{4,0},{6,2},{1,5},{3,7},{5,1},{7,3},{8,12},{10,14},{12... | collective-permute-start | bytes 168968 | tf_op jit(solution)/shard_map/ppermute | solution.py:117
  3.4 4.7 %collective-permute-start.3 = (bf16[11,2560]{1,0:T(8,128)(2,1)}, bf16[11,2560]{1,0:T(8,128)(2,1)S(1)}, u32[]{:S(2)}, u32[]{:S(2)}) collective-permute-start(bf16[11,2560]{1,0:T(8,128)(2,1)} %param.8), channel_id=1, source_target_pairs={{0,2},{2,4},{4,6},{6,0},{1,3},{3,5},{5,7},{7,1},{8,10},{10,12},{12... | collective-permute-start | bytes 168968 | tf_op jit(solution)/shard_map/ppermute | solution.py:117
  10.0 12.5 %collective-permute-start.4 = (bf16[44,2560]{1,0:T(8,128)(2,1)S(1)}, bf16[44,2560]{1,0:T(8,128)(2,1)S(1)}, u32[]{:S(2)}, u32[]{:S(2)}) collective-permute-start(bf16[44,2560]{1,0:T(8,128)(2,1)S(1)} %reshape.168), channel_id=1, source_target_pairs={{0,24},{8,0},{16,8},{24,16},{1,25},{9,1},{17,9},{25,17},{2,26},{10... | collective-permute-start | bytes 675848 | tf_op jit(solution)/shard_map/ppermute | solution.py:117
  12.9 10.4 %collective-permute-start.5 = (bf16[44,2560]{1,0:T(8,128)(2,1)S(1)}, bf16[44,2560]{1,0:T(8,128)(2,1)S(1)}, u32[]{:S(2)}, u32[]{:S(2)}) collective-permute-start(bf16[44,2560]{1,0:T(8,128)(2,1)S(1)} %reshape.168), channel_id=1, source_target_pairs={{0,16},{8,24},{16,0},{24,8},{1,17},{9,25},{17,1},{25,9},{2,18},{10... | collective-permute-start | bytes 675848 | tf_op jit(solution)/shard_map/ppermute | solution.py:117
  13.7 12.5 %collective-permute-start.6 = (bf16[44,2560]{1,0:T(8,128)(2,1)S(1)}, bf16[44,2560]{1,0:T(8,128)(2,1)S(1)}, u32[]{:S(2)}, u32[]{:S(2)}) collective-permute-start(bf16[44,2560]{1,0:T(8,128)(2,1)S(1)} %reshape.168), channel_id=1, source_target_pairs={{0,8},{8,16},{16,24},{24,0},{1,9},{9,17},{17,25},{25,1},{2,10},{10... | collective-permute-start | bytes 675848 | tf_op jit(solution)/shard_map/ppermute | solution.py:117
  27.5 47.2 %collective-permute-start.7 = (bf16[176,2560]{1,0:T(8,128)(2,1)}, bf16[176,2560]{1,0:T(8,128)(2,1)S(1)}, u32[]{:S(2)}, u32[]{:S(2)}) collective-permute-start(bf16[176,2560]{1,0:T(8,128)(2,1)} %reshape.169), channel_id=1, source_target_pairs={{0,224},{32,0},{64,32},{96,64},{128,96},{160,128},{192,160},{224,1... | collective-permute-start | bytes 2703368 | tf_op jit(solution)/shard_map/ppermute | solution.py:117
  33.4 67.9 %collective-permute-start.8 = (bf16[176,2560]{1,0:T(8,128)(2,1)}, bf16[176,2560]{1,0:T(8,128)(2,1)}, u32[]{:S(2)}, u32[]{:S(2)}) collective-permute-start(bf16[176,2560]{1,0:T(8,128)(2,1)} %reshape.169), channel_id=1, source_target_pairs={{0,192},{32,224},{64,0},{96,32},{128,64},{160,96},{192,128},{224,1... | collective-permute-start | bytes 2703368 | tf_op jit(solution)/shard_map/ppermute | solution.py:117
  34.8 153.5 %collective-permute-start.9 = (bf16[176,2560]{1,0:T(8,128)(2,1)}, bf16[176,2560]{1,0:T(8,128)(2,1)}, u32[]{:S(2)}, u32[]{:S(2)}) collective-permute-start(bf16[176,2560]{1,0:T(8,128)(2,1)} %reshape.169), channel_id=1, source_target_pairs={{0,160},{32,192},{64,224},{96,0},{128,32},{160,64},{192,96},{224,1... | collective-permute-start | bytes 2703368 | tf_op jit(solution)/shard_map/ppermute | solution.py:117
  35.3 155.2 %collective-permute-start.10 = (bf16[176,2560]{1,0:T(8,128)(2,1)}, bf16[176,2560]{1,0:T(8,128)(2,1)}, u32[]{:S(2)}, u32[]{:S(2)}) collective-permute-start(bf16[176,2560]{1,0:T(8,128)(2,1)} %reshape.169), channel_id=1, source_target_pairs={{0,128},{32,160},{64,192},{96,224},{128,0},{160,32},{192,64},{224,... | collective-permute-start | bytes 2703368 | tf_op jit(solution)/shard_map/ppermute | solution.py:117
  40.3 152.3 %collective-permute-start.11 = (bf16[176,2560]{1,0:T(8,128)(2,1)}, bf16[176,2560]{1,0:T(8,128)(2,1)}, u32[]{:S(2)}, u32[]{:S(2)}) collective-permute-start(bf16[176,2560]{1,0:T(8,128)(2,1)} %reshape.169), channel_id=1, source_target_pairs={{0,96},{32,128},{64,160},{96,192},{128,224},{160,0},{192,32},{224,... | collective-permute-start | bytes 2703368 | tf_op jit(solution)/shard_map/ppermute | solution.py:117
  74.7 120.1 %collective-permute-start.12 = (bf16[176,2560]{1,0:T(8,128)(2,1)}, bf16[176,2560]{1,0:T(8,128)(2,1)S(1)}, u32[]{:S(2)}, u32[]{:S(2)}) collective-permute-start(bf16[176,2560]{1,0:T(8,128)(2,1)} %reshape.169), channel_id=1, source_target_pairs={{0,64},{32,96},{64,128},{96,160},{128,192},{160,224},{192,0},{224,... | collective-permute-start | bytes 2703368 | tf_op jit(solution)/shard_map/ppermute | solution.py:117
  101.3 94.6 %collective-permute-start.13 = (bf16[176,2560]{1,0:T(8,128)(2,1)}, bf16[176,2560]{1,0:T(8,128)(2,1)S(1)}, u32[]{:S(2)}, u32[]{:S(2)}) collective-permute-start(bf16[176,2560]{1,0:T(8,128)(2,1)} %reshape.169), channel_id=1, source_target_pairs={{0,32},{32,64},{64,96},{96,128},{128,160},{160,192},{192,224},{224... | collective-permute-start | bytes 2703368 | tf_op jit(solution)/shard_map/ppermute | solution.py:117
  210.6 6.4 %copy-start.2 = (f32[1,40,768]{2,1,0:T(8,128)S(1)}, f32[1,40,768]{2,1,0:T(8,128)}, u32[]{:S(2)}) copy-start(f32[1,40,768]{2,1,0:T(8,128)} %param.7) | copy-start | bytes 368644
  217.0 11.8 %collective-permute-start.14 = (bf16[1408,2560]{1,0:T(8,128)(2,1)}, bf16[1408,2560]{1,0:T(8,128)(2,1)}, u32[]{:S(2)}, u32[]{:S(2)}) collective-permute-start(bf16[1408,2560]{1,0:T(8,128)(2,1)} %bitcast.18), channel_id=1, source_target_pairs={{0,1},{1,0},{2,3},{3,2},{4,5},{5,4},{6,7},{7,6},{8,9},{9,8},{10,11... | collective-permute-start | bytes 21626888 | tf_op jit(solution)/shard_map/ppermute | solution.py:125
  307.7 20.7 %copy-start.3 = (bf16[4,2816]{1,0:T(4,128)(2,1)S(1)}, bf16[4,2816]{1,0:T(4,128)(2,1)}, u32[]{:S(2)}) copy-start(bf16[4,2816]{1,0:T(4,128)(2,1)} %param.9) | copy-start | bytes 67588
  307.7 25.0 %copy-start.4 = (f32[2816]{0:T(1024)S(1)}, f32[2816]{0:T(1024)}, u32[]{:S(2)}) copy-start(f32[2816]{0:T(1024)} %param.10) | copy-start | bytes 33796
  324.2 2.1 copy-start
  326.4 6.4 %collective-permute-start.15 = (bf16[3,2816]{1,0:T(4,128)(2,1)S(1)}, bf16[3,2816]{1,0:T(4,128)(2,1)S(1)}, u32[]{:S(2)}, u32[]{:S(2)}) collective-permute-start(bf16[3,2816]{1,0:T(4,128)(2,1)S(1)} %slice.78), channel_id=1, source_target_pairs={{0,1},{1,2},{2,3},{3,4},{4,5},{5,6},{6,7},{8,9},{9,10},{10,11},{11... | collective-permute-start | bytes 50696 | tf_op jit(solution)/shard_map/ppermute | solution.py:22
  362.7 4.4 %copy-start.5 = (f32[40]{0:T(128)S(1)}, f32[40]{0:T(128)}, u32[]{:S(2)}) copy-start(f32[40]{0:T(128)} %param.11) | copy-start | bytes 484
  365.5 2.5 collective-permute-start.16
  366.3 1.6 collective-permute-start
  369.0 34.1 %collective-permute-start.17 = (f32[20,64,128]{2,1,0:T(8,128)}, f32[20,64,128]{2,1,0:T(8,128)S(1)}, u32[]{:S(2)}, u32[]{:S(2)}) collective-permute-start(f32[20,64,128]{2,1,0:T(8,128)} %fusion.4), channel_id=1, source_target_pairs={{0,2},{2,4},{4,6},{1,3},{3,5},{5,7},{8,10},{10,12},{12,14},{9,11},... | collective-permute-start | bytes 1966088 | tf_op jit(solution)/shard_map/ppermute | solution.py:50
  371.3 31.8 %collective-permute-start.19 = (f32[20,64,128]{2,1,0:T(8,128)}, f32[20,64,128]{2,1,0:T(8,128)S(1)}, u32[]{:S(2)}, u32[]{:S(2)}) collective-permute-start(f32[20,64,128]{2,1,0:T(8,128)} %fusion.4), channel_id=1, source_target_pairs={{0,4},{2,6},{1,5},{3,7},{8,12},{10,14},{9,13},{11,15},{16,20},{18,... | collective-permute-start | bytes 1966088 | tf_op jit(solution)/shard_map/ppermute | solution.py:50
  372.6 30.5 %collective-permute-start.21 = (f32[20,64,128]{2,1,0:T(8,128)}, f32[20,64,128]{2,1,0:T(8,128)}, u32[]{:S(2)}, u32[]{:S(2)}) collective-permute-start(f32[20,64,128]{2,1,0:T(8,128)} %fusion.4), channel_id=1, source_target_pairs={{0,6},{1,7},{8,14},{9,15},{16,22},{17,23},{24,30},{25,31},{32,38},... | collective-permute-start | bytes 1966088 | tf_op jit(solution)/shard_map/ppermute | solution.py:50
  374.1 19.9 %collective-permute-start.18 = (f32[20]{0:T(128)S(1)}, f32[20]{0:T(128)S(1)}, u32[]{:S(2)}, u32[]{:S(2)}) collective-permute-start(f32[20]{0:T(128)S(1)} %get-tuple-element.19), channel_id=1, source_target_pairs={{0,2},{2,4},{4,6},{1,3},{3,5},{5,7},{8,10},{10,12},{12,14},{9,11},... | collective-permute-start | bytes 248 | tf_op jit(solution)/shard_map/ppermute | solution.py:50
  376.0 27.0 %collective-permute-start.20 = (f32[20]{0:T(128)S(1)}, f32[20]{0:T(128)S(1)}, u32[]{:S(2)}, u32[]{:S(2)}) collective-permute-start(f32[20]{0:T(128)S(1)} %get-tuple-element.19), channel_id=1, source_target_pairs={{0,4},{2,6},{1,5},{3,7},{8,12},{10,14},{9,13},{11,15},{16,20},{18,... | collective-permute-start | bytes 248 | tf_op jit(solution)/shard_map/ppermute | solution.py:50
  403.1 0.8 copy-start.1
  405.6 2.2 collective-permute-start.22

commit v6 on v4

--- a/solution.py
+++ b/solution.py
@@ -108,17 +108,10 @@
         out_ref[:, lanes] = (part_ref[:, lanes] + pair_lanes(rise, pair) * readout).astype(jnp.bfloat16)
 
 
-def project(token_rows, input_weight, chunks=4):
-    width = token_rows.shape[1] // chunks
-    total = None
-    for chunk in range(chunks):
-        cols = slice(chunk * width, (chunk + 1) * width)
-        weight = lax.all_gather(input_weight[:, cols], ("dp",) + SEQ, axis=0, tiled=True)
-        piece = lax.dot_general(
-            token_rows[:, cols], weight, (((1,), (1,)), ((), ())), preferred_element_type=jnp.float32
-        )
-        total = piece if total is None else total + piece
-    return total.astype(jnp.bfloat16)
+def project(token_rows, input_weight):
+    weight = lax.all_gather(input_weight, ("dp",) + SEQ, axis=0, tiled=False)
+    flipped = lax.dot_general(weight, token_rows, (((2,), (1,)), ((), ())), preferred_element_type=jnp.float32)
+    return flipped.astype(jnp.bfloat16).reshape(COLS, token_rows.shape[0]).T
 
 
 def body(hidden, log_decay, input_weight, conv_weight, conv_bias, skip_gain):

time: 614 us -> 311 us (0.51)
  waiting for transfers between devices: 433 us -> 143 us
  local copies, waits for them, and re-layouts: 42.6 us -> 30.7 us
    all_gather x4 -> x1, waiting for transfers between devices: 421 us -> 132 us  [project(): weight = lax.all_gather(input_weight, ('dp',) + SEQ, axis=0, tiled=False)]
    unnamed x21 -> x8, local copies, waits for them, and re-layouts: 33 us -> 0.81 us
    reshape x2 -> x4, local copies, waits for them, and re-layouts: 0.98 us -> 15.2 us  [the longest x2 14.2 us: project(): return flipped.astype(jnp.bfloat16).reshape(COLS, token_rows.shape[0]).T]
    dot_general x4 -> x1, matrix products: 34.4 us -> 33.5 us  [project(): lax.dot_general(weight, token_rows, (((2,), (1,)), ((), ())), preferred_e...]
  transfers between devices with their start and end apart: 13 -> 10, of which waited for: 7 -> 4; matrix products, arithmetic and copies ran while one was open for 9% -> 4% of each run, Pallas kernels for 3% -> 5%
where the time goes in v6:
time: 311 us; the launch traced here: 308 us
  waiting for transfers between devices  143 us (46%)
  Pallas kernels  48.2 us (15%)
  matrix products  33.5 us (11%)
  local copies, waits for them, and re-layouts  30.7 us (10%)
  other arithmetic  26 us (8%)
  between operations  13.7 us (4%)
  starting transfers between devices  12 us (4%)
    all_gather x1, waiting for transfers between devices, project(): weight = lax.all_gather(input_weight, ('dp',) + SEQ, axis=0, tiled=False)  132 us
    dot_general x1, matrix products, project(): lax.dot_general(weight, token_rows, (((2,), (1,)), ((), ())), preferred_e...  33.5 us
    pallas_call x1, Pallas kernels, intra(): pl.pallas_call(intra_kernel, grid=(span_count, groups), in_specs=[x_spec,...  16.6 us
    pallas_call x1, Pallas kernels, body(): pl.pallas_call(states_kernel, grid=(span_count, groups), in_specs=[x_spec...  15.9 us
    pallas_call x1, Pallas kernels, body(): pl.pallas_call(readout_kernel, grid=(span_count, groups), in_specs=[x_spe...  15.8 us
    reshape x2, local copies, waits for them, and re-layouts, project(): return flipped.astype(jnp.bfloat16).reshape(COLS, token_rows.shape[0]).T  14.2 us
    convert_element_type x1, other arithmetic, body(): active = jax.nn.silu(filtered).astype(jnp.bfloat16)  13.9 us
    ppermute x2, waiting for transfers between devices, scan_entering(): lax.ppermute(chip_total, 'y', pairs)  8.44 us
  transfers between devices with their start and end apart: 10, of which 4 were waited for; matrix products, arithmetic and copies ran while one was open for 4% of the time, Pallas kernels for 5%

profile of v6, /device:TPU:16, one launch (start us, length us, event | category | flops | bytes accessed | tf_op | source)
XLA Modules:
  0.0 307.5 jit_solution(16284690640111300952)
XLA Ops:
  6.5 0.7 all-gather.4.cloned.1.call-update
  7.3 1.0 reshape.150
  8.2 1.8 reduce-window.6
  10.0 0.1 slice.75
  10.1 0.1 copy.34
  10.3 0.1 copy_bitcast_fusion
  10.4 0.2 slice_reduce_fusion.1
  10.6 1.6 negate_bitcast_fusion
  12.2 0.1 broadcast_add_fusion
  12.3 132.4 %all-gather.4.cloned.1.call-done = bf16[256,11,2560]{2,1,0:T(8,128)(2,1)} async-done(((bf16[1,11,2560]{2,1,0:T(8,128)(2,1)}), bf16[256,11,2560]{2,1,0:T(8,128)(2,1)}) %all-gather.4.cloned.1.call-update) | async-done | bytes 14417936 | tf_op jit(solution)/shard_map/all_gather | solution.py:112
  144.7 33.5 %fusion.5 = bf16[256,11,768]{2,0,1:T(8,128)(2,1)S(1)} fusion(bf16[1,768,2560]{2,1,0:T(8,128)(2,1)} %param.6, bf16[256,11,2560]{2,1,0:T(8,128)(2,1)} %all-gather.4.cloned.1.call-done), kind=kOutput, calls=%fused_computation.10 | convolution fusion | flops 11075125248 | bytes 22675456 | tf_op jit(solution)/shard_map/dot_general | solution.py:113
  178.2 5.3 %copy.38 = bf16[256,11,768]{2,1,0:T(8,128)(2,1)} copy(bf16[256,11,768]{2,0,1:T(8,128)(2,1)S(1)} %fusion.5) | data formatting | bytes 8650752 | tf_op jit(solution)/shard_map/convert_element_type | solution.py:114
  183.5 7.7 %reshape.153 = bf16[2816,768]{1,0:T(8,128)(2,1)} reshape(bf16[256,11,768]{2,1,0:T(8,128)(2,1)} %copy.38) | data formatting | bytes 8650752 | tf_op jit(solution)/shard_map/reshape | solution.py:114
  191.2 6.5 %copy.39 = bf16[2816,768]{0,1:T(8,128)(2,1)} copy(bf16[2816,768]{1,0:T(8,128)(2,1)} %reshape.153) | data formatting | bytes 8650752 | tf_op jit(solution)/shard_map/reshape | solution.py:114
  197.7 0.8 slice.78
  198.5 2.2 collective-permute-start.1
  200.7 0.1 convert_reduce_fusion.3
  200.9 0.1 reduce_window_sum.25
  201.0 1.8 copy.41
  202.9 1.9 copy.42
  204.7 0.1 mul.159
  204.8 0.1 exp.58
  204.9 0.1 exp.56
  205.0 13.9 %multiply_convert_fusion.x_ref.b_ref.c_ref = bf16[768,2816]{1,0:T(8,128)(2,1)} fusion(bf16[768,2816]{1,0:T(8,128)(2,1)} %bitcast.62, bf16[3,2816]{1,0:T(4,128)(2,1)S(1)} %collective-permute-done.1, f32[2816]{0:T(1024)S(1)} %get-tuple-element.35, f32[2816]{0:T(1024)S(1)} %get-tuple-element.36, f32[2816]{0:T(1024)S(1)} %get-tuple-element.34, ...), kind=kLoop, calls=%fused_computation.2 | loop fusion | flops 56229888 | bytes 8723968 | tf_op jit(solution)/shard_map/convert_element_type | solution.py:132
  218.9 15.9 %shard_map.64 = f32[3,2560,128]{2,1,0:T(8,128)} custom-call(bf16[768,2816]{1,0:T(8,128)(2,1)} %multiply_convert_fusion.x_ref.b_ref.c_ref, bf16[768,2816]{1,0:T(8,128)(2,1)} %multiply_convert_fusion.x_ref.b_ref.c_ref, f32[5,768,8]{2,1,0:T(8,128)} %bitcast.58, f32[5,768,8]{2,1,0:T(8,128)} %bitcast.64), custom_call_target="tpu_custom_call" | custom-call | flops 503316480 | bytes 8060928 | tf_op jit(solution)/shard_map/pallas_call | solution.py:149
  234.8 2.4 fusion.19
  237.2 0.3 multiply_add_fusion.2
  237.6 1.1 collective-permute-start.2
  238.9 0.7 reduce_window_sum.26.cum_row_ref
  239.7 0.7 broadcast_in_dim_reshape.3.gain_ref
  240.4 0.1 collective-permute-done
  240.5 1.0 fusion.10
  241.5 2.5 collective-permute-start.3
  244.0 1.3 collective-permute-start.5
  245.3 1.6 collective-permute-start.7
  246.8 1.9 collective-permute-start.4
  248.8 1.3 collective-permute-start.6
  250.1 16.6 %shard_map.65.part_ref = f32[768,2560]{1,0:T(8,128)} custom-call(bf16[768,2816]{1,0:T(8,128)(2,1)} %multiply_convert_fusion.x_ref.b_ref.c_ref, bf16[768,2816]{1,0:T(8,128)(2,1)} %multiply_convert_fusion.x_ref.b_ref.c_ref, bf16[768,2816]{1,0:T(8,128)(2,1)} %multiply_convert_fusion.x_ref.b_ref.c_ref, f32[5,768,8]{2,1,0:T(8,128)} %bitcast.59, ...), custom_call_target="tpu_custom_call" | custom-call | flops 2264924160 | bytes 12189696 | tf_op jit(solution)/shard_map/pallas_call | solution.py:166
  266.6 8.4 %collective-permute-done.6 = f32[20]{0:T(128)S(1)} collective-permute-done((f32[20]{0:T(128)S(1)}, f32[20]{0:T(128)S(1)}, u32[]{:S(2)}, u32[]{:S(2)}) %collective-permute-start.6) | collective-permute-done | bytes 112 | tf_op jit(solution)/shard_map/ppermute | solution.py:49
  275.1 0.8 copy-done
  275.9 1.6 select_bitcast_fusion
  277.4 0.2 fusion.11
  277.6 0.1 collective-permute-start.8
  278.0 1.8 collective-permute-done.8
  279.8 0.1 maximum_select_fusion
  279.9 2.8 multiply_add_fusion
  282.7 2.2 pad_maximum_fusion.1.enter_ref
  284.9 15.8 %shard_map.66 = bf16[768,2560]{1,0:T(8,128)(2,1)} custom-call(f32[768,2560]{1,0:T(8,128)} %shard_map.65.part_ref, bf16[768,2816]{1,0:T(8,128)(2,1)} %multiply_convert_fusion.x_ref.b_ref.c_ref, f32[5,768,8]{2,1,0:T(8,128)} %bitcast.60, f32[3,2560,128]{2,1,0:T(8,128)} %pad_maximum_fusion.1.enter_ref), custom_call_target="tpu_custom_call" | custom-call | flops 3019898880 | bytes 15728640 | tf_op jit(solution)/shard_map/pallas_call | solution.py:187
  (33 shorter events, 0.8 us)
Async XLA Ops:
  6.5 138.2 %all-gather.4.cloned.1.call-start = ((), (), s32[]{:S(2)}) async-start(), calls=%async_computation | async-start | bytes 21053440 | tf_op jit(solution)/shard_map/all_gather | solution.py:112
  191.2 9.5 %copy-start.1 = (bf16[4,2816]{1,0:T(4,128)(2,1)S(1)}, bf16[4,2816]{1,0:T(4,128)(2,1)}, u32[]{:S(2)}) copy-start(bf16[4,2816]{1,0:T(4,128)(2,1)} %param.9) | copy-start | bytes 67588
  197.7 7.3 %copy-start.2 = (f32[2816]{0:T(1024)S(1)}, f32[2816]{0:T(1024)}, u32[]{:S(2)}) copy-start(f32[2816]{0:T(1024)} %param.10) | copy-start | bytes 33796
  198.5 6.5 %collective-permute-start.1 = (bf16[3,2816]{1,0:T(4,128)(2,1)S(1)}, bf16[3,2816]{1,0:T(4,128)(2,1)S(1)}, u32[]{:S(2)}, u32[]{:S(2)}) collective-permute-start(bf16[3,2816]{1,0:T(4,128)(2,1)S(1)} %slice.78), channel_id=1, source_target_pairs={{0,1},{1,2},{2,3},{3,4},{4,5},{5,6},{6,7},{8,9},{9,10},{10,11},{11... | collective-permute-start | bytes 50696 | tf_op jit(solution)/shard_map/ppermute | solution.py:21
  237.2 2.4 copy-start.3
  237.6 2.9 collective-permute-start.2
  238.8 1.6 collective-permute-start
  241.5 33.6 %collective-permute-start.3 = (f32[20,64,128]{2,1,0:T(8,128)}, f32[20,64,128]{2,1,0:T(8,128)S(1)}, u32[]{:S(2)}, u32[]{:S(2)}) collective-permute-start(f32[20,64,128]{2,1,0:T(8,128)} %fusion.10), channel_id=1, source_target_pairs={{0,2},{2,4},{4,6},{1,3},{3,5},{5,7},{8,10},{10,12},{12,14},{9,11},... | collective-permute-start | bytes 1966088 | tf_op jit(solution)/shard_map/ppermute | solution.py:49
  244.0 31.1 %collective-permute-start.5 = (f32[20,64,128]{2,1,0:T(8,128)}, f32[20,64,128]{2,1,0:T(8,128)S(1)}, u32[]{:S(2)}, u32[]{:S(2)}) collective-permute-start(f32[20,64,128]{2,1,0:T(8,128)} %fusion.10), channel_id=1, source_target_pairs={{0,4},{2,6},{1,5},{3,7},{8,12},{10,14},{9,13},{11,15},{16,20},{18,... | collective-permute-start | bytes 1966088 | tf_op jit(solution)/shard_map/ppermute | solution.py:49
  245.3 29.8 %collective-permute-start.7 = (f32[20,64,128]{2,1,0:T(8,128)}, f32[20,64,128]{2,1,0:T(8,128)}, u32[]{:S(2)}, u32[]{:S(2)}) collective-permute-start(f32[20,64,128]{2,1,0:T(8,128)} %fusion.10), channel_id=1, source_target_pairs={{0,6},{1,7},{8,14},{9,15},{16,22},{17,23},{24,30},{25,31},{32,38},... | collective-permute-start | bytes 1966088 | tf_op jit(solution)/shard_map/ppermute | solution.py:49
  246.8 19.8 %collective-permute-start.4 = (f32[20]{0:T(128)S(1)}, f32[20]{0:T(128)S(1)}, u32[]{:S(2)}, u32[]{:S(2)}) collective-permute-start(f32[20]{0:T(128)S(1)} %get-tuple-element.19), channel_id=1, source_target_pairs={{0,2},{2,4},{4,6},{1,3},{3,5},{5,7},{8,10},{10,12},{12,14},{9,11},... | collective-permute-start | bytes 248 | tf_op jit(solution)/shard_map/ppermute | solution.py:49
  248.8 26.3 %collective-permute-start.6 = (f32[20]{0:T(128)S(1)}, f32[20]{0:T(128)S(1)}, u32[]{:S(2)}, u32[]{:S(2)}) collective-permute-start(f32[20]{0:T(128)S(1)} %get-tuple-element.19), channel_id=1, source_target_pairs={{0,4},{2,6},{1,5},{3,7},{8,12},{10,14},{9,13},{11,15},{16,20},{18,... | collective-permute-start | bytes 248 | tf_op jit(solution)/shard_map/ppermute | solution.py:49
  275.1 0.8 copy-start
  277.6 2.2 collective-permute-start.8
Sparse Core Ops, SparseCore 0:
  10.9 133.7 all-gather.3

commit v7 on v6

--- a/solution.py
+++ b/solution.py
@@ -109,9 +109,12 @@
 
 
 def project(token_rows, input_weight):
-    weight = lax.all_gather(input_weight, ("dp",) + SEQ, axis=0, tiled=False)
-    flipped = lax.dot_general(weight, token_rows, (((2,), (1,)), ((), ())), preferred_element_type=jnp.float32)
-    return flipped.astype(jnp.bfloat16).reshape(COLS, token_rows.shape[0]).T
+    return lax.dot_general(
+        token_rows,
+        lax.all_gather(input_weight, ("dp",) + SEQ, axis=0, tiled=True),
+        (((1,), (1,)), ((), ())),
+        preferred_element_type=jnp.float32,
+    ).astype(jnp.bfloat16)
 
 
 def body(hidden, log_decay, input_weight, conv_weight, conv_bias, skip_gain):

time: 311 us -> 301 us (0.968)
  matrix products: 33.5 us -> 16.5 us
  local copies, waits for them, and re-layouts: 30.7 us -> 37.4 us
    unnamed x8 -> x11, local copies, waits for them, and re-layouts: 0.81 us -> 27.8 us
    dot_general x1, matrix products: 33.5 us -> 16.5 us  [project(): lax.dot_general(token_rows, lax.all_gather(input_weight, ('dp',) + SEQ, a...]
    reshape x4 -> x2, local copies, waits for them, and re-layouts: 15.2 us -> 0.98 us  [the longest x2 14.2 us: project(): return flipped.astype(jnp.bfloat16).reshape(COLS, token_rows.shape[0]).T]
    convert_element_type x1 -> x0, local copies, waits for them, and re-layouts: 5.27 us -> none  [project(): return flipped.astype(jnp.bfloat16).reshape(COLS, token_rows.shape[0]).T]
  transfers between devices with their start and end apart: 10 -> 10, of which waited for: 4 -> 4; matrix products, arithmetic and copies ran while one was open for 4% -> 4% of each run, Pallas kernels for 5% -> 6%
where the time goes in v7:
time: 301 us; the launch traced here: 297 us
  waiting for transfers between devices  143 us (48%)
  Pallas kernels  48.2 us (16%)
  local copies, waits for them, and re-layouts  37.4 us (12%)
  other arithmetic  26.2 us (9%)
  matrix products  16.5 us (5%)
  between operations  13.7 us (5%)
  starting transfers between devices  12 us (4%)
    all_gather x1, waiting for transfers between devices, project(): lax.all_gather(input_weight, ('dp',) + SEQ, axis=0, tiled=True)  132 us
    unnamed x11, local copies, waits for them, and re-layouts  27.8 us
    pallas_call x1, Pallas kernels, intra(): pl.pallas_call(intra_kernel, grid=(span_count, groups), in_specs=[x_spec,...  16.6 us
    dot_general x1, matrix products, project(): lax.dot_general(token_rows, lax.all_gather(input_weight, ('dp',) + SEQ, a...  16.5 us
    pallas_call x1, Pallas kernels, body(): pl.pallas_call(states_kernel, grid=(span_count, groups), in_specs=[x_spec...  15.9 us
    pallas_call x1, Pallas kernels, body(): pl.pallas_call(readout_kernel, grid=(span_count, groups), in_specs=[x_spe...  15.8 us
    convert_element_type x1, other arithmetic, body(): active = jax.nn.silu(filtered).astype(jnp.bfloat16)  13.9 us
    ppermute x2, waiting for transfers between devices, scan_entering(): lax.ppermute(chip_total, 'y', pairs)  8.45 us
  transfers between devices with their start and end apart: 10, of which 4 were waited for; matrix products, arithmetic and copies ran while one was open for 4% of the time, Pallas kernels for 6%

profile of v7, /device:TPU:16, one launch (start us, length us, event | category | flops | bytes accessed | tf_op | source)
XLA Modules:
  0.0 297.4 jit_solution(7109136969979894714)
XLA Ops:
  6.5 0.7 all-gather.3.cloned.1.call-update
  7.3 1.0 reshape.147
  8.2 1.8 reduce-window.6
  10.0 0.1 slice.75
  10.1 0.1 copy.27
  10.3 0.1 copy_bitcast_fusion
  10.4 0.2 slice_reduce_fusion.1
  10.6 1.6 negate_bitcast_fusion
  12.2 0.1 broadcast_add_fusion
  12.3 132.4 %all-gather.3.cloned.1.call-done = bf16[256,11,2560]{2,1,0:T(8,128)(2,1)} async-done(((bf16[1,11,2560]{2,1,0:T(8,128)(2,1)}), bf16[256,11,2560]{2,1,0:T(8,128)(2,1)}) %all-gather.3.cloned.1.call-update) | async-done | bytes 14417936 | tf_op jit(solution)/shard_map/all_gather | solution.py:114
  144.7 25.0 %reshape.155 = bf16[2816,2560]{1,0:T(8,128)(2,1)} reshape(bf16[256,11,2560]{2,1,0:T(8,128)(2,1)} %all-gather.3.cloned.1.call-done) | data formatting | bytes 28835840
  169.8 16.5 %convolution_convert_fusion = bf16[768,2816]{1,0:T(8,128)(2,1)S(1)} fusion(bf16[2816,2560]{1,0:T(8,128)(2,1)} %reshape.155, bf16[1,768,2560]{2,1,0:T(8,128)(2,1)} %param.6), kind=kOutput, calls=%fused_computation.3 | convolution fusion | flops 11075125248 | bytes 22675456 | tf_op jit(solution)/shard_map/dot_general | solution.py:112
  186.3 2.0 copy-done
  188.3 2.2 collective-permute-start.1
  190.4 0.1 convert_reduce_fusion.3
  190.6 0.1 reduce_window_sum.25
  190.8 1.8 copy.31
  192.6 1.9 copy.32
  194.5 0.1 mul.159
  194.5 0.1 exp.58
  194.6 0.1 exp.56
  194.7 13.9 %multiply_convert_fusion.x_ref.b_ref.c_ref = bf16[768,2816]{1,0:T(8,128)(2,1)} fusion(bf16[768,2816]{1,0:T(8,128)(2,1)} %copy-done, bf16[3,2816]{1,0:T(4,128)(2,1)S(1)} %collective-permute-done.1, f32[2816]{0:T(1024)S(1)} %get-tuple-element.35, f32[2816]{0:T(1024)S(1)} %get-tuple-element.36, f32[2816]{0:T(1024)S(1)} %get-tuple-element.34, ...), kind=kLoop, calls=%fused_computation | loop fusion | flops 56229888 | bytes 8723968 | tf_op jit(solution)/shard_map/convert_element_type | solution.py:135
  208.7 15.9 %shard_map.64 = f32[3,2560,128]{2,1,0:T(8,128)} custom-call(bf16[768,2816]{1,0:T(8,128)(2,1)} %multiply_convert_fusion.x_ref.b_ref.c_ref, bf16[768,2816]{1,0:T(8,128)(2,1)} %multiply_convert_fusion.x_ref.b_ref.c_ref, f32[5,768,8]{2,1,0:T(8,128)} %bitcast.55, f32[5,768,8]{2,1,0:T(8,128)} %bitcast.59), custom_call_target="tpu_custom_call" | custom-call | flops 503316480 | bytes 8060928 | tf_op jit(solution)/shard_map/pallas_call | solution.py:152
  224.5 2.4 fusion.12
  226.9 0.3 multiply_add_fusion.2
  227.3 1.2 collective-permute-start.2
  228.5 0.1 reshape.149
  228.6 0.7 reduce_window_sum.26.cum_row_ref
  229.4 0.7 broadcast_in_dim_reshape.3.gain_ref
  230.1 0.1 collective-permute-done
  230.2 1.0 fusion.3
  231.2 2.4 collective-permute-start.3
  233.7 1.3 collective-permute-start.5
  235.0 1.6 collective-permute-start.7
  236.5 1.9 collective-permute-start.4
  238.5 1.3 collective-permute-start.6
  239.8 16.6 %shard_map.65.part_ref = f32[768,2560]{1,0:T(8,128)} custom-call(bf16[768,2816]{1,0:T(8,128)(2,1)} %multiply_convert_fusion.x_ref.b_ref.c_ref, bf16[768,2816]{1,0:T(8,128)(2,1)} %multiply_convert_fusion.x_ref.b_ref.c_ref, bf16[768,2816]{1,0:T(8,128)(2,1)} %multiply_convert_fusion.x_ref.b_ref.c_ref, f32[5,768,8]{2,1,0:T(8,128)} %bitcast.56, ...), custom_call_target="tpu_custom_call" | custom-call | flops 2264924160 | bytes 12189696 | tf_op jit(solution)/shard_map/pallas_call | solution.py:169
  256.3 8.4 %collective-permute-done.6 = f32[20]{0:T(128)S(1)} collective-permute-done((f32[20]{0:T(128)S(1)}, f32[20]{0:T(128)S(1)}, u32[]{:S(2)}, u32[]{:S(2)}) %collective-permute-start.6) | collective-permute-done | bytes 112 | tf_op jit(solution)/shard_map/ppermute | solution.py:49
  264.8 0.8 copy-done.1
  265.6 1.6 select_bitcast_fusion
  267.2 0.2 fusion.4
  267.3 0.1 collective-permute-start.8
  267.6 0.1 mul.188
  267.7 1.8 collective-permute-done.8
  269.5 0.1 maximum_select_fusion
  269.6 2.8 multiply_add_fusion
  272.5 2.3 pad_maximum_fusion.1.enter_ref
  274.8 15.8 %shard_map.66 = bf16[768,2560]{1,0:T(8,128)(2,1)} custom-call(f32[768,2560]{1,0:T(8,128)} %shard_map.65.part_ref, bf16[768,2816]{1,0:T(8,128)(2,1)} %multiply_convert_fusion.x_ref.b_ref.c_ref, f32[5,768,8]{2,1,0:T(8,128)} %bitcast.57, f32[3,2560,128]{2,1,0:T(8,128)} %pad_maximum_fusion.1.enter_ref), custom_call_target="tpu_custom_call" | custom-call | flops 3019898880 | bytes 15728640 | tf_op jit(solution)/shard_map/pallas_call | solution.py:190
  (33 shorter events, 0.6 us)
Async XLA Ops:
  6.5 138.2 %all-gather.3.cloned.1.call-start = ((), (), s32[]{:S(2)}) async-start(), calls=%async_computation | async-start | bytes 21053440 | tf_op jit(solution)/shard_map/all_gather | solution.py:114
  169.8 20.7 %copy-start.2 = (bf16[4,2816]{1,0:T(4,128)(2,1)S(1)}, bf16[4,2816]{1,0:T(4,128)(2,1)}, u32[]{:S(2)}) copy-start(bf16[4,2816]{1,0:T(4,128)(2,1)} %param.9) | copy-start | bytes 67588
  186.3 2.0 copy-start
  188.2 6.5 %copy-start.3 = (f32[2816]{0:T(1024)S(1)}, f32[2816]{0:T(1024)}, u32[]{:S(2)}) copy-start(f32[2816]{0:T(1024)} %param.10) | copy-start | bytes 33796
  188.3 6.5 %collective-permute-start.1 = (bf16[3,2816]{1,0:T(4,128)(2,1)S(1)}, bf16[3,2816]{1,0:T(4,128)(2,1)S(1)}, u32[]{:S(2)}, u32[]{:S(2)}) collective-permute-start(bf16[3,2816]{1,0:T(4,128)(2,1)S(1)} %slice.78), channel_id=1, source_target_pairs={{0,1},{1,2},{2,3},{3,4},{4,5},{5,6},{6,7},{8,9},{9,10},{10,11},{11... | collective-permute-start | bytes 50696 | tf_op jit(solution)/shard_map/ppermute | solution.py:21
  226.9 2.4 copy-start.4
  227.3 2.9 collective-permute-start.2
  228.5 1.6 collective-permute-start
  231.2 33.5 %collective-permute-start.3 = (f32[20,64,128]{2,1,0:T(8,128)}, f32[20,64,128]{2,1,0:T(8,128)S(1)}, u32[]{:S(2)}, u32[]{:S(2)}) collective-permute-start(f32[20,64,128]{2,1,0:T(8,128)} %fusion.3), channel_id=1, source_target_pairs={{0,2},{2,4},{4,6},{1,3},{3,5},{5,7},{8,10},{10,12},{12,14},{9,11},... | collective-permute-start | bytes 1966088 | tf_op jit(solution)/shard_map/ppermute | solution.py:49
  233.7 31.1 %collective-permute-start.5 = (f32[20,64,128]{2,1,0:T(8,128)}, f32[20,64,128]{2,1,0:T(8,128)S(1)}, u32[]{:S(2)}, u32[]{:S(2)}) collective-permute-start(f32[20,64,128]{2,1,0:T(8,128)} %fusion.3), channel_id=1, source_target_pairs={{0,4},{2,6},{1,5},{3,7},{8,12},{10,14},{9,13},{11,15},{16,20},{18,... | collective-permute-start | bytes 1966088 | tf_op jit(solution)/shard_map/ppermute | solution.py:49
  235.0 29.8 %collective-permute-start.7 = (f32[20,64,128]{2,1,0:T(8,128)}, f32[20,64,128]{2,1,0:T(8,128)}, u32[]{:S(2)}, u32[]{:S(2)}) collective-permute-start(f32[20,64,128]{2,1,0:T(8,128)} %fusion.3), channel_id=1, source_target_pairs={{0,6},{1,7},{8,14},{9,15},{16,22},{17,23},{24,30},{25,31},{32,38},... | collective-permute-start | bytes 1966088 | tf_op jit(solution)/shard_map/ppermute | solution.py:49
  236.5 19.8 %collective-permute-start.4 = (f32[20]{0:T(128)S(1)}, f32[20]{0:T(128)S(1)}, u32[]{:S(2)}, u32[]{:S(2)}) collective-permute-start(f32[20]{0:T(128)S(1)} %get-tuple-element.19), channel_id=1, source_target_pairs={{0,2},{2,4},{4,6},{1,3},{3,5},{5,7},{8,10},{10,12},{12,14},{9,11},... | collective-permute-start | bytes 248 | tf_op jit(solution)/shard_map/ppermute | solution.py:49
  238.5 26.3 %collective-permute-start.6 = (f32[20]{0:T(128)S(1)}, f32[20]{0:T(128)S(1)}, u32[]{:S(2)}, u32[]{:S(2)}) collective-permute-start(f32[20]{0:T(128)S(1)} %get-tuple-element.19), channel_id=1, source_target_pairs={{0,4},{2,6},{1,5},{3,7},{8,12},{10,14},{9,13},{11,15},{16,20},{18,... | collective-permute-start | bytes 248 | tf_op jit(solution)/shard_map/ppermute | solution.py:49
  264.8 0.8 copy-start.1
  267.3 2.2 collective-permute-start.8
Sparse Core Ops, SparseCore 0:
  10.9 133.7 all-gather.2

commit v8 on v7

--- a/solution.py
+++ b/solution.py
@@ -28,9 +28,9 @@
 def scan_entering(total, state, side, side_inputs):
     core = lax.axis_index("core")
     half = HALF_HEADS // 2
-    halves = state.reshape(2, half, HEAD_DIM, STATE)
-    mine = lax.dynamic_index_in_dim(halves, core, 0, False)
-    sent = swapped(lax.dynamic_index_in_dim(halves, 1 - core, 0, False))
+    halves = state.reshape(STATE, 2, half, HEAD_DIM)
+    mine = lax.dynamic_index_in_dim(halves, core, 1, False)
+    sent = swapped(lax.dynamic_index_in_dim(halves, 1 - core, 1, False))
     totals = total.reshape(2, half)
     my_total = lax.dynamic_index_in_dim(totals, core, 0, False)
     peer_total = swapped(lax.dynamic_index_in_dim(totals, 1 - core, 0, False))
@@ -39,7 +39,7 @@
     late_state = jnp.where(first, sent, mine)
     early_total = jnp.where(first, my_total, peer_total)
     late_total = jnp.where(first, peer_total, my_total)
-    chip_state = jnp.exp(late_total)[:, None, None] * early_state + late_state
+    chip_state = jnp.exp(late_total)[None, :, None] * early_state + late_state
     chip_total = early_total + late_total
     chips = lax.axis_size("y")
     chip_state, chip_total, side_inputs = lax.optimization_barrier((chip_state, chip_total, side_inputs))
@@ -52,12 +52,13 @@
     held = jnp.zeros_like(chip_state)
     gap = jnp.zeros_like(chip_total)
     for got_state, got_total in got:
-        held = held + jnp.exp(gap)[:, None, None] * got_state
+        held = held + jnp.exp(gap)[None, :, None] * got_state
         gap = gap + got_total
-    later = jnp.exp(early_total)[:, None, None] * held + early_state
+    later = jnp.exp(early_total)[None, :, None] * held + early_state
     mine_in = jnp.where(first, held, later)
     other_in = swapped(jnp.where(first, later, held))
-    return jnp.where(first, jnp.concatenate([mine_in, other_in]), jnp.concatenate([other_in, mine_in])), side_out
+    joined = jnp.where(first, jnp.concatenate([mine_in, other_in], 1), jnp.concatenate([other_in, mine_in], 1))
+    return joined, side_out
 
 
 def pair_lanes(columns, pair):
@@ -65,16 +66,14 @@
     return jnp.where(lane < HEAD_DIM, columns[:, 2 * pair : 2 * pair + 1], columns[:, 2 * pair + 1 : 2 * pair + 2])
 
 
-def states_kernel(x_ref, b_ref, cum_ref, step_ref, out_ref):
+def states_kernel(x_ref, bt_ref, cum_ref, step_ref, out_ref):
     cum = cum_ref[0]
     weight = jnp.exp(cum[SPAN - 1 : SPAN, :] - cum) * step_ref[0]
-    b_span = b_ref[...]
+    b_flipped = bt_ref[...]
     for pair in range(GROUP // 2):
         lanes = slice(2 * HEAD_DIM * pair, 2 * HEAD_DIM * (pair + 1))
         decayed = (x_ref[:, lanes].astype(jnp.float32) * pair_lanes(weight, pair)).astype(jnp.bfloat16)
-        out_ref[0, lanes, :] = lax.dot_general(
-            decayed, b_span, (((0,), (0,)), ((), ())), preferred_element_type=jnp.float32
-        )
+        out_ref[0, :, lanes] = jnp.dot(b_flipped, decayed, preferred_element_type=jnp.float32)
 
 
 def intra_kernel(x_ref, b_ref, c_ref, cum_ref, cum_row_ref, step_row_ref, gain_ref, part_ref):
@@ -101,9 +100,8 @@
     c32 = c_ref[...].astype(jnp.float32)
     for pair in range(GROUP // 2):
         lanes = slice(2 * HEAD_DIM * pair, 2 * HEAD_DIM * (pair + 1))
-        readout = lax.dot_general(
-            c32, enter_ref[0, lanes, :], (((1,), (1,)), ((), ())),
-            precision=lax.Precision.HIGHEST, preferred_element_type=jnp.float32,
+        readout = jnp.dot(
+            c32, enter_ref[0, :, lanes], precision=lax.Precision.HIGHEST, preferred_element_type=jnp.float32
         )
         out_ref[:, lanes] = (part_ref[:, lanes] + pair_lanes(rise, pair) * readout).astype(jnp.bfloat16)
 
@@ -146,25 +144,27 @@
     c_spec = pl.BlockSpec((SPAN, STATE), lambda c, g: (c, INNER // STATE + 1))
     col_spec = pl.BlockSpec((1, SPAN, GROUP), lambda c, g: (g, c, 0))
     row_spec = pl.BlockSpec((GROUP, SPAN), lambda c, g: (g, c))
-    state_spec = pl.BlockSpec((1, GROUP * HEAD_DIM, STATE), lambda c, g: (c, g, 0))
+    state_spec = pl.BlockSpec((1, STATE, GROUP * HEAD_DIM), lambda c, g: (c, 0, g))
+    bt_spec = pl.BlockSpec((STATE, SPAN), lambda c, g: (0, c))
+    b_flipped = active[:, INNER : INNER + STATE].T
     gain = jnp.repeat(skip_gain, HEAD_DIM)[None, :]
     gain_spec = pl.BlockSpec((1, GROUP * HEAD_DIM), lambda c, g: (0, g))
     states = pl.pallas_call(
         states_kernel,
         grid=(span_count, groups),
-        in_specs=[x_spec, b_spec, col_spec, col_spec],
+        in_specs=[x_spec, bt_spec, col_spec, col_spec],
         out_specs=state_spec,
-        out_shape=jax.ShapeDtypeStruct((span_count, INNER, STATE), jnp.float32),
+        out_shape=jax.ShapeDtypeStruct((span_count, STATE, INNER), jnp.float32),
         cost_estimate=pl.CostEstimate(
             flops=2 * length * INNER * STATE, transcendentals=length * HALF_HEADS,
             bytes_accessed=2 * length * (INNER + STATE) + 4 * span_count * INNER * STATE,
         ),
-    )(active, active, cum_grouped, step_grouped)
-    states = states.reshape(span_count, HALF_HEADS, HEAD_DIM, STATE)
-
-    local = jnp.zeros((HALF_HEADS, HEAD_DIM, STATE), jnp.float32)
+    )(active, b_flipped, cum_grouped, step_grouped)
+    states = states.reshape(span_count, STATE, HALF_HEADS, HEAD_DIM)
+
+    local = jnp.zeros((STATE, HALF_HEADS, HEAD_DIM), jnp.float32)
     for span in range(span_count):
-        local = jnp.exp(totals[span])[:, None, None] * local + states[span]
+        local = jnp.exp(totals[span])[None, :, None] * local + states[span]
     def intra(active, cum_grouped, cum_row, step_row, gain):
         return pl.pallas_call(
             intra_kernel,
@@ -184,8 +184,8 @@
     entering = []
     for span in range(span_count):
         entering.append(held)
-        held = jnp.exp(totals[span])[:, None, None] * held + states[span]
-    entering = jnp.stack(entering).reshape(span_count, INNER, STATE)
+        held = jnp.exp(totals[span])[None, :, None] * held + states[span]
+    entering = jnp.stack(entering).reshape(span_count, STATE, INNER)
 
     out = pl.pallas_call(
         readout_kernel,

time: 301 us -> 309 us (1.027)
  local copies, waits for them, and re-layouts: 37.4 us -> 48.5 us
    slice x3 -> x6, local copies, waits for them, and re-layouts: 2.55 us -> 10.1 us  [the longest x4 9.94 us: body(): local = jnp.exp(totals[span])[None, :, None] * local + states[span]]
    convert_element_type x1, other arithmetic: 13.9 us -> 10.6 us  [body(): active = jax.nn.silu(filtered).astype(jnp.bfloat16)]
    unnamed x11 -> x15, local copies, waits for them, and re-layouts: 27.8 us -> 30.1 us
  transfers between devices with their start and end apart: 10 -> 10, of which waited for: 4 -> 4; matrix products, arithmetic and copies ran while one was open for 4% -> 4% of each run, Pallas kernels for 6% -> 5%
where the time goes in v8:
time: 309 us; the launch traced here: 306 us
  waiting for transfers between devices  144 us (47%)
  local copies, waits for them, and re-layouts  48.5 us (16%)
  Pallas kernels  46.8 us (15%)
  other arithmetic  24.7 us (8%)
  matrix products  16.5 us (5%)
  between operations  13.7 us (4%)
  starting transfers between devices  11.9 us (4%)
    all_gather x1, waiting for transfers between devices, project(): lax.all_gather(input_weight, ('dp',) + SEQ, axis=0, tiled=True)  132 us
    unnamed x15, local copies, waits for them, and re-layouts  30.1 us
    pallas_call x1, Pallas kernels, intra(): pl.pallas_call(intra_kernel, grid=(span_count, groups), in_specs=[x_spec,...  16.6 us
    dot_general x1, matrix products, project(): lax.dot_general(token_rows, lax.all_gather(input_weight, ('dp',) + SEQ, a...  16.5 us
    pallas_call x1, Pallas kernels, body(): pl.pallas_call(readout_kernel, grid=(span_count, groups), in_specs=[x_spe...  15.7 us
    pallas_call x1, Pallas kernels, body(): pl.pallas_call(states_kernel, grid=(span_count, groups), in_specs=[x_spec...  14.6 us
    convert_element_type x1, other arithmetic, body(): active = jax.nn.silu(filtered).astype(jnp.bfloat16)  10.6 us
    slice x4, local copies, waits for them, and re-layouts, body(): local = jnp.exp(totals[span])[None, :, None] * local + states[span]  9.94 us
  transfers between devices with their start and end apart: 10, of which 4 were waited for; matrix products, arithmetic and copies ran while one was open for 4% of the time, Pallas kernels for 5%

profile of v8, /device:TPU:16, one launch (start us, length us, event | category | flops | bytes accessed | tf_op | source)
XLA Modules:
  0.0 305.8 jit_solution(3426384658403978282)
XLA Ops:
  6.5 0.7 all-gather.3.cloned.1.call-update
  7.3 1.0 reshape.144
  8.2 1.8 reduce-window.6
  10.0 0.1 slice.79
  10.1 0.1 copy.40
  10.3 0.1 copy_bitcast_fusion
  10.4 0.2 slice_reduce_fusion.1
  10.6 1.6 negate_bitcast_fusion
  12.2 0.1 broadcast_add_fusion
  12.3 132.4 %all-gather.3.cloned.1.call-done = bf16[256,11,2560]{2,1,0:T(8,128)(2,1)} async-done(((bf16[1,11,2560]{2,1,0:T(8,128)(2,1)}), bf16[256,11,2560]{2,1,0:T(8,128)(2,1)}) %all-gather.3.cloned.1.call-update) | async-done | bytes 14417936 | tf_op jit(solution)/shard_map/all_gather | solution.py:112
  144.7 25.0 %reshape.152 = bf16[2816,2560]{1,0:T(8,128)(2,1)} reshape(bf16[256,11,2560]{2,1,0:T(8,128)(2,1)} %all-gather.3.cloned.1.call-done) | data formatting | bytes 28835840
  169.8 16.5 %convolution_convert_fusion = bf16[768,2816]{1,0:T(8,128)(2,1)S(1)} fusion(bf16[2816,2560]{1,0:T(8,128)(2,1)} %reshape.152, bf16[1,768,2560]{2,1,0:T(8,128)(2,1)} %param.6), kind=kOutput, calls=%fused_computation.3 | convolution fusion | flops 11075125248 | bytes 22675456 | tf_op jit(solution)/shard_map/dot_general | solution.py:110
  186.3 2.0 copy-done.1
  188.3 2.2 collective-permute-start.1
  190.4 0.1 convert_reduce_fusion.3
  190.6 0.1 reduce_window_sum.25
  190.8 1.8 copy.44
  192.6 1.9 copy.45
  194.7 10.6 %multiply_convert_fusion.x_ref.b_ref.c_ref = bf16[768,2816]{1,0:T(8,128)(2,1)S(1)} fusion(bf16[768,2816]{1,0:T(8,128)(2,1)} %copy-done.1, bf16[3,2816]{1,0:T(4,128)(2,1)S(1)} %collective-permute-done.1, f32[2816]{0:T(1024)S(1)} %get-tuple-element.35, f32[2816]{0:T(1024)S(1)} %get-tuple-element.36, f32[2816]{0:T(1024)S(1)} %get-tuple-element.34, ...), kind=kLoop, calls=%fused_computation | loop fusion | flops 56229888 | bytes 8723968 | tf_op jit(solution)/shard_map/convert_element_type | solution.py:133
  205.4 2.0 copy-done
  207.4 0.8 copy.46.bt_ref
  208.2 14.6 %shard_map.64 = f32[3,128,2560]{2,1,0:T(8,128)} custom-call(bf16[768,2816]{1,0:T(8,128)(2,1)} %copy-done, bf16[128,768]{1,0:T(8,128)(2,1)} %copy.46.bt_ref, f32[5,768,8]{2,1,0:T(8,128)} %bitcast.55, f32[5,768,8]{2,1,0:T(8,128)} %bitcast.58), custom_call_target="tpu_custom_call" | custom-call | flops 503316480 | bytes 8060928 | tf_op jit(solution)/shard_map/pallas_call | solution.py:152
  222.8 3.9 %fusion.12 = (f32[1,128,2560]{2,1,0:T(8,128)S(1)}, f32[1,128,2560]{2,1,0:T(8,128)}, f32[1,128,2560]{2,1,0:T(8,128)}) fusion(f32[3,128,2560]{2,1,0:T(8,128)} %shard_map.64), kind=kLoop, calls=%fused_computation.48 | loop fusion | bytes 7864320 | tf_op jit(solution)/shard_map/slice | solution.py:167
  226.7 1.7 copy.49
  228.4 2.8 copy.48
  231.2 1.5 copy.47
  232.8 2.0 multiply_add_fusion.2
  234.9 1.1 collective-permute-start.2
  236.2 0.7 reduce_window_sum.26.cum_row_ref
  237.0 0.7 broadcast_in_dim_reshape.3.gain_ref
  237.8 1.0 fusion.3
  238.8 2.4 collective-permute-start.3
  241.3 1.3 collective-permute-start.5
  242.6 1.6 collective-permute-start.7
  244.1 1.9 collective-permute-start.4
  246.1 1.3 collective-permute-start.6
  247.4 16.6 %shard_map.65.part_ref = f32[768,2560]{1,0:T(8,128)} custom-call(bf16[768,2816]{1,0:T(8,128)(2,1)} %copy-done, bf16[768,2816]{1,0:T(8,128)(2,1)} %copy-done, bf16[768,2816]{1,0:T(8,128)(2,1)} %copy-done, f32[5,768,8]{2,1,0:T(8,128)} %bitcast.56, f32[40,768]{1,0:T(8,128)} %reduce_window_sum.26.cum_row_ref, f32[40,768]{1,0:T(8,128)} %get-tuple-element.23.step_row_ref, ...), custom_call_target="tpu_custom_call" | custom-call | flops 2264924160 | bytes 12189696 | tf_op jit(solution)/shard_map/pallas_call | solution.py:169
  263.9 8.4 %collective-permute-done.6 = f32[20]{0:T(128)S(1)} collective-permute-done((f32[20]{0:T(128)S(1)}, f32[20]{0:T(128)S(1)}, u32[]{:S(2)}, u32[]{:S(2)}) %collective-permute-start.6) | collective-permute-done | bytes 112 | tf_op jit(solution)/shard_map/ppermute | solution.py:49
  272.4 0.8 copy-done.2
  273.2 0.2 copy-done.3
  273.4 1.7 select_bitcast_fusion
  275.2 1.0 fusion.4
  276.5 2.0 collective-permute-done.8
  278.5 0.2 maximum_select_fusion
  278.7 0.4 copy.52
  279.1 2.0 multiply_add_fusion
  281.1 2.2 pad_maximum_fusion.1.enter_ref
  283.3 15.7 %shard_map.66 = bf16[768,2560]{1,0:T(8,128)(2,1)} custom-call(f32[768,2560]{1,0:T(8,128)} %shard_map.65.part_ref, bf16[768,2816]{1,0:T(8,128)(2,1)} %copy-done, f32[5,768,8]{2,1,0:T(8,128)} %bitcast.57, f32[3,128,2560]{2,1,0:T(8,128)} %pad_maximum_fusion.1.enter_ref), custom_call_target="tpu_custom_call" | custom-call | flops 3019898880 | bytes 15728640 | tf_op jit(solution)/shard_map/pallas_call | solution.py:190
  (43 shorter events, 1.1 us)
Async XLA Ops:
  6.5 138.2 %all-gather.3.cloned.1.call-start = ((), (), s32[]{:S(2)}) async-start(), calls=%async_computation | async-start | bytes 21053440 | tf_op jit(solution)/shard_map/all_gather | solution.py:112
  169.8 20.7 %copy-start.4 = (bf16[4,2816]{1,0:T(4,128)(2,1)S(1)}, bf16[4,2816]{1,0:T(4,128)(2,1)}, u32[]{:S(2)}) copy-start(bf16[4,2816]{1,0:T(4,128)(2,1)} %param.9) | copy-start | bytes 67588
  186.3 2.0 copy-start.1
  188.2 6.5 %copy-start.5 = (f32[2816]{0:T(1024)S(1)}, f32[2816]{0:T(1024)}, u32[]{:S(2)}) copy-start(f32[2816]{0:T(1024)} %param.10) | copy-start | bytes 33796
  188.3 6.5 %collective-permute-start.1 = (bf16[3,2816]{1,0:T(4,128)(2,1)S(1)}, bf16[3,2816]{1,0:T(4,128)(2,1)S(1)}, u32[]{:S(2)}, u32[]{:S(2)}) collective-permute-start(bf16[3,2816]{1,0:T(4,128)(2,1)S(1)} %slice.82), channel_id=1, source_target_pairs={{0,1},{1,2},{2,3},{3,4},{4,5},{5,6},{6,7},{8,9},{9,10},{10,11},{11... | collective-permute-start | bytes 50696 | tf_op jit(solution)/shard_map/ppermute | solution.py:21
  205.3 2.1 copy-start
  232.8 4.2 %copy-start.6 = (f32[40]{0:T(128)S(1)}, f32[40]{0:T(128)}, u32[]{:S(2)}) copy-start(f32[40]{0:T(128)} %param.11) | copy-start | bytes 484
  234.9 2.9 collective-permute-start.2
  236.1 1.6 collective-permute-start
  238.8 33.5 %collective-permute-start.3 = (f32[128,20,64]{0,2,1:T(8,128)}, f32[128,20,64]{0,2,1:T(8,128)S(1)}, u32[]{:S(2)}, u32[]{:S(2)}) collective-permute-start(f32[128,20,64]{0,2,1:T(8,128)} %fusion.3), channel_id=1, source_target_pairs={{0,2},{2,4},{4,6},{1,3},{3,5},{5,7},{8,10},{10,12},{12,14},{9,11},... | collective-permute-start | bytes 1966088 | tf_op jit(solution)/shard_map/ppermute | solution.py:49
  241.3 31.1 %collective-permute-start.5 = (f32[128,20,64]{0,2,1:T(8,128)}, f32[128,20,64]{0,2,1:T(8,128)S(1)}, u32[]{:S(2)}, u32[]{:S(2)}) collective-permute-start(f32[128,20,64]{0,2,1:T(8,128)} %fusion.3), channel_id=1, source_target_pairs={{0,4},{2,6},{1,5},{3,7},{8,12},{10,14},{9,13},{11,15},{16,20},{18,... | collective-permute-start | bytes 1966088 | tf_op jit(solution)/shard_map/ppermute | solution.py:49
  242.6 29.8 %collective-permute-start.7 = (f32[128,20,64]{0,2,1:T(8,128)}, f32[128,20,64]{0,2,1:T(8,128)}, u32[]{:S(2)}, u32[]{:S(2)}) collective-permute-start(f32[128,20,64]{0,2,1:T(8,128)} %fusion.3), channel_id=1, source_target_pairs={{0,6},{1,7},{8,14},{9,15},{16,22},{17,23},{24,30},{25,31},{32,38},... | collective-permute-start | bytes 1966088 | tf_op jit(solution)/shard_map/ppermute | solution.py:49
  244.1 19.8 %collective-permute-start.4 = (f32[20]{0:T(128)S(1)}, f32[20]{0:T(128)S(1)}, u32[]{:S(2)}, u32[]{:S(2)}) collective-permute-start(f32[20]{0:T(128)S(1)} %get-tuple-element.19), channel_id=1, source_target_pairs={{0,2},{2,4},{4,6},{1,3},{3,5},{5,7},{8,10},{10,12},{12,14},{9,11},... | collective-permute-start | bytes 248 | tf_op jit(solution)/shard_map/ppermute | solution.py:49
  246.1 26.3 %collective-permute-start.6 = (f32[20]{0:T(128)S(1)}, f32[20]{0:T(128)S(1)}, u32[]{:S(2)}, u32[]{:S(2)}) collective-permute-start(f32[20]{0:T(128)S(1)} %get-tuple-element.19), channel_id=1, source_target_pairs={{0,4},{2,6},{1,5},{3,7},{8,12},{10,14},{9,13},{11,15},{16,20},{18,... | collective-permute-start | bytes 248 | tf_op jit(solution)/shard_map/ppermute | solution.py:49
  272.4 0.8 copy-start.2
  272.4 1.1 copy-start.3
  276.2 2.3 collective-permute-start.8
Sparse Core Ops, SparseCore 0:
  10.9 133.7 all-gather.2

commit v9 on v7

--- a/solution.py
+++ b/solution.py
@@ -25,15 +25,25 @@
     return lax.ppermute(array, "core", [(0, 1), (1, 0)])
 
 
+def with_total(state, total):
+    row = jnp.broadcast_to(total[:, None, None], (state.shape[0], 1, state.shape[2]))
+    return jnp.concatenate([state, row], axis=1)
+
+
 def scan_entering(total, state, side, side_inputs):
     core = lax.axis_index("core")
     half = HALF_HEADS // 2
     halves = state.reshape(2, half, HEAD_DIM, STATE)
+    totals = total.reshape(2, half)
     mine = lax.dynamic_index_in_dim(halves, core, 0, False)
-    sent = swapped(lax.dynamic_index_in_dim(halves, 1 - core, 0, False))
-    totals = total.reshape(2, half)
     my_total = lax.dynamic_index_in_dim(totals, core, 0, False)
-    peer_total = swapped(lax.dynamic_index_in_dim(totals, 1 - core, 0, False))
+    packed = swapped(
+        with_total(
+            lax.dynamic_index_in_dim(halves, 1 - core, 0, False),
+            lax.dynamic_index_in_dim(totals, 1 - core, 0, False),
+        )
+    )
+    sent, peer_total = packed[:, :HEAD_DIM], packed[:, HEAD_DIM, 0]
     first = core == 0
     early_state = jnp.where(first, mine, sent)
     late_state = jnp.where(first, sent, mine)
@@ -42,22 +52,23 @@
     chip_state = jnp.exp(late_total)[:, None, None] * early_state + late_state
     chip_total = early_total + late_total
     chips = lax.axis_size("y")
-    chip_state, chip_total, side_inputs = lax.optimization_barrier((chip_state, chip_total, side_inputs))
+    chip_packed, side_inputs = lax.optimization_barrier((with_total(chip_state, chip_total), side_inputs))
     got = []
     for by in range(1, chips):
         pairs = [(i, i + by) for i in range(chips) if i + by < chips]
-        got.append((lax.ppermute(chip_state, "y", pairs), lax.ppermute(chip_total, "y", pairs)))
+        got.append(lax.ppermute(chip_packed, "y", pairs))
     side_out = side(*side_inputs)
     got, side_out = lax.optimization_barrier((got, side_out))
     held = jnp.zeros_like(chip_state)
     gap = jnp.zeros_like(chip_total)
-    for got_state, got_total in got:
-        held = held + jnp.exp(gap)[:, None, None] * got_state
-        gap = gap + got_total
+    for got_packed in got:
+        held = held + jnp.exp(gap)[:, None, None] * got_packed[:, :HEAD_DIM]
+        gap = gap + got_packed[:, HEAD_DIM, 0]
     later = jnp.exp(early_total)[:, None, None] * held + early_state
     mine_in = jnp.where(first, held, later)
     other_in = swapped(jnp.where(first, later, held))
-    return jnp.where(first, jnp.concatenate([mine_in, other_in]), jnp.concatenate([other_in, mine_in])), side_out
+    joined = jnp.where(first, jnp.concatenate([mine_in, other_in]), jnp.concatenate([other_in, mine_in]))
+    return joined, side_out
 
 
 def pair_lanes(columns, pair):

time: 301 us -> 306 us (1.017)
  waiting for transfers between devices: 143 us -> 152 us
  starting transfers between devices: 12 us -> 8.43 us
    ppermute x5 -> x3, waiting for transfers between devices: 8.46 us -> 18 us  [scan_entering(): got.append(lax.ppermute(chip_packed, 'y', pairs))]
    ppermute x5 -> x3, starting transfers between devices: 8.51 us -> 5.02 us  [scan_entering(): got.append(lax.ppermute(chip_packed, 'y', pairs))]
    unnamed x11 -> x8, local copies, waits for them, and re-layouts: 27.8 us -> 27.1 us
  transfers between devices with their start and end apart: 10 -> 7, of which waited for: 4 -> 5; matrix products, arithmetic and copies ran while one was open for 4% -> 4% of each run, Pallas kernels for 6% -> 5%
where the time goes in v9:
time: 306 us; the launch traced here: 303 us
  waiting for transfers between devices  152 us (50%)
  Pallas kernels  48.2 us (16%)
  local copies, waits for them, and re-layouts  36.9 us (12%)
  other arithmetic  27.3 us (9%)
  matrix products  16.5 us (5%)
  between operations  13.6 us (4%)
  starting transfers between devices  8.43 us (3%)
    all_gather x1, waiting for transfers between devices, project(): lax.all_gather(input_weight, ('dp',) + SEQ, axis=0, tiled=True)  131 us
    unnamed x8, local copies, waits for them, and re-layouts  27.1 us
    ppermute x3, waiting for transfers between devices, scan_entering(): got.append(lax.ppermute(chip_packed, 'y', pairs))  18 us
    pallas_call x1, Pallas kernels, intra(): pl.pallas_call(intra_kernel, grid=(span_count, groups), in_specs=[x_spec,...  16.6 us
    dot_general x1, matrix products, project(): lax.dot_general(token_rows, lax.all_gather(input_weight, ('dp',) + SEQ, a...  16.5 us
    pallas_call x1, Pallas kernels, body(): pl.pallas_call(states_kernel, grid=(span_count, groups), in_specs=[x_spec...  15.9 us
    pallas_call x1, Pallas kernels, body(): pl.pallas_call(readout_kernel, grid=(span_count, groups), in_specs=[x_spe...  15.8 us
    convert_element_type x1, other arithmetic, body(): active = jax.nn.silu(filtered).astype(jnp.bfloat16)  13.9 us
  transfers between devices with their start and end apart: 7, of which 5 were waited for; matrix products, arithmetic and copies ran while one was open for 4% of the time, Pallas kernels for 5%

profile of v9, /device:TPU:16, one launch (start us, length us, event | category | flops | bytes accessed | tf_op | source)
XLA Modules:
  0.0 303.1 jit_solution(2940741442105441443)
XLA Ops:
  6.5 0.7 all-gather.3.cloned.1.call-update
  7.3 1.0 reshape.152
  8.2 1.8 reduce-window.6
  10.0 0.1 slice.103
  10.1 0.1 copy.45
  10.3 0.1 copy_bitcast_fusion
  10.4 0.2 slice_reduce_fusion.1
  10.6 0.1 reshape.154
  10.7 1.0 convert_reduce_fusion.3
  11.7 1.6 negate_bitcast_fusion
  13.3 0.1 broadcast_add_fusion
  13.4 131.3 %all-gather.3.cloned.1.call-done = bf16[256,11,2560]{2,1,0:T(8,128)(2,1)} async-done(((bf16[1,11,2560]{2,1,0:T(8,128)(2,1)}), bf16[256,11,2560]{2,1,0:T(8,128)(2,1)}) %all-gather.3.cloned.1.call-update) | async-done | bytes 14417936 | tf_op jit(solution)/shard_map/all_gather | solution.py:125
  144.7 25.0 %reshape.160 = bf16[2816,2560]{1,0:T(8,128)(2,1)} reshape(bf16[256,11,2560]{2,1,0:T(8,128)(2,1)} %all-gather.3.cloned.1.call-done) | data formatting | bytes 28835840
  169.8 16.5 %convolution_convert_fusion = bf16[768,2816]{1,0:T(8,128)(2,1)S(1)} fusion(bf16[2816,2560]{1,0:T(8,128)(2,1)} %reshape.160, bf16[1,768,2560]{2,1,0:T(8,128)(2,1)} %param.6), kind=kOutput, calls=%fused_computation.3 | convolution fusion | flops 11075125248 | bytes 22675456 | tf_op jit(solution)/shard_map/dot_general | solution.py:123
  186.3 2.0 copy-done
  188.2 2.2 collective-permute-start
  190.5 0.1 exp.61
  190.6 0.1 mul.166
  190.7 0.1 exp.59
  190.8 0.1 reduce_window_sum.25
  190.9 1.8 copy.49
  192.7 1.9 copy.50
  194.6 13.9 %multiply_convert_fusion.x_ref.b_ref.c_ref = bf16[768,2816]{1,0:T(8,128)(2,1)} fusion(bf16[768,2816]{1,0:T(8,128)(2,1)} %copy-done, bf16[3,2816]{1,0:T(4,128)(2,1)S(1)} %collective-permute-done, f32[2816]{0:T(1024)S(1)} %get-tuple-element.31, f32[2816]{0:T(1024)S(1)} %get-tuple-element.32, f32[2816]{0:T(1024)S(1)} %get-tuple-element.30, ...), kind=kLoop, calls=%fused_computation | loop fusion | flops 56229888 | bytes 8723968 | tf_op jit(solution)/shard_map/convert_element_type | solution.py:146
  208.5 15.9 %shard_map.64 = f32[3,2560,128]{2,1,0:T(8,128)} custom-call(bf16[768,2816]{1,0:T(8,128)(2,1)} %multiply_convert_fusion.x_ref.b_ref.c_ref, bf16[768,2816]{1,0:T(8,128)(2,1)} %multiply_convert_fusion.x_ref.b_ref.c_ref, f32[5,768,8]{2,1,0:T(8,128)} %bitcast.61, f32[5,768,8]{2,1,0:T(8,128)} %bitcast.65), custom_call_target="tpu_custom_call" | custom-call | flops 503316480 | bytes 8060928 | tf_op jit(solution)/shard_map/pallas_call | solution.py:163
  224.4 2.4 fusion.10
  226.8 0.3 multiply_add_fusion.2
  227.2 0.1 broadcast_in_dim.19
  227.3 1.1 collective-permute-start.1
  228.5 0.7 reduce_window_sum.26.cum_row_ref
  229.3 0.7 broadcast_in_dim_reshape.3.gain_ref
  230.0 0.3 collective-permute-done.1
  230.3 0.1 copy.53
  230.5 0.1 fusion.3
  230.8 1.6 collective-permute-start.4
  232.3 1.3 collective-permute-start.3
  233.6 2.2 collective-permute-start.2
  235.8 16.6 %shard_map.65.part_ref = f32[768,2560]{1,0:T(8,128)} custom-call(bf16[768,2816]{1,0:T(8,128)(2,1)} %multiply_convert_fusion.x_ref.b_ref.c_ref, bf16[768,2816]{1,0:T(8,128)(2,1)} %multiply_convert_fusion.x_ref.b_ref.c_ref, bf16[768,2816]{1,0:T(8,128)(2,1)} %multiply_convert_fusion.x_ref.b_ref.c_ref, f32[5,768,8]{2,1,0:T(8,128)} %bitcast.62, ...), custom_call_target="tpu_custom_call" | custom-call | flops 2264924160 | bytes 12189696 | tf_op jit(solution)/shard_map/pallas_call | solution.py:180
  252.4 2.7 collective-permute-done.3
  255.1 15.3 %collective-permute-done.2 = f32[20,65,128]{2,1,0:T(8,128)} collective-permute-done((f32[20,65,128]{2,1,0:T(8,128)S(1)}, f32[20,65,128]{2,1,0:T(8,128)}, u32[]{:S(2)}, u32[]{:S(2)}) %collective-permute-start.2) | collective-permute-done | bytes 665632 | tf_op jit(solution)/shard_map/ppermute | solution.py:59
  270.3 1.1 exponential_reduce_fusion.1
  271.4 1.6 select_bitcast_fusion
  273.0 0.2 fusion.4
  273.2 0.1 collective-permute-start.5
  273.6 1.8 collective-permute-done.5
  275.4 0.1 maximum_select_fusion
  275.5 2.8 multiply_add_fusion
  278.3 2.2 pad_maximum_fusion.1.enter_ref
  280.5 15.8 %shard_map.66 = bf16[768,2560]{1,0:T(8,128)(2,1)} custom-call(f32[768,2560]{1,0:T(8,128)} %shard_map.65.part_ref, bf16[768,2816]{1,0:T(8,128)(2,1)} %multiply_convert_fusion.x_ref.b_ref.c_ref, f32[5,768,8]{2,1,0:T(8,128)} %bitcast.63, f32[3,2560,128]{2,1,0:T(8,128)} %pad_maximum_fusion.1.enter_ref), custom_call_target="tpu_custom_call" | custom-call | flops 3019898880 | bytes 15728640 | tf_op jit(solution)/shard_map/pallas_call | solution.py:201
  (28 shorter events, 0.8 us)
Async XLA Ops:
  6.5 138.2 %all-gather.3.cloned.1.call-start = ((), (), s32[]{:S(2)}) async-start(), calls=%async_computation | async-start | bytes 21053440 | tf_op jit(solution)/shard_map/all_gather | solution.py:125
  186.2 2.0 copy-start
  188.2 6.3 %copy-start.1 = (f32[2816]{0:T(1024)S(1)}, f32[2816]{0:T(1024)}, u32[]{:S(2)}) copy-start(f32[2816]{0:T(1024)} %param.10) | copy-start | bytes 33796
  188.2 6.3 %collective-permute-start = (bf16[3,2816]{1,0:T(4,128)(2,1)S(1)}, bf16[3,2816]{1,0:T(4,128)(2,1)S(1)}, u32[]{:S(2)}, u32[]{:S(2)}) collective-permute-start(bf16[3,2816]{1,0:T(4,128)(2,1)S(1)} %slice.106), channel_id=1, source_target_pairs={{0,1},{1,2},{2,3},{3,4},{4,5},{5,6},{6,7},{8,9},{9,10},{10,11},{11... | collective-permute-start | bytes 50696 | tf_op jit(solution)/shard_map/ppermute | solution.py:21
  226.8 2.5 copy-start.2
  227.3 3.0 collective-permute-start.1
  230.8 21.6 %collective-permute-start.4 = (f32[20,65,128]{2,1,0:T(8,128)S(1)}, f32[20,65,128]{2,1,0:T(8,128)}, u32[]{:S(2)}, u32[]{:S(2)}) collective-permute-start(f32[20,65,128]{2,1,0:T(8,128)S(1)} %pad_maximum_fusion.3), channel_id=1, source_target_pairs={{0,6},{1,7},{8,14},{9,15},{16,22},{17,23},{24,30},{25,31},{32,38},... | collective-permute-start | bytes 1996808 | tf_op jit(solution)/shard_map/ppermute | solution.py:59
  232.3 22.8 %collective-permute-start.3 = (f32[20,65,128]{2,1,0:T(8,128)S(1)}, f32[20,65,128]{2,1,0:T(8,128)S(1)}, u32[]{:S(2)}, u32[]{:S(2)}) collective-permute-start(f32[20,65,128]{2,1,0:T(8,128)S(1)} %pad_maximum_fusion.3), channel_id=1, source_target_pairs={{0,4},{2,6},{1,5},{3,7},{8,12},{10,14},{9,13},{11,15},{16,20},{18,... | collective-permute-start | bytes 1996808 | tf_op jit(solution)/shard_map/ppermute | solution.py:59
  233.6 36.7 %collective-permute-start.2 = (f32[20,65,128]{2,1,0:T(8,128)S(1)}, f32[20,65,128]{2,1,0:T(8,128)}, u32[]{:S(2)}, u32[]{:S(2)}) collective-permute-start(f32[20,65,128]{2,1,0:T(8,128)S(1)} %pad_maximum_fusion.3), channel_id=1, source_target_pairs={{0,2},{2,4},{4,6},{1,3},{3,5},{5,7},{8,10},{10,12},{12,14},{9,11},... | collective-permute-start | bytes 1996808 | tf_op jit(solution)/shard_map/ppermute | solution.py:59
  273.2 2.2 collective-permute-start.5
Sparse Core Ops, SparseCore 0:
  10.9 133.7 all-gather.2

commit v10 on v7

--- a/solution.py
+++ b/solution.py
@@ -103,7 +103,7 @@
         lanes = slice(2 * HEAD_DIM * pair, 2 * HEAD_DIM * (pair + 1))
         readout = lax.dot_general(
             c32, enter_ref[0, lanes, :], (((1,), (1,)), ((), ())),
-            precision=lax.Precision.HIGHEST, preferred_element_type=jnp.float32,
+            precision=lax.Precision.HIGH, preferred_element_type=jnp.float32,
         )
         out_ref[:, lanes] = (part_ref[:, lanes] + pair_lanes(rise, pair) * readout).astype(jnp.bfloat16)
 

time: 301 us -> 299 us (level)
  no operation moved by 1% of the time
where the time goes in v10:
time: 299 us; the launch traced here: 296 us
  waiting for transfers between devices  143 us (48%)
  Pallas kernels  46.7 us (16%)
  local copies, waits for them, and re-layouts  37.4 us (13%)
  other arithmetic  26.2 us (9%)
  matrix products  16.5 us (6%)
  between operations  13.7 us (5%)
  starting transfers between devices  12 us (4%)
    all_gather x1, waiting for transfers between devices, project(): lax.all_gather(input_weight, ('dp',) + SEQ, axis=0, tiled=True)  132 us
    unnamed x11, local copies, waits for them, and re-layouts  27.8 us
    pallas_call x1, Pallas kernels, intra(): pl.pallas_call(intra_kernel, grid=(span_count, groups), in_specs=[x_spec,...  16.6 us
    dot_general x1, matrix products, project(): lax.dot_general(token_rows, lax.all_gather(input_weight, ('dp',) + SEQ, a...  16.5 us
    pallas_call x1, Pallas kernels, body(): pl.pallas_call(states_kernel, grid=(span_count, groups), in_specs=[x_spec...  15.9 us
    pallas_call x1, Pallas kernels, body(): pl.pallas_call(readout_kernel, grid=(span_count, groups), in_specs=[x_spe...  14.3 us
    convert_element_type x1, other arithmetic, body(): active = jax.nn.silu(filtered).astype(jnp.bfloat16)  13.9 us
    ppermute x2, waiting for transfers between devices, scan_entering(): lax.ppermute(chip_total, 'y', pairs)  8.45 us
  transfers between devices with their start and end apart: 10, of which 4 were waited for; matrix products, arithmetic and copies ran while one was open for 4% of the time, Pallas kernels for 6%

profile of v10, /device:TPU:16, one launch (start us, length us, event | category | flops | bytes accessed | tf_op | source)
XLA Modules:
  0.0 295.9 jit_solution(10463248119257105175)
XLA Ops:
  6.5 0.7 all-gather.3.cloned.1.call-update
  7.3 1.0 reshape.147
  8.2 1.8 reduce-window.6
  10.0 0.1 slice.75
  10.1 0.1 copy.27
  10.3 0.1 copy_bitcast_fusion
  10.4 0.2 slice_reduce_fusion.1
  10.6 1.6 negate_bitcast_fusion
  12.2 0.1 broadcast_add_fusion
  12.3 132.4 %all-gather.3.cloned.1.call-done = bf16[256,11,2560]{2,1,0:T(8,128)(2,1)} async-done(((bf16[1,11,2560]{2,1,0:T(8,128)(2,1)}), bf16[256,11,2560]{2,1,0:T(8,128)(2,1)}) %all-gather.3.cloned.1.call-update) | async-done | bytes 14417936 | tf_op jit(solution)/shard_map/all_gather | solution.py:114
  144.7 25.0 %reshape.155 = bf16[2816,2560]{1,0:T(8,128)(2,1)} reshape(bf16[256,11,2560]{2,1,0:T(8,128)(2,1)} %all-gather.3.cloned.1.call-done) | data formatting | bytes 28835840
  169.8 16.5 %convolution_convert_fusion = bf16[768,2816]{1,0:T(8,128)(2,1)S(1)} fusion(bf16[2816,2560]{1,0:T(8,128)(2,1)} %reshape.155, bf16[1,768,2560]{2,1,0:T(8,128)(2,1)} %param.6), kind=kOutput, calls=%fused_computation.3 | convolution fusion | flops 11075125248 | bytes 22675456 | tf_op jit(solution)/shard_map/dot_general | solution.py:112
  186.3 2.0 copy-done
  188.3 2.2 collective-permute-start.1
  190.4 0.1 convert_reduce_fusion.3
  190.6 0.1 reduce_window_sum.25
  190.8 1.8 copy.31
  192.6 1.9 copy.32
  194.5 0.1 mul.159
  194.5 0.1 exp.58
  194.6 0.1 exp.56
  194.7 13.9 %multiply_convert_fusion.x_ref.b_ref.c_ref = bf16[768,2816]{1,0:T(8,128)(2,1)} fusion(bf16[768,2816]{1,0:T(8,128)(2,1)} %copy-done, bf16[3,2816]{1,0:T(4,128)(2,1)S(1)} %collective-permute-done.1, f32[2816]{0:T(1024)S(1)} %get-tuple-element.35, f32[2816]{0:T(1024)S(1)} %get-tuple-element.36, f32[2816]{0:T(1024)S(1)} %get-tuple-element.34, ...), kind=kLoop, calls=%fused_computation | loop fusion | flops 56229888 | bytes 8723968 | tf_op jit(solution)/shard_map/convert_element_type | solution.py:135
  208.7 15.9 %shard_map.64 = f32[3,2560,128]{2,1,0:T(8,128)} custom-call(bf16[768,2816]{1,0:T(8,128)(2,1)} %multiply_convert_fusion.x_ref.b_ref.c_ref, bf16[768,2816]{1,0:T(8,128)(2,1)} %multiply_convert_fusion.x_ref.b_ref.c_ref, f32[5,768,8]{2,1,0:T(8,128)} %bitcast.55, f32[5,768,8]{2,1,0:T(8,128)} %bitcast.59), custom_call_target="tpu_custom_call" | custom-call | flops 503316480 | bytes 8060928 | tf_op jit(solution)/shard_map/pallas_call | solution.py:152
  224.5 2.4 fusion.12
  226.9 0.3 multiply_add_fusion.2
  227.3 1.2 collective-permute-start.2
  228.5 0.1 reshape.149
  228.6 0.7 reduce_window_sum.26.cum_row_ref
  229.4 0.7 broadcast_in_dim_reshape.3.gain_ref
  230.1 0.1 collective-permute-done
  230.2 1.0 fusion.3
  231.2 2.4 collective-permute-start.3
  233.7 1.3 collective-permute-start.5
  235.0 1.6 collective-permute-start.7
  236.5 1.9 collective-permute-start.4
  238.5 1.3 collective-permute-start.6
  239.8 16.6 %shard_map.65.part_ref = f32[768,2560]{1,0:T(8,128)} custom-call(bf16[768,2816]{1,0:T(8,128)(2,1)} %multiply_convert_fusion.x_ref.b_ref.c_ref, bf16[768,2816]{1,0:T(8,128)(2,1)} %multiply_convert_fusion.x_ref.b_ref.c_ref, bf16[768,2816]{1,0:T(8,128)(2,1)} %multiply_convert_fusion.x_ref.b_ref.c_ref, f32[5,768,8]{2,1,0:T(8,128)} %bitcast.56, ...), custom_call_target="tpu_custom_call" | custom-call | flops 2264924160 | bytes 12189696 | tf_op jit(solution)/shard_map/pallas_call | solution.py:169
  256.3 8.4 %collective-permute-done.6 = f32[20]{0:T(128)S(1)} collective-permute-done((f32[20]{0:T(128)S(1)}, f32[20]{0:T(128)S(1)}, u32[]{:S(2)}, u32[]{:S(2)}) %collective-permute-start.6) | collective-permute-done | bytes 112 | tf_op jit(solution)/shard_map/ppermute | solution.py:49
  264.8 0.8 copy-done.1
  265.6 1.6 select_bitcast_fusion
  267.2 0.2 fusion.4
  267.3 0.1 collective-permute-start.8
  267.5 0.1 mul.192
  267.7 1.8 collective-permute-done.8
  269.5 0.1 maximum_select_fusion
  269.6 2.8 multiply_add_fusion
  272.5 2.3 pad_maximum_fusion.1.enter_ref
  274.8 14.3 %shard_map.66 = bf16[768,2560]{1,0:T(8,128)(2,1)} custom-call(f32[768,2560]{1,0:T(8,128)} %shard_map.65.part_ref, bf16[768,2816]{1,0:T(8,128)(2,1)} %multiply_convert_fusion.x_ref.b_ref.c_ref, f32[5,768,8]{2,1,0:T(8,128)} %bitcast.57, f32[3,2560,128]{2,1,0:T(8,128)} %pad_maximum_fusion.1.enter_ref), custom_call_target="tpu_custom_call" | custom-call | flops 3019898880 | bytes 15728640 | tf_op jit(solution)/shard_map/pallas_call | solution.py:190
  (33 shorter events, 0.6 us)
Async XLA Ops:
  6.5 138.2 %all-gather.3.cloned.1.call-start = ((), (), s32[]{:S(2)}) async-start(), calls=%async_computation | async-start | bytes 21053440 | tf_op jit(solution)/shard_map/all_gather | solution.py:114
  169.8 20.7 %copy-start.2 = (bf16[4,2816]{1,0:T(4,128)(2,1)S(1)}, bf16[4,2816]{1,0:T(4,128)(2,1)}, u32[]{:S(2)}) copy-start(bf16[4,2816]{1,0:T(4,128)(2,1)} %param.9) | copy-start | bytes 67588
  186.3 2.0 copy-start
  188.2 6.5 %copy-start.3 = (f32[2816]{0:T(1024)S(1)}, f32[2816]{0:T(1024)}, u32[]{:S(2)}) copy-start(f32[2816]{0:T(1024)} %param.10) | copy-start | bytes 33796
  188.3 6.5 %collective-permute-start.1 = (bf16[3,2816]{1,0:T(4,128)(2,1)S(1)}, bf16[3,2816]{1,0:T(4,128)(2,1)S(1)}, u32[]{:S(2)}, u32[]{:S(2)}) collective-permute-start(bf16[3,2816]{1,0:T(4,128)(2,1)S(1)} %slice.78), channel_id=1, source_target_pairs={{0,1},{1,2},{2,3},{3,4},{4,5},{5,6},{6,7},{8,9},{9,10},{10,11},{11... | collective-permute-start | bytes 50696 | tf_op jit(solution)/shard_map/ppermute | solution.py:21
  226.9 2.4 copy-start.4
  227.3 2.9 collective-permute-start.2
  228.5 1.6 collective-permute-start
  231.2 33.5 %collective-permute-start.3 = (f32[20,64,128]{2,1,0:T(8,128)}, f32[20,64,128]{2,1,0:T(8,128)S(1)}, u32[]{:S(2)}, u32[]{:S(2)}) collective-permute-start(f32[20,64,128]{2,1,0:T(8,128)} %fusion.3), channel_id=1, source_target_pairs={{0,2},{2,4},{4,6},{1,3},{3,5},{5,7},{8,10},{10,12},{12,14},{9,11},... | collective-permute-start | bytes 1966088 | tf_op jit(solution)/shard_map/ppermute | solution.py:49
  233.7 31.1 %collective-permute-start.5 = (f32[20,64,128]{2,1,0:T(8,128)}, f32[20,64,128]{2,1,0:T(8,128)S(1)}, u32[]{:S(2)}, u32[]{:S(2)}) collective-permute-start(f32[20,64,128]{2,1,0:T(8,128)} %fusion.3), channel_id=1, source_target_pairs={{0,4},{2,6},{1,5},{3,7},{8,12},{10,14},{9,13},{11,15},{16,20},{18,... | collective-permute-start | bytes 1966088 | tf_op jit(solution)/shard_map/ppermute | solution.py:49
  235.0 29.8 %collective-permute-start.7 = (f32[20,64,128]{2,1,0:T(8,128)}, f32[20,64,128]{2,1,0:T(8,128)}, u32[]{:S(2)}, u32[]{:S(2)}) collective-permute-start(f32[20,64,128]{2,1,0:T(8,128)} %fusion.3), channel_id=1, source_target_pairs={{0,6},{1,7},{8,14},{9,15},{16,22},{17,23},{24,30},{25,31},{32,38},... | collective-permute-start | bytes 1966088 | tf_op jit(solution)/shard_map/ppermute | solution.py:49
  236.5 19.8 %collective-permute-start.4 = (f32[20]{0:T(128)S(1)}, f32[20]{0:T(128)S(1)}, u32[]{:S(2)}, u32[]{:S(2)}) collective-permute-start(f32[20]{0:T(128)S(1)} %get-tuple-element.19), channel_id=1, source_target_pairs={{0,2},{2,4},{4,6},{1,3},{3,5},{5,7},{8,10},{10,12},{12,14},{9,11},... | collective-permute-start | bytes 248 | tf_op jit(solution)/shard_map/ppermute | solution.py:49
  238.5 26.3 %collective-permute-start.6 = (f32[20]{0:T(128)S(1)}, f32[20]{0:T(128)S(1)}, u32[]{:S(2)}, u32[]{:S(2)}) collective-permute-start(f32[20]{0:T(128)S(1)} %get-tuple-element.19), channel_id=1, source_target_pairs={{0,4},{2,6},{1,5},{3,7},{8,12},{10,14},{9,13},{11,15},{16,20},{18,... | collective-permute-start | bytes 248 | tf_op jit(solution)/shard_map/ppermute | solution.py:49
  264.8 0.8 copy-start.1
  267.3 2.2 collective-permute-start.8
Sparse Core Ops, SparseCore 0:
  10.9 133.7 all-gather.2

commit v11 on v10

--- a/solution.py
+++ b/solution.py
@@ -11,7 +11,7 @@
 CONV = 4
 INNER = 2560
 COLS = 2816
-GROUP = 8
+GROUP = 40
 SEQ = ("y", "core")
 
 

time: 299 us -> 287 us (0.960)
  Pallas kernels: 46.7 us -> 33.3 us
  waiting for transfers between devices: 143 us -> 147 us
    pallas_call x1, Pallas kernels: 14.3 us -> 9.37 us  [body(): pl.pallas_call(readout_kernel, grid=(span_count, groups), in_specs=[x_spe...]
    pallas_call x1, Pallas kernels: 15.9 us -> 11.5 us  [body(): pl.pallas_call(states_kernel, grid=(span_count, groups), in_specs=[x_spec...]
    pallas_call x1, Pallas kernels: 16.6 us -> 12.4 us  [intra(): pl.pallas_call(intra_kernel, grid=(span_count, groups), in_specs=[x_spec,...]
    ppermute x2, waiting for transfers between devices: 8.45 us -> 11.7 us  [scan_entering(): lax.ppermute(chip_total, 'y', pairs)]
  transfers between devices with their start and end apart: 10 -> 10, of which waited for: 4 -> 4; matrix products, arithmetic and copies ran while one was open for 4% -> 3% of each run, Pallas kernels for 6% -> 4%
where the time goes in v11:
time: 287 us; the launch traced here: 284 us
  waiting for transfers between devices  147 us (51%)
  local copies, waits for them, and re-layouts  35.5 us (12%)
  Pallas kernels  33.3 us (12%)
  other arithmetic  26 us (9%)
  matrix products  16.5 us (6%)
  between operations  13.7 us (5%)
  starting transfers between devices  12.2 us (4%)
    all_gather x1, waiting for transfers between devices, project(): lax.all_gather(input_weight, ('dp',) + SEQ, axis=0, tiled=True)  132 us
    unnamed x11, local copies, waits for them, and re-layouts  27.8 us
    dot_general x1, matrix products, project(): lax.dot_general(token_rows, lax.all_gather(input_weight, ('dp',) + SEQ, a...  16.5 us
    convert_element_type x1, other arithmetic, body(): active = jax.nn.silu(filtered).astype(jnp.bfloat16)  13.9 us
    pallas_call x1, Pallas kernels, intra(): pl.pallas_call(intra_kernel, grid=(span_count, groups), in_specs=[x_spec,...  12.4 us
    ppermute x2, waiting for transfers between devices, scan_entering(): lax.ppermute(chip_total, 'y', pairs)  11.7 us
    pallas_call x1, Pallas kernels, body(): pl.pallas_call(states_kernel, grid=(span_count, groups), in_specs=[x_spec...  11.5 us
    pallas_call x1, Pallas kernels, body(): pl.pallas_call(readout_kernel, grid=(span_count, groups), in_specs=[x_spe...  9.37 us
  transfers between devices with their start and end apart: 10, of which 4 were waited for; matrix products, arithmetic and copies ran while one was open for 3% of the time, Pallas kernels for 4%

profile of v11, /device:TPU:16, one launch (start us, length us, event | category | flops | bytes accessed | tf_op | source)
XLA Modules:
  0.0 284.5 jit_solution(17694327480690262638)
XLA Ops:
  6.5 0.7 all-gather.3.cloned.1.call-update
  7.3 1.0 reshape.162
  8.2 1.8 reduce-window.6
  10.0 0.1 slice.75
  10.1 0.1 copy.26
  10.3 0.1 copy_bitcast_fusion
  10.4 0.2 slice_reduce_fusion.1
  10.6 1.6 negate_bitcast_fusion
  12.2 0.1 broadcast_add_fusion
  12.3 132.4 %all-gather.3.cloned.1.call-done = bf16[256,11,2560]{2,1,0:T(8,128)(2,1)} async-done(((bf16[1,11,2560]{2,1,0:T(8,128)(2,1)}), bf16[256,11,2560]{2,1,0:T(8,128)(2,1)}) %all-gather.3.cloned.1.call-update) | async-done | bytes 14417936 | tf_op jit(solution)/shard_map/all_gather | solution.py:114
  144.7 25.0 %reshape.170 = bf16[2816,2560]{1,0:T(8,128)(2,1)} reshape(bf16[256,11,2560]{2,1,0:T(8,128)(2,1)} %all-gather.3.cloned.1.call-done) | data formatting | bytes 28835840
  169.8 16.5 %convolution_convert_fusion = bf16[768,2816]{1,0:T(8,128)(2,1)S(1)} fusion(bf16[2816,2560]{1,0:T(8,128)(2,1)} %reshape.170, bf16[1,768,2560]{2,1,0:T(8,128)(2,1)} %param.6), kind=kOutput, calls=%fused_computation.3 | convolution fusion | flops 11075125248 | bytes 22675456 | tf_op jit(solution)/shard_map/dot_general | solution.py:112
  186.3 2.0 copy-done
  188.3 2.2 collective-permute-start.1
  190.5 0.1 convert_reduce_fusion.3
  190.6 0.9 copy.29
  191.5 0.9 copy.30.step_ref
  192.4 0.1 mul.159
  192.5 0.1 exp.58
  192.6 0.1 exp.56
  192.7 0.7 collective-permute-done.1
  193.4 13.9 %multiply_convert_fusion.x_ref.b_ref.c_ref = bf16[768,2816]{1,0:T(8,128)(2,1)} fusion(bf16[768,2816]{1,0:T(8,128)(2,1)} %copy-done, bf16[3,2816]{1,0:T(4,128)(2,1)S(1)} %collective-permute-done.1, f32[2816]{0:T(1024)S(1)} %get-tuple-element.35, f32[2816]{0:T(1024)S(1)} %get-tuple-element.36, f32[2816]{0:T(1024)S(1)} %get-tuple-element.34, ...), kind=kLoop, calls=%fused_computation | loop fusion | flops 56229888 | bytes 8723968 | tf_op jit(solution)/shard_map/convert_element_type | solution.py:135
  207.3 11.5 %shard_map.64 = f32[3,2560,128]{2,1,0:T(8,128)} custom-call(bf16[768,2816]{1,0:T(8,128)(2,1)} %multiply_convert_fusion.x_ref.b_ref.c_ref, bf16[768,2816]{1,0:T(8,128)(2,1)} %multiply_convert_fusion.x_ref.b_ref.c_ref, f32[1,768,40]{2,1,0:T(8,128)} %bitcast.57, f32[1,768,40]{2,1,0:T(8,128)} %copy.30.step_ref), custom_call_target="tpu_custom_call" | custom-call | flops 503316480 | bytes 8060928 | tf_op jit(solution)/shard_map/pallas_call | solution.py:152
  218.9 2.4 fusion.12
  221.2 0.3 multiply_add_fusion.2
  221.6 0.4 collective-permute-start.2
  222.1 0.1 reshape.164
  222.2 0.2 collective-permute-start
  222.4 0.8 reduce_window_sum.32.cum_row_ref
  223.2 0.7 broadcast_in_dim_reshape.3.gain_ref
  224.0 1.0 fusion.3
  225.0 3.1 %collective-permute-start.3 = (f32[20,64,128]{2,1,0:T(8,128)}, f32[20,64,128]{2,1,0:T(8,128)S(1)}, u32[]{:S(2)}, u32[]{:S(2)}) collective-permute-start(f32[20,64,128]{2,1,0:T(8,128)} %fusion.3), channel_id=1, source_target_pairs={{0,2},{2,4},{4,6},{1,3},{3,5},{5,7},{8,10},{10,12},{12,14},{9,11},... | collective-permute-start | bytes 1966088 | tf_op jit(solution)/shard_map/ppermute | solution.py:49
  228.1 1.3 collective-permute-start.5
  229.4 1.6 collective-permute-start.7
  230.9 1.9 collective-permute-start.4
  232.8 1.5 collective-permute-start.6
  234.3 12.4 %shard_map.65.part_ref = f32[768,2560]{1,0:T(8,128)} custom-call(bf16[768,2816]{1,0:T(8,128)(2,1)} %multiply_convert_fusion.x_ref.b_ref.c_ref, bf16[768,2816]{1,0:T(8,128)(2,1)} %multiply_convert_fusion.x_ref.b_ref.c_ref, bf16[768,2816]{1,0:T(8,128)(2,1)} %multiply_convert_fusion.x_ref.b_ref.c_ref, f32[1,768,40]{2,1,0:T(8,128)} %bitcast.58, ...), custom_call_target="tpu_custom_call" | custom-call | flops 2063597568 | bytes 12189696 | tf_op jit(solution)/shard_map/pallas_call | solution.py:169
  246.7 11.7 %collective-permute-done.6 = f32[20]{0:T(128)S(1)} collective-permute-done((f32[20]{0:T(128)S(1)}, f32[20]{0:T(128)S(1)}, u32[]{:S(2)}, u32[]{:S(2)}) %collective-permute-start.6) | collective-permute-done | bytes 112 | tf_op jit(solution)/shard_map/ppermute | solution.py:49
  258.5 0.8 copy-done.1
  259.3 1.6 select_bitcast_fusion
  260.8 0.2 fusion.4
  261.0 0.1 collective-permute-start.8
  261.2 0.1 mul.192
  261.4 1.8 collective-permute-done.8
  263.2 0.1 maximum_select_fusion
  263.3 2.8 multiply_add_fusion
  266.1 2.2 pad_maximum_fusion.1.enter_ref
  268.3 9.4 %shard_map.66 = bf16[768,2560]{1,0:T(8,128)(2,1)} custom-call(f32[768,2560]{1,0:T(8,128)} %shard_map.65.part_ref, bf16[768,2816]{1,0:T(8,128)(2,1)} %multiply_convert_fusion.x_ref.b_ref.c_ref, f32[1,768,40]{2,1,0:T(8,128)} %bitcast.59, f32[3,2560,128]{2,1,0:T(8,128)} %pad_maximum_fusion.1.enter_ref), custom_call_target="tpu_custom_call" | custom-call | flops 3019898880 | bytes 15728640 | tf_op jit(solution)/shard_map/pallas_call | solution.py:190
  (32 shorter events, 0.6 us)
Async XLA Ops:
  6.5 138.2 %all-gather.3.cloned.1.call-start = ((), (), s32[]{:S(2)}) async-start(), calls=%async_computation | async-start | bytes 21053440 | tf_op jit(solution)/shard_map/all_gather | solution.py:114
  169.8 20.7 %copy-start.2 = (bf16[4,2816]{1,0:T(4,128)(2,1)S(1)}, bf16[4,2816]{1,0:T(4,128)(2,1)}, u32[]{:S(2)}) copy-start(bf16[4,2816]{1,0:T(4,128)(2,1)} %param.9) | copy-start | bytes 67588
  169.8 23.6 %copy-start.3 = (f32[2816]{0:T(1024)S(1)}, f32[2816]{0:T(1024)}, u32[]{:S(2)}) copy-start(f32[2816]{0:T(1024)} %param.10) | copy-start | bytes 33796
  186.3 2.0 copy-start
  188.3 5.1 %collective-permute-start.1 = (bf16[3,2816]{1,0:T(4,128)(2,1)S(1)}, bf16[3,2816]{1,0:T(4,128)(2,1)S(1)}, u32[]{:S(2)}, u32[]{:S(2)}) collective-permute-start(bf16[3,2816]{1,0:T(4,128)(2,1)S(1)} %slice.78), channel_id=1, source_target_pairs={{0,1},{1,2},{2,3},{3,4},{4,5},{5,6},{6,7},{8,9},{9,10},{10,11},{11... | collective-permute-start | bytes 50696 | tf_op jit(solution)/shard_map/ppermute | solution.py:21
  221.2 1.9 copy-start.4
  221.6 2.3 collective-permute-start.2
  222.2 1.8 collective-permute-start
  225.0 33.5 %collective-permute-start.3 = (f32[20,64,128]{2,1,0:T(8,128)}, f32[20,64,128]{2,1,0:T(8,128)S(1)}, u32[]{:S(2)}, u32[]{:S(2)}) collective-permute-start(f32[20,64,128]{2,1,0:T(8,128)} %fusion.3), channel_id=1, source_target_pairs={{0,2},{2,4},{4,6},{1,3},{3,5},{5,7},{8,10},{10,12},{12,14},{9,11},... | collective-permute-start | bytes 1966088 | tf_op jit(solution)/shard_map/ppermute | solution.py:49
  228.1 30.4 %collective-permute-start.5 = (f32[20,64,128]{2,1,0:T(8,128)}, f32[20,64,128]{2,1,0:T(8,128)S(1)}, u32[]{:S(2)}, u32[]{:S(2)}) collective-permute-start(f32[20,64,128]{2,1,0:T(8,128)} %fusion.3), channel_id=1, source_target_pairs={{0,4},{2,6},{1,5},{3,7},{8,12},{10,14},{9,13},{11,15},{16,20},{18,... | collective-permute-start | bytes 1966088 | tf_op jit(solution)/shard_map/ppermute | solution.py:49
  229.4 29.1 %collective-permute-start.7 = (f32[20,64,128]{2,1,0:T(8,128)}, f32[20,64,128]{2,1,0:T(8,128)}, u32[]{:S(2)}, u32[]{:S(2)}) collective-permute-start(f32[20,64,128]{2,1,0:T(8,128)} %fusion.3), channel_id=1, source_target_pairs={{0,6},{1,7},{8,14},{9,15},{16,22},{17,23},{24,30},{25,31},{32,38},... | collective-permute-start | bytes 1966088 | tf_op jit(solution)/shard_map/ppermute | solution.py:49
  230.9 15.8 %collective-permute-start.4 = (f32[20]{0:T(128)S(1)}, f32[20]{0:T(128)S(1)}, u32[]{:S(2)}, u32[]{:S(2)}) collective-permute-start(f32[20]{0:T(128)S(1)} %get-tuple-element.19), channel_id=1, source_target_pairs={{0,2},{2,4},{4,6},{1,3},{3,5},{5,7},{8,10},{10,12},{12,14},{9,11},... | collective-permute-start | bytes 248 | tf_op jit(solution)/shard_map/ppermute | solution.py:49
  232.8 25.6 %collective-permute-start.6 = (f32[20]{0:T(128)S(1)}, f32[20]{0:T(128)S(1)}, u32[]{:S(2)}, u32[]{:S(2)}) collective-permute-start(f32[20]{0:T(128)S(1)} %get-tuple-element.19), channel_id=1, source_target_pairs={{0,4},{2,6},{1,5},{3,7},{8,12},{10,14},{9,13},{11,15},{16,20},{18,... | collective-permute-start | bytes 248 | tf_op jit(solution)/shard_map/ppermute | solution.py:49
  258.4 0.8 copy-start.1
  261.0 2.2 collective-permute-start.8
Sparse Core Ops, SparseCore 0:
  10.9 133.7 all-gather.2

commit v12 on v11

--- a/solution.py
+++ b/solution.py
@@ -89,7 +89,7 @@
         for half in range(2):
             head = 2 * pair + half
             spread = cum[:, head : head + 1] - cum_row_ref[head : head + 1, :]
-            decay = jnp.where(causal, jnp.exp(jnp.where(causal, spread, 0.0)), 0.0)
+            decay = jnp.exp(jnp.where(causal, spread, -jnp.inf))
             mixing = (scores * decay * step_row_ref[head : head + 1, :]).astype(jnp.bfloat16)
             parts.append(jnp.dot(mixing, x_pair, preferred_element_type=jnp.float32))
         intra = jnp.where(lane < HEAD_DIM, parts[0], parts[1])

time: 287 us -> 287 us (level)
  no operation moved by 1% of the time
where the time goes in v12:
time: 287 us; the launch traced here: 284 us
  waiting for transfers between devices  148 us (52%)
  local copies, waits for them, and re-layouts  35.5 us (12%)
  Pallas kernels  32.8 us (11%)
  other arithmetic  26 us (9%)
  matrix products  16.5 us (6%)
  between operations  13.7 us (5%)
  starting transfers between devices  12.2 us (4%)
    all_gather x1, waiting for transfers between devices, project(): lax.all_gather(input_weight, ('dp',) + SEQ, axis=0, tiled=True)  132 us
    unnamed x11, local copies, waits for them, and re-layouts  27.8 us
    dot_general x1, matrix products, project(): lax.dot_general(token_rows, lax.all_gather(input_weight, ('dp',) + SEQ, a...  16.5 us
    convert_element_type x1, other arithmetic, body(): active = jax.nn.silu(filtered).astype(jnp.bfloat16)  13.9 us
    ppermute x2, waiting for transfers between devices, scan_entering(): lax.ppermute(chip_total, 'y', pairs)  12.1 us
    pallas_call x1, Pallas kernels, intra(): pl.pallas_call(intra_kernel, grid=(span_count, groups), in_specs=[x_spec,...  12 us
    pallas_call x1, Pallas kernels, body(): pl.pallas_call(states_kernel, grid=(span_count, groups), in_specs=[x_spec...  11.5 us
    pallas_call x1, Pallas kernels, body(): pl.pallas_call(readout_kernel, grid=(span_count, groups), in_specs=[x_spe...  9.37 us
  transfers between devices with their start and end apart: 10, of which 4 were waited for; matrix products, arithmetic and copies ran while one was open for 3% of the time, Pallas kernels for 4%

profile of v12, /device:TPU:16, one launch (start us, length us, event | category | flops | bytes accessed | tf_op | source)
XLA Modules:
  0.0 284.5 jit_solution(6021258297312216319)
XLA Ops:
  6.5 0.7 all-gather.3.cloned.1.call-update
  7.3 1.0 reshape.162
  8.2 1.8 reduce-window.6
  10.0 0.1 slice.75
  10.1 0.1 copy.26
  10.3 0.1 copy_bitcast_fusion
  10.4 0.2 slice_reduce_fusion.1
  10.6 1.6 negate_bitcast_fusion
  12.2 0.1 broadcast_add_fusion
  12.3 132.4 %all-gather.3.cloned.1.call-done = bf16[256,11,2560]{2,1,0:T(8,128)(2,1)} async-done(((bf16[1,11,2560]{2,1,0:T(8,128)(2,1)}), bf16[256,11,2560]{2,1,0:T(8,128)(2,1)}) %all-gather.3.cloned.1.call-update) | async-done | bytes 14417936 | tf_op jit(solution)/shard_map/all_gather | solution.py:114
  144.7 25.0 %reshape.170 = bf16[2816,2560]{1,0:T(8,128)(2,1)} reshape(bf16[256,11,2560]{2,1,0:T(8,128)(2,1)} %all-gather.3.cloned.1.call-done) | data formatting | bytes 28835840
  169.8 16.5 %convolution_convert_fusion = bf16[768,2816]{1,0:T(8,128)(2,1)S(1)} fusion(bf16[2816,2560]{1,0:T(8,128)(2,1)} %reshape.170, bf16[1,768,2560]{2,1,0:T(8,128)(2,1)} %param.6), kind=kOutput, calls=%fused_computation.3 | convolution fusion | flops 11075125248 | bytes 22675456 | tf_op jit(solution)/shard_map/dot_general | solution.py:112
  186.3 2.0 copy-done
  188.3 2.2 collective-permute-start.1
  190.5 0.1 convert_reduce_fusion.3
  190.6 0.9 copy.29
  191.5 0.9 copy.30.step_ref
  192.4 0.1 mul.159
  192.5 0.1 exp.58
  192.6 0.1 exp.56
  192.7 0.7 collective-permute-done.1
  193.4 13.9 %multiply_convert_fusion.x_ref.b_ref.c_ref = bf16[768,2816]{1,0:T(8,128)(2,1)} fusion(bf16[768,2816]{1,0:T(8,128)(2,1)} %copy-done, bf16[3,2816]{1,0:T(4,128)(2,1)S(1)} %collective-permute-done.1, f32[2816]{0:T(1024)S(1)} %get-tuple-element.35, f32[2816]{0:T(1024)S(1)} %get-tuple-element.36, f32[2816]{0:T(1024)S(1)} %get-tuple-element.34, ...), kind=kLoop, calls=%fused_computation | loop fusion | flops 56229888 | bytes 8723968 | tf_op jit(solution)/shard_map/convert_element_type | solution.py:135
  207.3 11.5 %shard_map.64 = f32[3,2560,128]{2,1,0:T(8,128)} custom-call(bf16[768,2816]{1,0:T(8,128)(2,1)} %multiply_convert_fusion.x_ref.b_ref.c_ref, bf16[768,2816]{1,0:T(8,128)(2,1)} %multiply_convert_fusion.x_ref.b_ref.c_ref, f32[1,768,40]{2,1,0:T(8,128)} %bitcast.57, f32[1,768,40]{2,1,0:T(8,128)} %copy.30.step_ref), custom_call_target="tpu_custom_call" | custom-call | flops 503316480 | bytes 8060928 | tf_op jit(solution)/shard_map/pallas_call | solution.py:152
  218.9 2.4 fusion.12
  221.2 0.3 multiply_add_fusion.2
  221.6 0.4 collective-permute-start.2
  222.1 0.1 reshape.164
  222.2 0.2 collective-permute-start
  222.4 0.8 reduce_window_sum.32.cum_row_ref
  223.2 0.7 broadcast_in_dim_reshape.3.gain_ref
  224.0 1.0 fusion.3
  225.0 3.1 %collective-permute-start.3 = (f32[20,64,128]{2,1,0:T(8,128)}, f32[20,64,128]{2,1,0:T(8,128)S(1)}, u32[]{:S(2)}, u32[]{:S(2)}) collective-permute-start(f32[20,64,128]{2,1,0:T(8,128)} %fusion.3), channel_id=1, source_target_pairs={{0,2},{2,4},{4,6},{1,3},{3,5},{5,7},{8,10},{10,12},{12,14},{9,11},... | collective-permute-start | bytes 1966088 | tf_op jit(solution)/shard_map/ppermute | solution.py:49
  228.1 1.3 collective-permute-start.5
  229.4 1.6 collective-permute-start.7
  230.9 1.9 collective-permute-start.4
  232.8 1.5 collective-permute-start.6
  234.3 12.0 %shard_map.65.part_ref = f32[768,2560]{1,0:T(8,128)} custom-call(bf16[768,2816]{1,0:T(8,128)(2,1)} %multiply_convert_fusion.x_ref.b_ref.c_ref, bf16[768,2816]{1,0:T(8,128)(2,1)} %multiply_convert_fusion.x_ref.b_ref.c_ref, bf16[768,2816]{1,0:T(8,128)(2,1)} %multiply_convert_fusion.x_ref.b_ref.c_ref, f32[1,768,40]{2,1,0:T(8,128)} %bitcast.58, ...), custom_call_target="tpu_custom_call" | custom-call | flops 2063597568 | bytes 12189696 | tf_op jit(solution)/shard_map/pallas_call | solution.py:169
  246.3 12.1 %collective-permute-done.6 = f32[20]{0:T(128)S(1)} collective-permute-done((f32[20]{0:T(128)S(1)}, f32[20]{0:T(128)S(1)}, u32[]{:S(2)}, u32[]{:S(2)}) %collective-permute-start.6) | collective-permute-done | bytes 112 | tf_op jit(solution)/shard_map/ppermute | solution.py:49
  258.5 0.8 copy-done.1
  259.3 1.6 select_bitcast_fusion
  260.8 0.2 fusion.4
  261.0 0.1 collective-permute-start.8
  261.2 0.1 mul.192
  261.4 1.8 collective-permute-done.8
  263.2 0.1 maximum_select_fusion
  263.3 2.8 multiply_add_fusion
  266.1 2.2 pad_maximum_fusion.1.enter_ref
  268.3 9.4 %shard_map.66 = bf16[768,2560]{1,0:T(8,128)(2,1)} custom-call(f32[768,2560]{1,0:T(8,128)} %shard_map.65.part_ref, bf16[768,2816]{1,0:T(8,128)(2,1)} %multiply_convert_fusion.x_ref.b_ref.c_ref, f32[1,768,40]{2,1,0:T(8,128)} %bitcast.59, f32[3,2560,128]{2,1,0:T(8,128)} %pad_maximum_fusion.1.enter_ref), custom_call_target="tpu_custom_call" | custom-call | flops 3019898880 | bytes 15728640 | tf_op jit(solution)/shard_map/pallas_call | solution.py:190
  (32 shorter events, 0.6 us)
Async XLA Ops:
  6.5 138.2 %all-gather.3.cloned.1.call-start = ((), (), s32[]{:S(2)}) async-start(), calls=%async_computation | async-start | bytes 21053440 | tf_op jit(solution)/shard_map/all_gather | solution.py:114
  169.8 20.7 %copy-start.2 = (bf16[4,2816]{1,0:T(4,128)(2,1)S(1)}, bf16[4,2816]{1,0:T(4,128)(2,1)}, u32[]{:S(2)}) copy-start(bf16[4,2816]{1,0:T(4,128)(2,1)} %param.9) | copy-start | bytes 67588
  169.8 23.6 %copy-start.3 = (f32[2816]{0:T(1024)S(1)}, f32[2816]{0:T(1024)}, u32[]{:S(2)}) copy-start(f32[2816]{0:T(1024)} %param.10) | copy-start | bytes 33796
  186.3 2.0 copy-start
  188.3 5.1 %collective-permute-start.1 = (bf16[3,2816]{1,0:T(4,128)(2,1)S(1)}, bf16[3,2816]{1,0:T(4,128)(2,1)S(1)}, u32[]{:S(2)}, u32[]{:S(2)}) collective-permute-start(bf16[3,2816]{1,0:T(4,128)(2,1)S(1)} %slice.78), channel_id=1, source_target_pairs={{0,1},{1,2},{2,3},{3,4},{4,5},{5,6},{6,7},{8,9},{9,10},{10,11},{11... | collective-permute-start | bytes 50696 | tf_op jit(solution)/shard_map/ppermute | solution.py:21
  221.2 1.9 copy-start.4
  221.6 2.3 collective-permute-start.2
  222.2 1.8 collective-permute-start
  225.0 33.5 %collective-permute-start.3 = (f32[20,64,128]{2,1,0:T(8,128)}, f32[20,64,128]{2,1,0:T(8,128)S(1)}, u32[]{:S(2)}, u32[]{:S(2)}) collective-permute-start(f32[20,64,128]{2,1,0:T(8,128)} %fusion.3), channel_id=1, source_target_pairs={{0,2},{2,4},{4,6},{1,3},{3,5},{5,7},{8,10},{10,12},{12,14},{9,11},... | collective-permute-start | bytes 1966088 | tf_op jit(solution)/shard_map/ppermute | solution.py:49
  228.1 30.4 %collective-permute-start.5 = (f32[20,64,128]{2,1,0:T(8,128)}, f32[20,64,128]{2,1,0:T(8,128)S(1)}, u32[]{:S(2)}, u32[]{:S(2)}) collective-permute-start(f32[20,64,128]{2,1,0:T(8,128)} %fusion.3), channel_id=1, source_target_pairs={{0,4},{2,6},{1,5},{3,7},{8,12},{10,14},{9,13},{11,15},{16,20},{18,... | collective-permute-start | bytes 1966088 | tf_op jit(solution)/shard_map/ppermute | solution.py:49
  229.4 29.1 %collective-permute-start.7 = (f32[20,64,128]{2,1,0:T(8,128)}, f32[20,64,128]{2,1,0:T(8,128)}, u32[]{:S(2)}, u32[]{:S(2)}) collective-permute-start(f32[20,64,128]{2,1,0:T(8,128)} %fusion.3), channel_id=1, source_target_pairs={{0,6},{1,7},{8,14},{9,15},{16,22},{17,23},{24,30},{25,31},{32,38},... | collective-permute-start | bytes 1966088 | tf_op jit(solution)/shard_map/ppermute | solution.py:49
  230.9 15.4 %collective-permute-start.4 = (f32[20]{0:T(128)S(1)}, f32[20]{0:T(128)S(1)}, u32[]{:S(2)}, u32[]{:S(2)}) collective-permute-start(f32[20]{0:T(128)S(1)} %get-tuple-element.19), channel_id=1, source_target_pairs={{0,2},{2,4},{4,6},{1,3},{3,5},{5,7},{8,10},{10,12},{12,14},{9,11},... | collective-permute-start | bytes 248 | tf_op jit(solution)/shard_map/ppermute | solution.py:49
  232.8 25.6 %collective-permute-start.6 = (f32[20]{0:T(128)S(1)}, f32[20]{0:T(128)S(1)}, u32[]{:S(2)}, u32[]{:S(2)}) collective-permute-start(f32[20]{0:T(128)S(1)} %get-tuple-element.19), channel_id=1, source_target_pairs={{0,4},{2,6},{1,5},{3,7},{8,12},{10,14},{9,13},{11,15},{16,20},{18,... | collective-permute-start | bytes 248 | tf_op jit(solution)/shard_map/ppermute | solution.py:49
  258.4 0.8 copy-start.1
  261.0 2.2 collective-permute-start.8
Sparse Core Ops, SparseCore 0:
  10.9 133.7 all-gather.2
